TPU v7x, 128 devices: a whole 4x4x4 slice. The times are simulated.
128 devices in a mesh: dom: 128 (over x, z, y, core).
Axes of the slice: x: 4, y: 4, z: 4, core: 2. Of those that a mesh axis runs over, the one named last changes fastest.
Arguments:
- loads: float32 [4, 3, 8192, 2, 128], P(None, None, 'dom'), may hold values from -6 to 6
- modal_disp: float32 [4, 3, 8192, 2, 128], P(None, None, 'dom'), may hold values from -6 to 6
- material: int32 [8192, 2, 128], P('dom'), may hold values from 0 to 7
- moduli: float32 [8], replicated, may hold values from 0.05 to 0.4
- part_device: int32 [128], replicated, may hold values from 0 to 127, as said below
- partners: int32 [2, 128], replicated, may hold values from 0 to 127, as said below
- low_bound: float32 [1], replicated, may hold values from 0.02 to 0.3
- high_bound: float32 [1], replicated, may hold values from 1.5 to 2.5
Outputs:
- displacement: float32 [4, 3, 8192, 2, 128], P(None, None, 'dom')
- residual: float32 [4, 3, 8192, 2, 128], P(None, None, 'dom')
Inputs may be any that keep to these rules, and one draw needn't show every extreme that they name: `part_device`: each device is named once. `partners`: round 0 pairs the devices of partitions 2i and 2i+1, round 1 those of partitions 2i+1 and 2i+2, partitions as given by part_device; a device without a partner in a round is its own partner.
All inputs are finite; a program needn't handle non-finite values.
Results may differ from a plain program's by a relative error of at most 0.00002.
Values sent between devices are 32-bit elements; how exact they have to be, the bound alone decides.
No kernel may reach another device: no remote copies, remote signals or barrier semaphores. Data moves between devices by JAX's collectives and lax.ppermute only.
A program may use at most 128 MiB of HBM per device.

v0:
```python
import jax
import jax.numpy as jnp
from jax import lax
from jax.experimental import pallas as pl
from jax.experimental.pallas import tpu as pltpu
from jax.sharding import Mesh, PartitionSpec as P

MATERIALS = 8
GROUP = 8
PAD = 8

GAMMA = 0.2
BETA = 0.5
EDGE_WEIGHTS = (0.0, 1.0, 0.5, 0.25)
OFFSETS = [
    (a, b, c) for a in (-1, 0, 1) for b in (-1, 0, 1) for c in (-1, 0, 1) if (a, b, c) != (0, 0, 0)
]


def shift_cells(array, axis, step):
    if step == 0:
        return array
    length = array.shape[axis]
    zero = jnp.zeros_like(lax.slice_in_dim(array, 0, 1, axis=axis))
    if step > 0:
        return jnp.concatenate([lax.slice_in_dim(array, 1, length, axis=axis), zero], axis=axis)
    return jnp.concatenate([zero, lax.slice_in_dim(array, 0, length - 1, axis=axis)], axis=axis)


def mod_neighbour(mod_ext, off_x, off_y, off_z, depth):
    rows = lax.slice_in_dim(mod_ext, 1 + off_x, 1 + off_x + depth, axis=1)
    return shift_cells(shift_cells(rows, 0, off_y), 2, off_z)


def edges_of(mod_ext, depth):
    centre = mod_neighbour(mod_ext, 0, 0, 0, depth)
    edges = []
    for offset in OFFSETS:
        norm_sq = offset[0] * offset[0] + offset[1] * offset[1] + offset[2] * offset[2]
        edges.append(
            EDGE_WEIGHTS[norm_sq]
            * 0.5
            * (centre + mod_neighbour(mod_ext, offset[0], offset[1], offset[2], depth))
        )
    return centre, edges


def diagonal_of(centre, edges):
    comps = [GAMMA * centre, GAMMA * centre, GAMMA * centre]
    for offset, edge in zip(OFFSETS, edges):
        norm_sq = offset[0] * offset[0] + offset[1] * offset[1] + offset[2] * offset[2]
        for comp in range(3):
            comps[comp] = comps[comp] + edge * (1.0 + BETA * offset[comp] * offset[comp] / norm_sq)
    return jnp.stack(comps, axis=0)


def stencil_kernel(field_ref, edge_ref, cm_ref, out_ref):
    samples, _, rows_y, padded, width = field_ref.shape
    depth = padded - 2 * PAD
    chunks = depth // 8
    sub = lax.broadcasted_iota(jnp.int32, (8, width), 0)
    lane = lax.broadcasted_iota(jnp.int32, (8, width), 1)

    def body(it, carry):
        s = it // chunks
        r = pl.multiple_of((it % chunks) * 8, 8)

        def rows(c, y, off):
            return field_ref[s, c, y, pl.ds(r + off, 8), :]

        centre = [[rows(c, y, PAD) for y in range(rows_y)] for c in range(3)]
        acc = [
            [GAMMA * cm_ref[y, pl.ds(r, 8), :] * centre[c][y] for y in range(rows_y)]
            for c in range(3)
        ]
        index = 0
        for off_x in (-1, 0, 1):
            if off_x == 0:
                shifted_x = centre
            elif off_x < 0:
                shifted_x = [
                    [
                        jnp.where(
                            sub == 0,
                            pltpu.roll(rows(c, y, PAD - 8), 1, 0),
                            pltpu.roll(centre[c][y], 1, 0),
                        )
                        for y in range(rows_y)
                    ]
                    for c in range(3)
                ]
            else:
                shifted_x = [
                    [
                        jnp.where(
                            sub == 7,
                            pltpu.roll(rows(c, y, PAD + 8), 7, 0),
                            pltpu.roll(centre[c][y], 7, 0),
                        )
                        for y in range(rows_y)
                    ]
                    for c in range(3)
                ]
            shifted = {}
            for off_z in (-1, 0, 1):
                if off_z == 0:
                    shifted[off_z] = shifted_x
                elif off_z < 0:
                    shifted[off_z] = [
                        [
                            jnp.where(lane == 0, jnp.float32(0.0), pltpu.roll(v, 1, 1))
                            for v in per_c
                        ]
                        for per_c in shifted_x
                    ]
                else:
                    shifted[off_z] = [
                        [
                            jnp.where(lane == width - 1, jnp.float32(0.0), pltpu.roll(v, width - 1, 1))
                            for v in per_c
                        ]
                        for per_c in shifted_x
                    ]
            for off_y in (-1, 0, 1):
                for off_z in (-1, 0, 1):
                    if (off_x, off_y, off_z) == (0, 0, 0):
                        continue
                    offset = (off_x, off_y, off_z)
                    norm_sq = off_x * off_x + off_y * off_y + off_z * off_z
                    for y in range(rows_y):
                        edge = edge_ref[index, y, pl.ds(r, 8), :]
                        source = y + off_y
                        if 0 <= source < rows_y:
                            delta = [centre[c][y] - shifted[off_z][c][source] for c in range(3)]
                        else:
                            delta = [centre[c][y] for c in range(3)]
                        project = None
                        for c in range(3):
                            if offset[c] > 0:
                                project = delta[c] if project is None else project + delta[c]
                            elif offset[c] < 0:
                                project = -delta[c] if project is None else project - delta[c]
                        if norm_sq == 2:
                            project = project * 0.5
                        elif norm_sq == 3:
                            project = project * (1.0 / 3.0)
                        for c in range(3):
                            if offset[c] != 0:
                                acc[c][y] = acc[c][y] + edge * (delta[c] + BETA * offset[c] * project)
                            else:
                                acc[c][y] = acc[c][y] + edge * delta[c]
                    index += 1
        for c in range(3):
            for y in range(rows_y):
                out_ref[s, c, y, pl.ds(r, 8), :] = acc[c][y]
        return carry

    lax.fori_loop(0, samples * chunks, body, 0)


def stiffness(field, below, above, edges, centre_mod):
    samples, _, rows_y, depth, width = field.shape
    zeros = jnp.zeros((samples, 3, rows_y, PAD - 1, width), jnp.float32)
    padded = jnp.concatenate([zeros, below[:, :, :, None], field, above[:, :, :, None], zeros], axis=3)
    vmem = pl.BlockSpec(memory_space=pltpu.VMEM)
    size = samples * 3 * rows_y * depth * width
    return pl.pallas_call(
        stencil_kernel,
        out_shape=jax.ShapeDtypeStruct(field.shape, jnp.float32),
        in_specs=[vmem, vmem, vmem],
        out_specs=vmem,
        cost_estimate=pl.CostEstimate(flops=26 * 20 * size, bytes_accessed=4 * (2 * size + 28 * size // samples // 3), transcendentals=0),
    )(padded, edges, centre_mod)


def lookup_modulus(material, moduli):
    modulus = jnp.zeros(material.shape, jnp.float32)
    for index in range(MATERIALS):
        modulus = modulus + jnp.where(material == index, moduli[index], jnp.float32(0.0))
    return modulus


def neighbour_devices(part_device, partners):
    count = part_device.shape[0]
    ids = jnp.arange(count, dtype=jnp.int32)
    place = jnp.zeros((count,), jnp.int32).at[part_device].set(ids)
    parity = place % 2
    up_dev = partners[parity, ids]
    low_dev = partners[1 - parity, ids]
    return up_dev, low_dev


def exchange(first, last, up_dev, low_dev):
    col = lax.axis_index("col")
    grp = lax.axis_index("grp")
    me = col * GROUP + grp
    cols = up_dev.shape[0] // GROUP
    pack = jnp.stack([first, last], axis=0)[None]
    held = lax.all_gather(pack, "grp", axis=0, tiled=True)
    targets = jnp.arange(cols, dtype=jnp.int32) * GROUP + grp
    t_up = up_dev[targets]
    t_low = low_dev[targets]
    up_here = (t_up // GROUP) == col
    low_here = (t_low // GROUP) == col
    from_up = held[t_up % GROUP, 0]
    from_low = held[t_low % GROUP, 1]
    shape = (cols,) + (1,) * (from_up.ndim - 1)
    from_up = jnp.where(up_here.reshape(shape), from_up, jnp.float32(0.0))
    from_low = jnp.where(low_here.reshape(shape), from_low, jnp.float32(0.0))
    slots = jnp.stack([from_up, from_low], axis=1)
    got = lax.all_to_all(slots, "col", 0, 0, tiled=True)
    my_up = up_dev[me]
    my_low = low_dev[me]
    above = got[my_up // GROUP, 0]
    below = got[my_low // GROUP, 1]
    above = jnp.where(my_up != me, above, jnp.float32(0.0))
    below = jnp.where(my_low != me, below, jnp.float32(0.0))
    return below, above


def on_device(loads, modal_disp, material, moduli, part_device, partners, low_bound, high_bound):
    up_dev, low_dev = neighbour_devices(part_device, partners)
    samples, _, depth, rows_y, width = loads.shape
    loads = jnp.transpose(loads, (0, 1, 3, 2, 4))
    modal_disp = jnp.transpose(modal_disp, (0, 1, 3, 2, 4))
    modulus = jnp.transpose(lookup_modulus(material, moduli), (1, 0, 2))
    plane = (samples, 3, rows_y, width)
    plane_size = samples * 3 * rows_y * width

    first = jnp.concatenate([modal_disp[:, :, :, 0].reshape(-1), modulus[:, 0].reshape(-1)])
    last = jnp.concatenate([modal_disp[:, :, :, depth - 1].reshape(-1), modulus[:, depth - 1].reshape(-1)])
    below, above = exchange(first, last, up_dev, low_dev)
    mod_ext = jnp.concatenate(
        [
            below[plane_size:].reshape(rows_y, 1, width),
            modulus,
            above[plane_size:].reshape(rows_y, 1, width),
        ],
        axis=1,
    )
    centre_mod, edges = edges_of(mod_ext, depth)
    jacobi = diagonal_of(centre_mod, edges)
    edges = jnp.stack(edges, axis=0)

    def apply(field):
        below, above = exchange(field[:, :, :, 0], field[:, :, :, depth - 1], up_dev, low_dev)
        return stiffness(field, below, above, edges, centre_mod)

    theta = (high_bound[0] + low_bound[0]) / 2.0
    half = (high_bound[0] - low_bound[0]) / 2.0
    sigma = theta / half
    rho0 = 1.0 / sigma
    rho1 = 1.0 / (2.0 * sigma - rho0)
    first_k = stiffness(
        modal_disp,
        below[:plane_size].reshape(plane),
        above[:plane_size].reshape(plane),
        edges,
        centre_mod,
    )
    start = loads - first_k
    step0 = start / (theta * jacobi)
    residual1 = start - apply(step0)
    step1 = rho1 * rho0 * step0 + 2.0 * rho1 / half * residual1 / jacobi
    displacement = modal_disp + step0 + step1
    residual = residual1 - apply(step1)
    return (
        jnp.transpose(displacement, (0, 1, 3, 2, 4)),
        jnp.transpose(residual, (0, 1, 3, 2, 4)),
    )


def solution(mesh):
    devices = mesh.devices.reshape(-1)
    grid = Mesh(devices.reshape(devices.size // GROUP, GROUP), ("col", "grp"))
    slab = ("col", "grp")
    in_specs = (
        P(None, None, slab, None, None),
        P(None, None, slab, None, None),
        P(slab, None, None),
        P(),
        P(),
        P(),
        P(),
        P(),
    )
    out_specs = (P(None, None, slab, None, None), P(None, None, slab, None, None))
    return jax.shard_map(
        on_device, mesh=grid, in_specs=in_specs, out_specs=out_specs, check_vma=False
    )
```

profile of v0, /device:TPU:0, one launch (start us, length us, event | category | flops | bytes accessed | tf_op | source)
XLA Modules:
  0.0 262.6 jit_solution(12644074746678601435)
XLA Ops:
  12.7 13.4 %all-gather.3 = f32[8,2,3328]{2,1,0:T(2,128)S(1)} all-gather(f32[1,2,3328]{2,1,0:T(2,128)S(1)} %maximum_bitcast_fusion), channel_id=2, replica_groups=mesh['col'=16,'grp'=8] {'grp'}, dimensions={0}, use_global_device_ids=true | all-gather | bytes 239616 | tf_op jit(solution)/shard_map/all_gather | solution.py:199
  29.2 7.9 %all-to-all-start = ((f32[16,2,3328]{2,1,0:T(2,128)}), f32[16,2,3328]{2,1,0:T(2,128)S(1)}, u32[]{:S(2)}, u32[]{:S(2)}) async-start(f32[16,2,3328]{2,1,0:T(2,128)} %copy.74), calls=%async_computation | async-start | bytes 851968 | tf_op jit(solution)/shard_map/all_to_all | solution.py:211
  48.4 4.9 %bitcast_dynamic-update-slice_fusion.25 = f32[26,2,64,128]{3,2,1,0:T(8,128)S(1)} fusion(f32[2,64,127]{2,1,0:T(8,128)S(1)} %get-tuple-element.59, f32[]{:T(128)} %bitcast.16, f32[]{:T(128)} %bitcast.15, f32[]{:T(128)} %bitcast.14, f32[]{:T(128)} %bitcast.13, f32[]{:T(128)} %bitcast.12, f32[]{:T(128)} %bitcast.11, f32[]{:T(128)} %bitcast.10, f32[]{:T(128)} %bitcast.9, ...), kind=kLoop, calls=%fused_computation.93 | loop fusion | flops 409599 | bytes 196128
  58.2 4.9 %bitcast_dynamic-update-slice_fusion.23 = f32[26,2,64,128]{3,2,1,0:T(8,128)S(1)} fusion(f32[26,2,64,128]{3,2,1,0:T(8,128)S(1)} %bitcast_dynamic-update-slice_fusion.24, f32[2,64,127]{2,1,0:T(8,128)S(1)} %get-tuple-element.58, f32[]{:T(128)} %bitcast.16, f32[]{:T(128)} %bitcast.15, f32[]{:T(128)} %bitcast.14, f32[]{:T(128)} %bitcast.13, f32[]{:T(128)} %bitcast.12, ...), kind=kLoop, calls=%fused_computation.91 | loop fusion | flops 409600 | bytes 196640
  63.0 4.9 %bitcast_dynamic-update-slice_fusion.22 = f32[26,2,64,128]{3,2,1,0:T(8,128)S(1)} fusion(f32[26,2,64,128]{3,2,1,0:T(8,128)S(1)} %bitcast_dynamic-update-slice_fusion.23, f32[2,64,127]{2,1,0:T(8,128)S(1)} %get-tuple-element.42, f32[]{:T(128)} %bitcast.16, f32[]{:T(128)} %bitcast.15, f32[]{:T(128)} %bitcast.14, f32[]{:T(128)} %bitcast.13, f32[]{:T(128)} %bitcast.12, ...), kind=kLoop, calls=%fused_computation.90 | loop fusion | flops 409600 | bytes 196640
  67.9 4.9 %bitcast_dynamic-update-slice_fusion.20 = f32[26,2,64,128]{3,2,1,0:T(8,128)S(1)} fusion(f32[26,2,64,128]{3,2,1,0:T(8,128)S(1)} %get-tuple-element.14, f32[2,64,127]{2,1,0:T(8,128)S(1)} %get-tuple-element.43, f32[]{:T(128)} %bitcast.16, f32[]{:T(128)} %bitcast.15, f32[]{:T(128)} %bitcast.14, f32[]{:T(128)} %bitcast.13, f32[]{:T(128)} %bitcast.12, ...), kind=kLoop, calls=%fused_computation.88 | loop fusion | flops 409600 | bytes 196640
  72.8 4.9 %bitcast_dynamic-update-slice_fusion.19 = f32[26,2,64,128]{3,2,1,0:T(8,128)S(1)} fusion(f32[26,2,64,128]{3,2,1,0:T(8,128)S(1)} %bitcast_dynamic-update-slice_fusion.20, f32[2,64,127]{2,1,0:T(8,128)S(1)} %get-tuple-element.49, f32[]{:T(128)} %bitcast.16, f32[]{:T(128)} %bitcast.15, f32[]{:T(128)} %bitcast.14, f32[]{:T(128)} %bitcast.13, f32[]{:T(128)} %bitcast.12, ...), kind=kLoop, calls=%fused_computation.87 | loop fusion | flops 409600 | bytes 196640
  77.7 4.9 %bitcast_dynamic-update-slice_fusion.17 = f32[26,2,64,128]{3,2,1,0:T(8,128)S(1)} fusion(f32[26,2,64,128]{3,2,1,0:T(8,128)S(1)} %bitcast_dynamic-update-slice_fusion.18, f32[2,64,127]{2,1,0:T(8,128)S(1)} %get-tuple-element.48, f32[]{:T(128)} %bitcast.16, f32[]{:T(128)} %bitcast.15, f32[]{:T(128)} %bitcast.14, f32[]{:T(128)} %bitcast.13, f32[]{:T(128)} %bitcast.12, ...), kind=kLoop, calls=%fused_computation.85 | loop fusion | flops 409600 | bytes 196640
  82.5 4.9 %bitcast_dynamic-update-slice_fusion.16 = f32[26,2,64,128]{3,2,1,0:T(8,128)S(1)} fusion(f32[26,2,64,128]{3,2,1,0:T(8,128)S(1)} %bitcast_dynamic-update-slice_fusion.17, f32[2,64,127]{2,1,0:T(8,128)S(1)} %get-tuple-element.57, f32[]{:T(128)} %bitcast.16, f32[]{:T(128)} %bitcast.15, f32[]{:T(128)} %bitcast.14, f32[]{:T(128)} %bitcast.13, f32[]{:T(128)} %bitcast.12, ...), kind=kLoop, calls=%fused_computation.84 | loop fusion | flops 409600 | bytes 196640
  92.3 4.9 %bitcast_dynamic-update-slice_fusion.14 = f32[26,2,64,128]{3,2,1,0:T(8,128)S(1)} fusion(f32[26,2,64,128]{3,2,1,0:T(8,128)S(1)} %bitcast_dynamic-update-slice_fusion.15, f32[2,64,127]{2,1,0:T(8,128)S(1)} %get-tuple-element.56, f32[]{:T(128)} %bitcast.16, f32[]{:T(128)} %bitcast.15, f32[]{:T(128)} %bitcast.14, f32[]{:T(128)} %bitcast.13, f32[]{:T(128)} %bitcast.12, ...), kind=kLoop, calls=%fused_computation.82 | loop fusion | flops 409600 | bytes 196640
  97.1 4.9 %bitcast_dynamic-update-slice_fusion.13 = f32[26,2,64,128]{3,2,1,0:T(8,128)S(1)} fusion(f32[26,2,64,128]{3,2,1,0:T(8,128)S(1)} %bitcast_dynamic-update-slice_fusion.14, f32[2,64,127]{2,1,0:T(8,128)S(1)} %get-tuple-element.41, f32[]{:T(128)} %bitcast.16, f32[]{:T(128)} %bitcast.15, f32[]{:T(128)} %bitcast.14, f32[]{:T(128)} %bitcast.13, f32[]{:T(128)} %bitcast.12, ...), kind=kLoop, calls=%fused_computation.81 | loop fusion | flops 409600 | bytes 196640
  106.9 4.9 %bitcast_dynamic-update-slice_fusion.11 = f32[26,2,64,128]{3,2,1,0:T(8,128)S(1)} fusion(f32[26,2,64,128]{3,2,1,0:T(8,128)S(1)} %bitcast_dynamic-update-slice_fusion.12, f32[2,64,127]{2,1,0:T(8,128)S(1)} %get-tuple-element.55, f32[]{:T(128)} %bitcast.16, f32[]{:T(128)} %bitcast.15, f32[]{:T(128)} %bitcast.14, f32[]{:T(128)} %bitcast.13, f32[]{:T(128)} %bitcast.12, ...), kind=kLoop, calls=%fused_computation.79 | loop fusion | flops 409600 | bytes 196640
  116.6 4.9 %bitcast_dynamic-update-slice_fusion.9 = f32[26,2,64,128]{3,2,1,0:T(8,128)S(1)} fusion(f32[26,2,64,128]{3,2,1,0:T(8,128)S(1)} %bitcast_dynamic-update-slice_fusion.10, f32[2,64,127]{2,1,0:T(8,128)S(1)} %get-tuple-element.54, f32[]{:T(128)} %bitcast.16, f32[]{:T(128)} %bitcast.15, f32[]{:T(128)} %bitcast.14, f32[]{:T(128)} %bitcast.13, f32[]{:T(128)} %bitcast.12, ...), kind=kLoop, calls=%fused_computation.77 | loop fusion | flops 409600 | bytes 196640
  121.4 4.9 %bitcast_dynamic-update-slice_fusion.8 = f32[26,2,64,128]{3,2,1,0:T(8,128)S(1)} fusion(f32[26,2,64,128]{3,2,1,0:T(8,128)S(1)} %bitcast_dynamic-update-slice_fusion.9, f32[2,64,127]{2,1,0:T(8,128)S(1)} %get-tuple-element.53, f32[]{:T(128)} %bitcast.16, f32[]{:T(128)} %bitcast.15, f32[]{:T(128)} %bitcast.14, f32[]{:T(128)} %bitcast.13, f32[]{:T(128)} %bitcast.12, ...), kind=kLoop, calls=%fused_computation.76 | loop fusion | flops 409600 | bytes 196640
  136.0 4.9 %bitcast_dynamic-update-slice_fusion.5 = f32[26,2,64,128]{3,2,1,0:T(8,128)S(1)} fusion(f32[26,2,64,128]{3,2,1,0:T(8,128)S(1)} %bitcast_dynamic-update-slice_fusion.6, f32[2,64,127]{2,1,0:T(8,128)S(1)} %get-tuple-element.33, f32[]{:T(128)} %bitcast.16, f32[]{:T(128)} %bitcast.15, f32[]{:T(128)} %bitcast.14, f32[]{:T(128)} %bitcast.13, f32[]{:T(128)} %bitcast.12, ...), kind=kLoop, calls=%fused_computation.73 | loop fusion | flops 409600 | bytes 196640
  148.6 4.9 %bitcast_dynamic-update-slice_fusion.2 = f32[26,2,64,128]{3,2,1,0:T(8,128)S(1)} fusion(f32[26,2,64,128]{3,2,1,0:T(8,128)S(1)} %bitcast_dynamic-update-slice_fusion.3, f32[2,64,127]{2,1,0:T(8,128)S(1)} %get-tuple-element.37, f32[]{:T(128)} %bitcast.16, f32[]{:T(128)} %bitcast.15, f32[]{:T(128)} %bitcast.14, f32[]{:T(128)} %bitcast.13, f32[]{:T(128)} %bitcast.12, ...), kind=kLoop, calls=%fused_computation.70 | loop fusion | flops 409600 | bytes 196640
  161.4 7.3 %shard_map.95 = f32[4,3,2,64,128]{4,3,2,1,0:T(8,128)} custom-call(f32[4,3,2,80,128]{4,3,2,1,0:T(8,128)} %concatenate.132.field_ref, f32[26,2,64,128]{3,2,1,0:T(8,128)} %copy-done.3, f32[2,64,128]{2,1,0:T(8,128)} %copy-done.2), custom_call_target="tpu_custom_call" | custom-call | flops 102236160 | bytes 3407872 | tf_op jit(solution)/shard_map/pallas_call | solution.py:167
  171.6 12.8 %all-gather.1 = f32[16,4,3,2,128]{4,1,3,2,0:T(4,128)S(1)} all-gather(f32[2,4,3,2,128]{4,1,3,2,0:T(4,128)S(1)} %copy.76), channel_id=3, replica_groups=mesh['col'=16,'grp'=8] {'grp'}, dimensions={0}, use_global_device_ids=true | all-gather | bytes 221184 | tf_op jit(solution)/shard_map/all_gather | solution.py:199
  187.0 5.8 %all-to-all-start.1 = ((f32[16,2,4,3,2,128]{5,4,3,2,1,0:T(2,128)}), f32[16,2,4,3,2,128]{5,4,3,2,1,0:T(2,128)S(1)}, u32[]{:S(2)}, u32[]{:S(2)}) async-start(f32[16,2,4,3,2,128]{5,4,3,2,1,0:T(2,128)} %pad_maximum_fusion.1), calls=%async_computation.1 | async-start | bytes 786432 | tf_op jit(solution)/shard_map/all_to_all | solution.py:211
  192.9 10.2 %all-to-all-done.1 = f32[16,2,4,3,2,128]{5,4,3,2,1,0:T(2,128)S(1)} async-done(((f32[16,2,4,3,2,128]{5,4,3,2,1,0:T(2,128)}), f32[16,2,4,3,2,128]{5,4,3,2,1,0:T(2,128)S(1)}, u32[]{:S(2)}, u32[]{:S(2)}) %all-to-all-start.1) | async-done | bytes 393248 | tf_op jit(solution)/shard_map/all_to_all | solution.py:211
  206.0 7.3 %shard_map.96 = f32[4,3,2,64,128]{4,3,2,1,0:T(8,128)} custom-call(f32[4,3,2,80,128]{4,3,2,1,0:T(8,128)} %concatenate.159.field_ref, f32[26,2,64,128]{3,2,1,0:T(8,128)} %copy-done.3, f32[2,64,128]{2,1,0:T(8,128)} %copy-done.2), custom_call_target="tpu_custom_call" | custom-call | flops 102236160 | bytes 3407872 | tf_op jit(solution)/shard_map/pallas_call | solution.py:167
  216.8 12.9 %all-gather.2 = f32[16,4,3,2,128]{4,1,3,2,0:T(4,128)S(1)} all-gather(f32[2,4,3,2,128]{4,1,3,2,0:T(4,128)S(1)} %copy.82), channel_id=4, replica_groups=mesh['col'=16,'grp'=8] {'grp'}, dimensions={0}, use_global_device_ids=true | all-gather | bytes 221184 | tf_op jit(solution)/shard_map/all_gather | solution.py:199
  239.7 9.1 %all-to-all-done.2 = f32[16,2,4,3,2,128]{5,4,3,2,1,0:T(2,128)} async-done(((f32[16,2,4,3,2,128]{5,4,3,2,1,0:T(2,128)}), f32[16,2,4,3,2,128]{5,4,3,2,1,0:T(2,128)}, u32[]{:S(2)}, u32[]{:S(2)}) %all-to-all-start.2) | async-done | bytes 393248 | tf_op jit(solution)/shard_map/all_to_all | solution.py:211
  252.5 7.3 %shard_map.97 = f32[4,3,2,64,128]{4,3,2,1,0:T(8,128)} custom-call(f32[4,3,2,80,128]{4,3,2,1,0:T(8,128)} %concatenate.160.field_ref, f32[26,2,64,128]{3,2,1,0:T(8,128)} %copy-done.3, f32[2,64,128]{2,1,0:T(8,128)} %copy-done.2), custom_call_target="tpu_custom_call" | custom-call | flops 102236160 | bytes 3407872 | tf_op jit(solution)/shard_map/pallas_call | solution.py:167
  (118 shorter events, 91.3 us)
Async XLA Ops:
  0.6 1.8 copy-start
  0.6 6.2 %copy-start.13 = (f32[8]{0:T(128)S(1)}, f32[8]{0:T(128)}, u32[]{:S(2)}) copy-start(f32[8]{0:T(128)} %param.11) | copy-start | bytes 100
  0.7 6.9 %copy-start.1 = (s32[64,2,128]{2,1,0:T(2,128)S(1)}, s32[64,2,128]{2,1,0:T(2,128)}, u32[]{:S(2)}) copy-start(s32[64,2,128]{2,1,0:T(2,128)} %param.10) | copy-start | bytes 196612
  0.7 11.8 %copy-start.9 = (f32[4,3,64,2,128]{4,3,2,1,0:T(2,128)S(1)}, f32[4,3,64,2,128]{4,3,2,1,0:T(2,128)}, u32[]{:S(2)}) copy-start(f32[4,3,64,2,128]{4,3,2,1,0:T(2,128)} %param.9) | copy-start | bytes 2359300
  12.4 141.1 %copy-start.2 = (f32[2,64,128]{2,1,0:T(8,128)}, f32[2,64,128]{2,1,0:T(8,128)S(1)}, u32[]{:S(2)}) copy-start(f32[2,64,128]{2,1,0:T(8,128)S(1)} %add_bitcast_fusion.4.cm_ref) | copy-start | bytes 196612
  29.2 18.5 %all-to-all-start = ((f32[16,2,3328]{2,1,0:T(2,128)}), f32[16,2,3328]{2,1,0:T(2,128)S(1)}, u32[]{:S(2)}, u32[]{:S(2)}) async-start(f32[16,2,3328]{2,1,0:T(2,128)} %copy.74), calls=%async_computation | async-start | bytes 851968 | tf_op jit(solution)/shard_map/all_to_all | solution.py:211
  158.3 3.0 %copy-start.3 = (f32[26,2,64,128]{3,2,1,0:T(8,128)}, f32[26,2,64,128]{3,2,1,0:T(8,128)S(1)}, u32[]{:S(2)}) copy-start(f32[26,2,64,128]{3,2,1,0:T(8,128)S(1)} %bitcast_dynamic-update-slice_fusion.edge_ref) | copy-start | bytes 5111812
  161.4 7.3 %copy-start.11 = (f32[1,2,64,128]{3,2,1,0:T(8,128)S(1)}, f32[1,2,64,128]{3,2,1,0:T(8,128)}, u32[]{:S(2)}) copy-start(f32[1,2,64,128]{3,2,1,0:T(8,128)} %add_bitcast_fusion.1) | copy-start | bytes 196612
  161.4 7.3 %copy-start.12 = (f32[1,2,64,128]{3,2,1,0:T(8,128)S(1)}, f32[1,2,64,128]{3,2,1,0:T(8,128)}, u32[]{:S(2)}) copy-start(f32[1,2,64,128]{3,2,1,0:T(8,128)} %add_bitcast_fusion.3) | copy-start | bytes 196612
  161.4 8.8 %copy-start.6 = (f32[4,3,64,2,128]{4,3,2,1,0:T(2,128)S(1)}, f32[4,3,64,2,128]{4,3,2,1,0:T(2,128)}, u32[]{:S(2)}) copy-start(f32[4,3,64,2,128]{4,3,2,1,0:T(2,128)} %param.8) | copy-start | bytes 2359300
  187.0 16.1 %all-to-all-start.1 = ((f32[16,2,4,3,2,128]{5,4,3,2,1,0:T(2,128)}), f32[16,2,4,3,2,128]{5,4,3,2,1,0:T(2,128)S(1)}, u32[]{:S(2)}, u32[]{:S(2)}) async-start(f32[16,2,4,3,2,128]{5,4,3,2,1,0:T(2,128)} %pad_maximum_fusion.1), calls=%async_computation.1 | async-start | bytes 786432 | tf_op jit(solution)/shard_map/all_to_all | solution.py:211
  206.0 7.3 %copy-start.4 = (f32[4,3,2,64,128]{4,3,2,1,0:T(8,128)S(1)}, f32[4,3,2,64,128]{4,3,2,1,0:T(8,128)}, u32[]{:S(2)}) copy-start(f32[4,3,2,64,128]{4,3,2,1,0:T(8,128)} %shard_map.95) | copy-start | bytes 2359300
  215.8 0.9 copy-start.7
  216.8 21.5 %copy-start.10 = (f32[4,3,64,2,128]{4,2,3,1,0:T(8,128)S(1)}, f32[4,3,64,2,128]{4,2,3,1,0:T(8,128)}, u32[]{:S(2)}) copy-start(f32[4,3,64,2,128]{4,2,3,1,0:T(8,128)} %get-tuple-element.10) | copy-start | bytes 2359300
  231.9 17.7 %copy-start.8 = (f32[4,3,2,64,128]{4,3,2,1,0:T(8,128)S(1)}, f32[4,3,2,64,128]{4,3,2,1,0:T(8,128)}, u32[]{:S(2)}) copy-start(f32[4,3,2,64,128]{4,3,2,1,0:T(8,128)} %copy-done.7) | copy-start | bytes 2359300
  234.0 14.8 %all-to-all-start.2 = ((f32[16,2,4,3,2,128]{5,4,3,2,1,0:T(2,128)}), f32[16,2,4,3,2,128]{5,4,3,2,1,0:T(2,128)}, u32[]{:S(2)}, u32[]{:S(2)}) async-start(f32[16,2,4,3,2,128]{5,4,3,2,1,0:T(2,128)} %pad_maximum_fusion.2), calls=%async_computation.2 | async-start | bytes 786432 | tf_op jit(solution)/shard_map/all_to_all | solution.py:211
  252.5 7.3 %copy-start.5 = (f32[4,3,2,64,128]{4,3,2,1,0:T(8,128)S(1)}, f32[4,3,2,64,128]{4,3,2,1,0:T(8,128)}, u32[]{:S(2)}) copy-start(f32[4,3,2,64,128]{4,3,2,1,0:T(8,128)} %shard_map.96) | copy-start | bytes 2359300
where the time goes:
time: 265 us; the launch traced here: 263 us
  other arithmetic  127 us (48%)
  blocking collectives  39.2 us (15%)
  local copies, waits for them, and re-layouts  26.8 us (10%)
  Pallas kernels  21.8 us (8%)
  waiting for transfers between devices  20.7 us (8%)
  starting transfers between devices  17.9 us (7%)
  between operations  9.36 us (4%)
    unnamed x26, other arithmetic  102 us
    all_gather x3, blocking collectives, exchange(): held = lax.all_gather(pack, 'grp', axis=0, tiled=True)  39.2 us
    pallas_call x3, Pallas kernels, stiffness(): pl.pallas_call(stencil_kernel, out_shape=jax.ShapeDtypeStruct(field.shape...  21.8 us
    all_to_all x3, waiting for transfers between devices, exchange(): got = lax.all_to_all(slots, 'col', 0, 0, tiled=True)  20.7 us
    all_to_all x3, starting transfers between devices, exchange(): got = lax.all_to_all(slots, 'col', 0, 0, tiled=True)  17.9 us
    concatenate x3, local copies, waits for them, and re-layouts, stiffness(): jnp.concatenate([zeros, below[:, :, :, None], field, above[:, :, :, None]...  8.78 us
  transfers between devices with their start and end apart: 3, of which 3 were waited for; matrix products, arithmetic and copies ran while one was open for 1% of the time, Pallas kernels for 0%

commit v1 on v0

--- a/solution.py
+++ b/solution.py
@@ -7,7 +7,6 @@
 
 MATERIALS = 8
 GROUP = 8
-PAD = 8
 
 GAMMA = 0.2
 BETA = 0.5
@@ -54,21 +53,116 @@
     return jnp.stack(comps, axis=0)
 
 
-def stencil_kernel(field_ref, edge_ref, cm_ref, out_ref):
-    samples, _, rows_y, padded, width = field_ref.shape
-    depth = padded - 2 * PAD
+def edges_kernel(mod_ref, below_ref, above_ref, edge_ref, centre_ref, diag_ref):
+    rows_y, depth, width = mod_ref.shape
     chunks = depth // 8
     sub = lax.broadcasted_iota(jnp.int32, (8, width), 0)
     lane = lax.broadcasted_iota(jnp.int32, (8, width), 1)
 
     def body(it, carry):
+        r = pl.multiple_of(it * 8, 8)
+        centre = [mod_ref[y, pl.ds(r, 8), :] for y in range(rows_y)]
+        prev = [
+            jnp.where(it == 0, below_ref[y], mod_ref[y, pl.ds(jnp.maximum(r - 8, 0), 8), :])
+            for y in range(rows_y)
+        ]
+        nxt = [
+            jnp.where(
+                it == chunks - 1, above_ref[y], mod_ref[y, pl.ds(jnp.minimum(r + 8, depth - 8), 8), :]
+            )
+            for y in range(rows_y)
+        ]
+        comps = [[GAMMA * centre[y] for y in range(rows_y)] for c in range(3)]
+        index = 0
+        for off_x in (-1, 0, 1):
+            if off_x == 0:
+                shifted_x = centre
+            elif off_x < 0:
+                shifted_x = [
+                    jnp.where(sub == 0, pltpu.roll(prev[y], 1, 0), pltpu.roll(centre[y], 1, 0))
+                    for y in range(rows_y)
+                ]
+            else:
+                shifted_x = [
+                    jnp.where(sub == 7, pltpu.roll(nxt[y], 7, 0), pltpu.roll(centre[y], 7, 0))
+                    for y in range(rows_y)
+                ]
+            shifted = {0: shifted_x}
+            shifted[-1] = [jnp.where(lane == 0, jnp.float32(0.0), pltpu.roll(v, 1, 1)) for v in shifted_x]
+            shifted[1] = [
+                jnp.where(lane == width - 1, jnp.float32(0.0), pltpu.roll(v, width - 1, 1))
+                for v in shifted_x
+            ]
+            for off_y in (-1, 0, 1):
+                for off_z in (-1, 0, 1):
+                    if (off_x, off_y, off_z) == (0, 0, 0):
+                        continue
+                    offset = (off_x, off_y, off_z)
+                    norm_sq = off_x * off_x + off_y * off_y + off_z * off_z
+                    for y in range(rows_y):
+                        source = y + off_y
+                        if 0 <= source < rows_y:
+                            other = shifted[off_z][source]
+                        else:
+                            other = jnp.zeros_like(centre[y])
+                        edge = EDGE_WEIGHTS[norm_sq] * 0.5 * (centre[y] + other)
+                        edge_ref[index, y, pl.ds(r, 8), :] = edge
+                        for c in range(3):
+                            comps[c][y] = comps[c][y] + edge * (
+                                1.0 + BETA * offset[c] * offset[c] / norm_sq
+                            )
+                    index += 1
+        for y in range(rows_y):
+            centre_ref[y, pl.ds(r, 8), :] = centre[y]
+            for c in range(3):
+                diag_ref[c, y, pl.ds(r, 8), :] = comps[c][y]
+        return carry
+
+    lax.fori_loop(0, chunks, body, 0)
+
+
+def edges_and_diagonal(modulus, below, above):
+    rows_y, depth, width = modulus.shape
+    vmem = pl.BlockSpec(memory_space=pltpu.VMEM)
+    halo_below = jnp.broadcast_to(below[:, None], (rows_y, 8, width))
+    halo_above = jnp.broadcast_to(above[:, None], (rows_y, 8, width))
+    return pl.pallas_call(
+        edges_kernel,
+        out_shape=(
+            jax.ShapeDtypeStruct((len(OFFSETS), rows_y, depth, width), jnp.float32),
+            jax.ShapeDtypeStruct((rows_y, depth, width), jnp.float32),
+            jax.ShapeDtypeStruct((3, rows_y, depth, width), jnp.float32),
+        ),
+        in_specs=[vmem, vmem, vmem],
+        out_specs=(vmem, vmem, vmem),
+    )(modulus, halo_below, halo_above)
+
+
+def stencil_kernel(field_ref, below_ref, above_ref, edge_ref, cm_ref, out_ref):
+    samples, _, rows_y, depth, width = field_ref.shape
+    chunks = depth // 8
+    sub = lax.broadcasted_iota(jnp.int32, (8, width), 0)
+    lane = lax.broadcasted_iota(jnp.int32, (8, width), 1)
+
+    def body(it, carry):
         s = it // chunks
         r = pl.multiple_of((it % chunks) * 8, 8)
 
+        first = (it % chunks) == 0
+        last = (it % chunks) == chunks - 1
+
         def rows(c, y, off):
-            return field_ref[s, c, y, pl.ds(r + off, 8), :]
-
-        centre = [[rows(c, y, PAD) for y in range(rows_y)] for c in range(3)]
+            if off == 0:
+                return field_ref[s, c, y, pl.ds(r, 8), :]
+            if off < 0:
+                return jnp.where(
+                    first, below_ref[s, c, y], field_ref[s, c, y, pl.ds(jnp.maximum(r - 8, 0), 8), :]
+                )
+            return jnp.where(
+                last, above_ref[s, c, y], field_ref[s, c, y, pl.ds(jnp.minimum(r + 8, depth - 8), 8), :]
+            )
+
+        centre = [[rows(c, y, 0) for y in range(rows_y)] for c in range(3)]
         acc = [
             [GAMMA * cm_ref[y, pl.ds(r, 8), :] * centre[c][y] for y in range(rows_y)]
             for c in range(3)
@@ -82,7 +176,7 @@
                     [
                         jnp.where(
                             sub == 0,
-                            pltpu.roll(rows(c, y, PAD - 8), 1, 0),
+                            pltpu.roll(rows(c, y, -1), 1, 0),
                             pltpu.roll(centre[c][y], 1, 0),
                         )
                         for y in range(rows_y)
@@ -94,7 +188,7 @@
                     [
                         jnp.where(
                             sub == 7,
-                            pltpu.roll(rows(c, y, PAD + 8), 7, 0),
+                            pltpu.roll(rows(c, y, 1), 7, 0),
                             pltpu.roll(centre[c][y], 7, 0),
                         )
                         for y in range(rows_y)
@@ -160,17 +254,18 @@
 
 def stiffness(field, below, above, edges, centre_mod):
     samples, _, rows_y, depth, width = field.shape
-    zeros = jnp.zeros((samples, 3, rows_y, PAD - 1, width), jnp.float32)
-    padded = jnp.concatenate([zeros, below[:, :, :, None], field, above[:, :, :, None], zeros], axis=3)
+    halo_shape = (samples, 3, rows_y, 8, width)
+    halo_below = jnp.broadcast_to(below[:, :, :, None], halo_shape)
+    halo_above = jnp.broadcast_to(above[:, :, :, None], halo_shape)
     vmem = pl.BlockSpec(memory_space=pltpu.VMEM)
     size = samples * 3 * rows_y * depth * width
     return pl.pallas_call(
         stencil_kernel,
         out_shape=jax.ShapeDtypeStruct(field.shape, jnp.float32),
-        in_specs=[vmem, vmem, vmem],
+        in_specs=[vmem] * 5,
         out_specs=vmem,
         cost_estimate=pl.CostEstimate(flops=26 * 20 * size, bytes_accessed=4 * (2 * size + 28 * size // samples // 3), transcendentals=0),
-    )(padded, edges, centre_mod)
+    )(field, halo_below, halo_above, edges, centre_mod)
 
 
 def lookup_modulus(material, moduli):
@@ -230,17 +325,11 @@
     first = jnp.concatenate([modal_disp[:, :, :, 0].reshape(-1), modulus[:, 0].reshape(-1)])
     last = jnp.concatenate([modal_disp[:, :, :, depth - 1].reshape(-1), modulus[:, depth - 1].reshape(-1)])
     below, above = exchange(first, last, up_dev, low_dev)
-    mod_ext = jnp.concatenate(
-        [
-            below[plane_size:].reshape(rows_y, 1, width),
-            modulus,
-            above[plane_size:].reshape(rows_y, 1, width),
-        ],
-        axis=1,
-    )
-    centre_mod, edges = edges_of(mod_ext, depth)
-    jacobi = diagonal_of(centre_mod, edges)
-    edges = jnp.stack(edges, axis=0)
+    edges, centre_mod, jacobi = edges_and_diagonal(
+        modulus,
+        below[plane_size:].reshape(rows_y, width),
+        above[plane_size:].reshape(rows_y, width),
+    )
 
     def apply(field):
         below, above = exchange(field[:, :, :, 0], field[:, :, :, depth - 1], up_dev, low_dev)

time: 265 us -> 149 us (0.56)
  other arithmetic: 127 us -> 14 us
  local copies, waits for them, and re-layouts: 26.8 us -> 23.2 us
  Pallas kernels: 21.8 us -> 25.1 us
    unnamed x26 -> x1, other arithmetic: 102 us -> 0.03 us
    another operation x5 -> x0, other arithmetic: 9.18 us -> none  [the longest x1 4.85 us: on_device(): edges = jnp.stack(edges, axis=0)]
    concatenate x3 -> x0, local copies, waits for them, and re-layouts: 8.78 us -> none  [stiffness(): jnp.concatenate([zeros, below[:, :, :, None], field, above[:, :, :, None]...]
    broadcast_in_dim x0 -> x8, local copies, waits for them, and re-layouts: none -> 5.05 us  [the longest x3 1.94 us: stiffness(): halo_below = jnp.broadcast_to(below[:, :, :, None], halo_shape)]
    pallas_call x0 -> x1, Pallas kernels: none -> 3.02 us  [edges_and_diagonal(): pl.pallas_call(edges_kernel, out_shape=(jax.ShapeDtypeStruct((len(OFFSETS...]
  transfers between devices with their start and end apart: 3 -> 3, of which waited for: 3 -> 3; matrix products, arithmetic and copies ran while one was open for 1% -> 2% of each run, Pallas kernels for 0% -> 0%
where the time goes in v1:
time: 149 us; the launch traced here: 148 us
  blocking collectives  39 us (26%)
  Pallas kernels  25.1 us (17%)
  local copies, waits for them, and re-layouts  23.2 us (16%)
  waiting for transfers between devices  21.3 us (14%)
  starting transfers between devices  16.6 us (11%)
  other arithmetic  14 us (9%)
  between operations  8.6 us (6%)
    all_gather x3, blocking collectives, exchange(): held = lax.all_gather(pack, 'grp', axis=0, tiled=True)  39 us
    pallas_call x3, Pallas kernels, stiffness(): pl.pallas_call(stencil_kernel, out_shape=jax.ShapeDtypeStruct(field.shape...  22.1 us
    all_to_all x3, waiting for transfers between devices, exchange(): got = lax.all_to_all(slots, 'col', 0, 0, tiled=True)  21.3 us
    all_to_all x3, starting transfers between devices, exchange(): got = lax.all_to_all(slots, 'col', 0, 0, tiled=True)  16.6 us
    transpose x1, other arithmetic, on_device(): modulus = jnp.transpose(lookup_modulus(material, moduli), (1, 0, 2))  5.06 us
    unnamed x33, local copies, waits for them, and re-layouts  3.13 us
    pallas_call x1, Pallas kernels, edges_and_diagonal(): pl.pallas_call(edges_kernel, out_shape=(jax.ShapeDtypeStruct((len(OFFSETS...  3.02 us
  transfers between devices with their start and end apart: 3, of which 3 were waited for; matrix products, arithmetic and copies ran while one was open for 2% of the time, Pallas kernels for 0%

profile of v1, /device:TPU:0, one launch (start us, length us, event | category | flops | bytes accessed | tf_op | source)
XLA Modules:
  0.0 147.9 jit_solution(6808071444439881213)
XLA Ops:
  2.5 1.5 %gather_fusion.1 = s32[128]{0:T(128)S(1)} fusion(s32[2,128]{1,0:T(2,128)S(1)} %copy-done, s32[128]{0:T(128)S(1)} %get-tuple-element.20), kind=kCustom, calls=%fused_computation.1 | custom fusion | bytes 2048 | tf_op jit(solution)/shard_map/gather | solution.py:283
  4.0 1.5 %gather_fusion = s32[128]{0:T(128)S(1)} fusion(s32[2,128]{1,0:T(2,128)S(1)} %copy-done, s32[128]{0:T(128)S(1)} %fusion.17), kind=kCustom, calls=%fused_computation | custom fusion | bytes 2048 | tf_op jit(solution)/shard_map/gather | solution.py:284
  7.6 5.1 %add_bitcast_fusion.1.mod_ref = f32[2,64,128]{2,1,0:T(8,128)S(1)} fusion(s32[64,2,128]{2,1,0:T(2,128)S(1)} %copy-done.12, f32[]{:T(128)} %bitcast.16, f32[]{:T(128)} %bitcast.15, f32[]{:T(128)} %bitcast.14, f32[]{:T(128)} %bitcast.13, f32[]{:T(128)} %bitcast.12, f32[]{:T(128)} %bitcast.11, f32[]{:T(128)} %bitcast.10, f32[]{:T(128)} %bitcast.9), kind=kLoop, calls=%fused_computation.28 | loop fusion | flops 376832 | bytes 131104 | tf_op jit(solution)/shard_map/transpose | solution.py:321
  12.9 13.4 %all-gather.3 = f32[8,2,3328]{2,1,0:T(2,128)S(1)} all-gather(f32[1,2,3328]{2,1,0:T(2,128)S(1)} %maximum_bitcast_fusion), channel_id=2, replica_groups=mesh['col'=16,'grp'=8] {'grp'}, dimensions={0}, use_global_device_ids=true | all-gather | bytes 239616 | tf_op jit(solution)/shard_map/all_gather | solution.py:294
  28.3 1.1 copy.86
  29.4 7.9 %all-to-all-start = ((f32[16,2,3328]{2,1,0:T(2,128)}), f32[16,2,3328]{2,1,0:T(2,128)S(1)}, u32[]{:S(2)}, u32[]{:S(2)}) async-start(f32[16,2,3328]{2,1,0:T(2,128)} %copy.86), calls=%async_computation | async-start | bytes 851968 | tf_op jit(solution)/shard_map/all_to_all | solution.py:306
  45.7 2.2 %all-to-all-done = f32[16,2,3328]{2,1,0:T(2,128)S(1)} async-done(((f32[16,2,3328]{2,1,0:T(2,128)}), f32[16,2,3328]{2,1,0:T(2,128)S(1)}, u32[]{:S(2)}, u32[]{:S(2)}) %all-to-all-start) | async-done | bytes 426016 | tf_op jit(solution)/shard_map/all_to_all | solution.py:306
  49.2 3.0 %shard_map.95 = (f32[26,2,64,128]{3,2,1,0:T(8,128)}, f32[2,64,128]{2,1,0:T(8,128)}, f32[3,2,64,128]{3,2,1,0:T(8,128)}) custom-call(f32[2,64,128]{2,1,0:T(8,128)} %copy-done.11, f32[2,8,128]{2,1,0:T(8,128)} %broadcast_in_dim.200.below_ref, f32[2,8,128]{2,1,0:T(8,128)} %broadcast_in_dim.202.above_ref), custom_call_target="tpu_custom_call" | custom-call | tf_op jit(solution)/shard_map/pallas_call | solution.py:129
  54.5 7.4 %shard_map.96 = f32[4,3,2,64,128]{4,3,2,1,0:T(8,128)} custom-call(f32[4,3,2,64,128]{4,3,2,1,0:T(8,128)} %bitcast.100, f32[4,3,2,8,128]{4,3,2,1,0:T(8,128)} %broadcast_in_dim.196.below_ref, f32[4,3,2,8,128]{4,3,2,1,0:T(8,128)} %broadcast_in_dim.198.above_ref, f32[26,2,64,128]{3,2,1,0:T(8,128)} %get-tuple-element.5.edge_ref, f32[2,64,128]{2,1,0:T(8,128)} %get-tuple-element.6.cm_ref), custom_call_target="tpu_custom_call" | custom-call | flops 102236160 | bytes 3407872 | tf_op jit(solution)/shard_map/pallas_call | solution.py:262
  61.9 1.3 broadcast_divide_fusion.field_ref
  63.2 12.8 %all-gather.1 = f32[16,4,3,2,128]{4,1,3,2,0:T(4,128)S(1)} all-gather(f32[2,4,3,2,128]{4,1,3,2,0:T(4,128)S(1)} %copy.88), channel_id=3, replica_groups=mesh['col'=16,'grp'=8] {'grp'}, dimensions={0}, use_global_device_ids=true | all-gather | bytes 221184 | tf_op jit(solution)/shard_map/all_gather | solution.py:294
  78.5 5.0 %all-to-all-start.1 = ((f32[16,2,4,3,2,128]{5,2,4,3,1,0:T(4,128)}), f32[16,2,4,3,2,128]{5,2,4,3,1,0:T(4,128)S(1)}, u32[]{:S(2)}, u32[]{:S(2)}) async-start(f32[16,2,4,3,2,128]{5,2,4,3,1,0:T(4,128)} %copy.89), calls=%async_computation.1 | async-start | bytes 786432 | tf_op jit(solution)/shard_map/all_to_all | solution.py:306
  83.7 10.2 %all-to-all-done.1 = f32[16,2,4,3,2,128]{5,2,4,3,1,0:T(4,128)S(1)} async-done(((f32[16,2,4,3,2,128]{5,2,4,3,1,0:T(4,128)}), f32[16,2,4,3,2,128]{5,2,4,3,1,0:T(4,128)S(1)}, u32[]{:S(2)}, u32[]{:S(2)}) %all-to-all-start.1) | async-done | bytes 393248 | tf_op jit(solution)/shard_map/all_to_all | solution.py:306
  95.2 7.4 %shard_map.97 = f32[4,3,2,64,128]{4,3,2,1,0:T(8,128)} custom-call(f32[4,3,2,64,128]{4,3,2,1,0:T(8,128)} %copy-done.2, f32[4,3,2,8,128]{4,3,2,1,0:T(8,128)} %broadcast_in_dim.208.below_ref, f32[4,3,2,8,128]{4,3,2,1,0:T(8,128)} %broadcast_in_dim.209.above_ref, f32[26,2,64,128]{3,2,1,0:T(8,128)} %get-tuple-element.5.edge_ref, f32[2,64,128]{2,1,0:T(8,128)} %get-tuple-element.6.cm_ref), custom_call_target="tpu_custom_call" | custom-call | flops 102236160 | bytes 3407872 | tf_op jit(solution)/shard_map/pallas_call | solution.py:262
  102.6 2.7 %add_bitcast_fusion = (f32[4,3,64,2,128]{4,2,3,1,0:T(8,128)}, f32[4,3,2,64,128]{4,3,2,1,0:T(8,128)S(1)}) fusion(f32[4,3,2,64,128]{4,3,2,1,0:T(8,128)S(1)} %copy-done.3, f32[4,3,64,2,128]{4,3,2,1,0:T(2,128)} %param.9, f32[3,2,64,128]{3,2,1,0:T(8,128)S(1)} %copy-done.10, f32[4,3,2,64,128]{4,3,2,1,0:T(8,128)} %shard_map.97, ...), kind=kLoop, calls=%fused_computation.14 | loop fusion | flops 1572864 | bytes 5701640 | tf_op jit(solution)/shard_map/transpose | solution.py:357
  105.3 12.8 %all-gather.2 = f32[16,4,3,2,128]{4,1,3,2,0:T(4,128)S(1)} all-gather(f32[2,4,3,2,128]{4,1,3,2,0:T(4,128)S(1)} %copy.93), channel_id=4, replica_groups=mesh['col'=16,'grp'=8] {'grp'}, dimensions={0}, use_global_device_ids=true | all-gather | bytes 221184 | tf_op jit(solution)/shard_map/all_gather | solution.py:294
  118.8 1.3 gather_fusion.8
  120.2 1.0 bitcast_select_fusion.3
  122.2 3.7 %all-to-all-start.2 = ((f32[16,2,4,3,2,128]{5,2,4,3,1,0:T(4,128)}), f32[16,2,4,3,2,128]{5,2,4,3,1,0:T(4,128)S(1)}, u32[]{:S(2)}, u32[]{:S(2)}) async-start(f32[16,2,4,3,2,128]{5,2,4,3,1,0:T(4,128)} %copy.94), calls=%async_computation.2 | async-start | bytes 786432 | tf_op jit(solution)/shard_map/all_to_all | solution.py:306
  125.9 1.5 %copy.97 = f32[4,3,64,2,128]{4,3,2,1,0:T(2,128)} copy(f32[4,3,64,2,128]{4,2,3,1,0:T(8,128)S(1)} %copy-done.9) | data formatting | bytes 1572864
  127.4 8.9 %all-to-all-done.2 = f32[16,2,4,3,2,128]{5,2,4,3,1,0:T(4,128)S(1)} async-done(((f32[16,2,4,3,2,128]{5,2,4,3,1,0:T(4,128)}), f32[16,2,4,3,2,128]{5,2,4,3,1,0:T(4,128)S(1)}, u32[]{:S(2)}, u32[]{:S(2)}) %all-to-all-start.2) | async-done | bytes 393248 | tf_op jit(solution)/shard_map/all_to_all | solution.py:306
  137.6 7.4 %shard_map.98 = f32[4,3,2,64,128]{4,3,2,1,0:T(8,128)} custom-call(f32[4,3,2,64,128]{4,3,2,1,0:T(8,128)} %copy-done.6, f32[4,3,2,8,128]{4,3,2,1,0:T(8,128)} %broadcast_in_dim.211.below_ref, f32[4,3,2,8,128]{4,3,2,1,0:T(8,128)} %broadcast_in_dim.212.above_ref, f32[26,2,64,128]{3,2,1,0:T(8,128)} %get-tuple-element.5.edge_ref, f32[2,64,128]{2,1,0:T(8,128)} %get-tuple-element.6.cm_ref), custom_call_target="tpu_custom_call" | custom-call | flops 102236160 | bytes 3407872 | tf_op jit(solution)/shard_map/pallas_call | solution.py:262
  145.0 1.4 subtract_bitcast_fusion
  146.4 1.5 %copy.98 = f32[4,3,64,2,128]{4,3,2,1,0:T(2,128)} copy(f32[4,3,64,2,128]{4,2,3,1,0:T(8,128)S(1)} %subtract_bitcast_fusion) | data formatting | bytes 1572864
  (93 shorter events, 17.4 us)
Async XLA Ops:
  0.6 1.8 %copy-start = (s32[2,128]{1,0:T(2,128)S(1)}, s32[2,128]{1,0:T(2,128)}, u32[]{:S(2)}) copy-start(s32[2,128]{1,0:T(2,128)} %param.13) | copy-start | bytes 3076
  0.6 6.2 %copy-start.13 = (f32[8]{0:T(128)S(1)}, f32[8]{0:T(128)}, u32[]{:S(2)}) copy-start(f32[8]{0:T(128)} %param.11) | copy-start | bytes 100
  0.7 6.9 %copy-start.12 = (s32[64,2,128]{2,1,0:T(2,128)S(1)}, s32[64,2,128]{2,1,0:T(2,128)}, u32[]{:S(2)}) copy-start(s32[64,2,128]{2,1,0:T(2,128)} %param.10) | copy-start | bytes 196612
  0.7 12.0 %copy-start.8 = (f32[4,3,64,2,128]{4,3,2,1,0:T(2,128)S(1)}, f32[4,3,64,2,128]{4,3,2,1,0:T(2,128)}, u32[]{:S(2)}) copy-start(f32[4,3,64,2,128]{4,3,2,1,0:T(2,128)} %param.9) | copy-start | bytes 2359300
  6.9 70.5 %copy-start.14 = (pred[16]{0:T(512)(128)(4,1)}, pred[16]{0:T(512)(128)(4,1)S(1)}, u32[]{:S(2)}) copy-start(pred[16]{0:T(512)(128)(4,1)S(1)} %get-tuple-element.47) | copy-start | bytes 52
  12.6 14.6 %copy-start.11 = (f32[2,64,128]{2,1,0:T(8,128)}, f32[2,64,128]{2,1,0:T(8,128)S(1)}, u32[]{:S(2)}) copy-start(f32[2,64,128]{2,1,0:T(8,128)S(1)} %add_bitcast_fusion.1.mod_ref) | copy-start | bytes 196612
  12.8 15.3 %copy-start.7 = (f32[4,3,64,2,128]{4,2,3,1,0:T(8,128)}, f32[4,3,64,2,128]{4,2,3,1,0:T(8,128)S(1)}, u32[]{:S(2)}) copy-start(f32[4,3,64,2,128]{4,2,3,1,0:T(8,128)S(1)} %copy.115) | copy-start | bytes 2359300
  29.4 18.5 %all-to-all-start = ((f32[16,2,3328]{2,1,0:T(2,128)}), f32[16,2,3328]{2,1,0:T(2,128)S(1)}, u32[]{:S(2)}, u32[]{:S(2)}) async-start(f32[16,2,3328]{2,1,0:T(2,128)} %copy.86), calls=%async_computation | async-start | bytes 851968 | tf_op jit(solution)/shard_map/all_to_all | solution.py:306
  54.5 7.4 %copy-start.5 = (f32[4,3,64,2,128]{4,3,2,1,0:T(2,128)S(1)}, f32[4,3,64,2,128]{4,3,2,1,0:T(2,128)}, u32[]{:S(2)}) copy-start(f32[4,3,64,2,128]{4,3,2,1,0:T(2,128)} %param.8) | copy-start | bytes 2359300
  63.1 15.3 %copy-start.2 = (f32[4,3,2,64,128]{4,3,2,1,0:T(8,128)}, f32[4,3,2,64,128]{4,3,2,1,0:T(8,128)S(1)}, u32[]{:S(2)}) copy-start(f32[4,3,2,64,128]{4,3,2,1,0:T(8,128)S(1)} %broadcast_divide_fusion.field_ref) | copy-start | bytes 2359300
  78.5 15.3 %all-to-all-start.1 = ((f32[16,2,4,3,2,128]{5,2,4,3,1,0:T(4,128)}), f32[16,2,4,3,2,128]{5,2,4,3,1,0:T(4,128)S(1)}, u32[]{:S(2)}, u32[]{:S(2)}) async-start(f32[16,2,4,3,2,128]{5,2,4,3,1,0:T(4,128)} %copy.89), calls=%async_computation.1 | async-start | bytes 786432 | tf_op jit(solution)/shard_map/all_to_all | solution.py:306
  95.2 7.4 %copy-start.1 = (f32[4,3,2,64,128]{4,3,2,1,0:T(8,128)S(1)}, f32[4,3,2,64,128]{4,3,2,1,0:T(8,128)}, u32[]{:S(2)}) copy-start(f32[4,3,2,64,128]{4,3,2,1,0:T(8,128)} %shard_map.96) | copy-start | bytes 2359300
  95.2 7.4 %copy-start.3 = (f32[4,3,2,64,128]{4,3,2,1,0:T(8,128)S(1)}, f32[4,3,2,64,128]{4,3,2,1,0:T(8,128)}, u32[]{:S(2)}) copy-start(f32[4,3,2,64,128]{4,3,2,1,0:T(8,128)} %copy-done.2) | copy-start | bytes 2359300
  95.2 7.4 %copy-start.10 = (f32[3,2,64,128]{3,2,1,0:T(8,128)S(1)}, f32[3,2,64,128]{3,2,1,0:T(8,128)}, u32[]{:S(2)}) copy-start(f32[3,2,64,128]{3,2,1,0:T(8,128)} %get-tuple-element.7) | copy-start | bytes 589828
  105.3 16.9 %copy-start.6 = (f32[4,3,2,64,128]{4,3,2,1,0:T(8,128)}, f32[4,3,2,64,128]{4,3,2,1,0:T(8,128)S(1)}, u32[]{:S(2)}) copy-start(f32[4,3,2,64,128]{4,3,2,1,0:T(8,128)S(1)} %get-tuple-element.19.field_ref) | copy-start | bytes 2359300
  118.8 7.1 %copy-start.9 = (f32[4,3,64,2,128]{4,2,3,1,0:T(8,128)S(1)}, f32[4,3,64,2,128]{4,2,3,1,0:T(8,128)}, u32[]{:S(2)}) copy-start(f32[4,3,64,2,128]{4,2,3,1,0:T(8,128)} %get-tuple-element.18) | copy-start | bytes 2359300
  122.2 14.1 %all-to-all-start.2 = ((f32[16,2,4,3,2,128]{5,2,4,3,1,0:T(4,128)}), f32[16,2,4,3,2,128]{5,2,4,3,1,0:T(4,128)S(1)}, u32[]{:S(2)}, u32[]{:S(2)}) async-start(f32[16,2,4,3,2,128]{5,2,4,3,1,0:T(4,128)} %copy.94), calls=%async_computation.2 | async-start | bytes 786432 | tf_op jit(solution)/shard_map/all_to_all | solution.py:306
  137.6 7.4 %copy-start.4 = (f32[4,3,2,64,128]{4,3,2,1,0:T(8,128)S(1)}, f32[4,3,2,64,128]{4,3,2,1,0:T(8,128)}, u32[]{:S(2)}) copy-start(f32[4,3,2,64,128]{4,3,2,1,0:T(8,128)} %shard_map.97) | copy-start | bytes 2359300

commit v2 on v1

--- a/solution.py
+++ b/solution.py
@@ -321,42 +321,79 @@
     modulus = jnp.transpose(lookup_modulus(material, moduli), (1, 0, 2))
     plane = (samples, 3, rows_y, width)
     plane_size = samples * 3 * rows_y * width
-
-    first = jnp.concatenate([modal_disp[:, :, :, 0].reshape(-1), modulus[:, 0].reshape(-1)])
-    last = jnp.concatenate([modal_disp[:, :, :, depth - 1].reshape(-1), modulus[:, depth - 1].reshape(-1)])
+    mod_size = rows_y * width
+
+    def pack(md_rows, load_rows):
+        parts = [modal_disp[:, :, :, r].reshape(-1) for r in md_rows]
+        parts += [loads[:, :, :, r].reshape(-1) for r in load_rows]
+        parts += [modulus[:, r].reshape(-1) for r in md_rows]
+        return jnp.concatenate(parts)
+
+    first = pack((0, 1, 2), (0, 1))
+    last = pack((depth - 3, depth - 2, depth - 1), (depth - 2, depth - 1))
     below, above = exchange(first, last, up_dev, low_dev)
-    edges, centre_mod, jacobi = edges_and_diagonal(
-        modulus,
-        below[plane_size:].reshape(rows_y, width),
-        above[plane_size:].reshape(rows_y, width),
-    )
+
+    def planes_of(got, count, start, size, shape):
+        return [got[start + i * size : start + (i + 1) * size].reshape(shape) for i in range(count)]
+
+    md_below = planes_of(below, 3, 0, plane_size, plane)
+    md_above = planes_of(above, 3, 0, plane_size, plane)
+    ld_below = planes_of(below, 2, 3 * plane_size, plane_size, plane)
+    ld_above = planes_of(above, 2, 3 * plane_size, plane_size, plane)
+    mod_below = planes_of(below, 3, 5 * plane_size, mod_size, (rows_y, width))
+    mod_above = planes_of(above, 3, 5 * plane_size, mod_size, (rows_y, width))
+
+    def extend(own, lower, upper, axis):
+        zero = jnp.zeros_like(lower[0])
+        rows = [zero] * (8 - len(lower)) + list(lower)
+        tail = list(upper) + [zero] * (8 - len(upper))
+        return jnp.concatenate(
+            [jnp.stack(rows, axis=axis), own, jnp.stack(tail, axis=axis)], axis=axis
+        )
+
+    md_ext = extend(modal_disp, md_below, md_above, 3)
+    loads_ext = extend(loads, ld_below, ld_above, 3)
+    mod_ext = extend(modulus, mod_below, mod_above, 1)
+    low_on = low_dev[col_grp_index()] != col_grp_index()
+    up_on = up_dev[col_grp_index()] != col_grp_index()
+    zero_mod = jnp.zeros((rows_y, width), jnp.float32)
+    edges, centre_mod, jacobi = edges_and_diagonal(mod_ext, zero_mod, zero_mod)
+
+    row = lax.broadcasted_iota(jnp.int32, (depth + 16,), 0) - 8
+
+    def valid(reach):
+        keep = (row >= 0) & (row < depth)
+        keep = keep | (low_on & (row >= -reach) & (row < 0))
+        keep = keep | (up_on & (row >= depth) & (row < depth + reach))
+        return keep.reshape(depth + 16, 1)
+
+    zero_plane = jnp.zeros(plane, jnp.float32)
 
     def apply(field):
-        below, above = exchange(field[:, :, :, 0], field[:, :, :, depth - 1], up_dev, low_dev)
-        return stiffness(field, below, above, edges, centre_mod)
+        return stiffness(field, zero_plane, zero_plane, edges, centre_mod)
 
     theta = (high_bound[0] + low_bound[0]) / 2.0
     half = (high_bound[0] - low_bound[0]) / 2.0
     sigma = theta / half
     rho0 = 1.0 / sigma
     rho1 = 1.0 / (2.0 * sigma - rho0)
-    first_k = stiffness(
-        modal_disp,
-        below[:plane_size].reshape(plane),
-        above[:plane_size].reshape(plane),
-        edges,
-        centre_mod,
+    start = loads_ext - apply(md_ext)
+    step0 = jnp.where(valid(2), start / (theta * jacobi), jnp.float32(0.0))
+    residual1 = start - apply(step0)
+    step1 = jnp.where(
+        valid(1), rho1 * rho0 * step0 + 2.0 * rho1 / half * residual1 / jacobi, jnp.float32(0.0)
     )
-    start = loads - first_k
-    step0 = start / (theta * jacobi)
-    residual1 = start - apply(step0)
-    step1 = rho1 * rho0 * step0 + 2.0 * rho1 / half * residual1 / jacobi
-    displacement = modal_disp + step0 + step1
-    residual = residual1 - apply(step1)
+    inner = slice(8, 8 + depth)
+    displacement = modal_disp + step0[:, :, :, inner] + step1[:, :, :, inner]
+    residual = residual1[:, :, :, inner] - apply(step1)[:, :, :, inner]
     return (
         jnp.transpose(displacement, (0, 1, 3, 2, 4)),
         jnp.transpose(residual, (0, 1, 3, 2, 4)),
     )
+
+
+def col_grp_index():
+    return lax.axis_index("col") * GROUP + lax.axis_index("grp")
 
 
 def solution(mesh):

time: 149 us -> 122 us (0.82)
  blocking collectives: 39 us -> 14.3 us
  starting transfers between devices: 16.6 us -> 8.02 us
  Pallas kernels: 25.1 us -> 30 us
  local copies, waits for them, and re-layouts: 23.2 us -> 26 us
    all_gather x3 -> x1, blocking collectives: 39 us -> 14.3 us  [exchange(): held = lax.all_gather(pack, 'grp', axis=0, tiled=True)]
    all_to_all x3 -> x1, starting transfers between devices: 16.6 us -> 8.02 us  [exchange(): got = lax.all_to_all(slots, 'col', 0, 0, tiled=True)]
    concatenate x0 -> x5, local copies, waits for them, and re-layouts: none -> 5.24 us  [the longest x3 5.23 us: extend(): jnp.concatenate([jnp.stack(rows, axis=axis), own, jnp.stack(tail, axis=ax...]
    broadcast_in_dim x8 -> x0, local copies, waits for them, and re-layouts: 5.05 us -> none  [the longest x3 1.94 us: stiffness(): halo_below = jnp.broadcast_to(below[:, :, :, None], halo_shape)]
    pallas_call x3, Pallas kernels: 22.1 us -> 26.6 us  [stiffness(): pl.pallas_call(stencil_kernel, out_shape=jax.ShapeDtypeStruct(field.shape...]
    select_n x0 -> x2, other arithmetic: none -> 3.67 us  [the longest x1 2.45 us: on_device(): jnp.where(valid(1), rho1 * rho0 * step0 + 2.0 * rho1 / half * residual1 /...]
    unnamed x33 -> x46, local copies, waits for them, and re-layouts: 3.13 us -> 5.01 us
    all_to_all x3 -> x1, waiting for transfers between devices: 21.3 us -> 21.4 us  [exchange(): got = lax.all_to_all(slots, 'col', 0, 0, tiled=True)]
  transfers between devices with their start and end apart: 3 -> 1, of which waited for: 3 -> 1; matrix products, arithmetic and copies ran while one was open for 2% -> 1% of each run, Pallas kernels for 0% -> 0%
where the time goes in v2:
time: 122 us; the launch traced here: 121 us
  Pallas kernels  30 us (25%)
  local copies, waits for them, and re-layouts  26 us (21%)
  waiting for transfers between devices  21.4 us (18%)
  blocking collectives  14.3 us (12%)
  other arithmetic  12.7 us (10%)
  between operations  8.95 us (7%)
  starting transfers between devices  8.02 us (7%)
    pallas_call x3, Pallas kernels, stiffness(): pl.pallas_call(stencil_kernel, out_shape=jax.ShapeDtypeStruct(field.shape...  26.6 us
    all_to_all x1, waiting for transfers between devices, exchange(): got = lax.all_to_all(slots, 'col', 0, 0, tiled=True)  21.4 us
    all_gather x1, blocking collectives, exchange(): held = lax.all_gather(pack, 'grp', axis=0, tiled=True)  14.3 us
    all_to_all x1, starting transfers between devices, exchange(): got = lax.all_to_all(slots, 'col', 0, 0, tiled=True)  8.02 us
    concatenate x3, local copies, waits for them, and re-layouts, extend(): jnp.concatenate([jnp.stack(rows, axis=axis), own, jnp.stack(tail, axis=ax...  5.23 us
    transpose x1, other arithmetic, on_device(): modulus = jnp.transpose(lookup_modulus(material, moduli), (1, 0, 2))  5.01 us
    unnamed x46, local copies, waits for them, and re-layouts  5.01 us
    pallas_call x1, Pallas kernels, edges_and_diagonal(): pl.pallas_call(edges_kernel, out_shape=(jax.ShapeDtypeStruct((len(OFFSETS...  3.48 us
  transfers between devices with their start and end apart: 1, of which 1 were waited for; matrix products, arithmetic and copies ran while one was open for 1% of the time, Pallas kernels for 0%

profile of v2, /device:TPU:0, one launch (start us, length us, event | category | flops | bytes accessed | tf_op | source)
XLA Modules:
  0.0 121.4 jit_solution(3985381581331187261)
XLA Ops:
  1.5 1.0 scatter_custom_fusion
  2.5 1.5 %gather_fusion.1 = s32[128]{0:T(128)S(1)} fusion(s32[2,128]{1,0:T(2,128)S(1)} %copy-done, s32[128]{0:T(128)S(1)} %get-tuple-element.18), kind=kCustom, calls=%fused_computation.1 | custom fusion | bytes 2048 | tf_op jit(solution)/shard_map/gather | solution.py:283
  4.0 1.5 %gather_fusion = s32[128]{0:T(128)S(1)} fusion(s32[2,128]{1,0:T(2,128)S(1)} %copy-done, s32[128]{0:T(128)S(1)} %fusion.18), kind=kCustom, calls=%fused_computation | custom fusion | bytes 2048 | tf_op jit(solution)/shard_map/gather | solution.py:284
  7.6 5.0 %add_bitcast_fusion = f32[2,64,128]{2,1,0:T(8,128)S(1)} fusion(s32[64,2,128]{2,1,0:T(2,128)S(1)} %copy-done.12, f32[]{:T(128)} %bitcast.21, f32[]{:T(128)} %bitcast.20, f32[]{:T(128)} %bitcast.19, f32[]{:T(128)} %bitcast.18, f32[]{:T(128)} %bitcast.17, f32[]{:T(128)} %bitcast.16, f32[]{:T(128)} %bitcast.15, f32[]{:T(128)} %bitcast.14), kind=kLoop, calls=%fused_computation.23 | loop fusion | flops 376832 | bytes 131104 | tf_op jit(solution)/shard_map/transpose | solution.py:321
  12.8 0.9 copy-done.6
  14.3 14.3 %all-gather.1 = f32[8,2,16128]{2,1,0:T(2,128)S(1)} all-gather(f32[1,2,16128]{2,1,0:T(2,128)S(1)} %maximum_bitcast_fusion), channel_id=2, replica_groups=mesh['col'=16,'grp'=8] {'grp'}, dimensions={0}, use_global_device_ids=true | all-gather | bytes 1161216 | tf_op jit(solution)/shard_map/all_gather | solution.py:294
  28.6 2.1 %gather_fusion.3 = f32[16,16128]{1,0:T(8,128)S(1)} fusion(f32[8,2,16128]{2,1,0:T(2,128)S(1)} %all-gather.1, s32[16]{0:T(128)S(1)} %get-tuple-element.64), kind=kCustom, calls=%fused_computation.3 | custom fusion | bytes 2064512 | tf_op jit(solution)/shard_map/gather | solution.py:300
  30.7 2.1 %gather_fusion.5 = f32[16,16128]{1,0:T(8,128)S(1)} fusion(f32[8,2,16128]{2,1,0:T(2,128)S(1)} %all-gather.1, s32[16]{0:T(128)S(1)} %get-tuple-element.65), kind=kCustom, calls=%fused_computation.5 | custom fusion | bytes 2064512 | tf_op jit(solution)/shard_map/gather | solution.py:301
  33.2 2.9 %copy.44 = f32[16,2,16128]{2,1,0:T(2,128)} copy(f32[16,2,16128]{2,0,1:T(8,128)S(1)} %pad_maximum_fusion) | data formatting | bytes 4128768 | tf_op jit(solution)/shard_map/stack | solution.py:305
  36.1 8.0 %all-to-all-start = ((f32[16,2,16128]{2,1,0:T(2,128)}), f32[16,2,16128]{2,1,0:T(2,128)S(1)}, u32[]{:S(2)}, u32[]{:S(2)}) async-start(f32[16,2,16128]{2,1,0:T(2,128)} %copy.44), calls=%async_computation | async-start | bytes 4128768 | tf_op jit(solution)/shard_map/all_to_all | solution.py:306
  53.2 21.4 %all-to-all-done = f32[16,2,16128]{2,1,0:T(2,128)S(1)} async-done(((f32[16,2,16128]{2,1,0:T(2,128)}), f32[16,2,16128]{2,1,0:T(2,128)S(1)}, u32[]{:S(2)}, u32[]{:S(2)}) %all-to-all-start) | async-done | bytes 2064416 | tf_op jit(solution)/shard_map/all_to_all | solution.py:306
  74.8 1.9 %concatenate.35.mod_ref = f32[2,80,128]{2,1,0:T(8,128)} concatenate(f32[2,1,128]{2,1,0:T(1,128)S(1)} %broadcast.426, f32[2,4,128]{2,1,0:T(4,128)S(1)} %broadcast.427, f32[2,1,128]{2,1,0:T(1,128)S(1)} %get-tuple-element.53, f32[2,1,128]{2,1,0:T(1,128)S(1)} %get-tuple-element.52, f32[2,1,128]{2,1,0:T(1,128)S(1)} %get-tuple-element.51, f32[2,64,128]{2,1,0:T(8,128)S(1)} %add_bitcast_fusion, ...), dimensions={1} | concatenate | bytes 163840 | tf_op jit(solution)/shard_map/concatenate | solution.py:350
  77.2 3.5 %shard_map.95 = (f32[26,2,80,128]{3,2,1,0:T(8,128)}, f32[2,80,128]{2,1,0:T(8,128)}, f32[3,2,80,128]{3,2,1,0:T(8,128)}) custom-call(f32[2,80,128]{2,1,0:T(8,128)} %concatenate.35.mod_ref, f32[2,8,128]{2,1,0:T(8,128)} %broadcast_28_below_ref_above_ref.2.below_ref.above_ref, f32[2,8,128]{2,1,0:T(8,128)} %broadcast_28_below_ref_above_ref.2.below_ref.above_ref), custom_call_target="tpu_custom_call" | custom-call | tf_op jit(solution)/shard_map/pallas_call | solution.py:129
  80.7 1.0 broadcast_multiply_fusion
  81.7 3.0 %concatenate.34.field_ref = f32[4,3,2,80,128]{4,3,2,1,0:T(8,128)} concatenate(f32[4,3,2,1,128]{4,3,2,1,0:T(1,128)S(1)} %broadcast.425, f32[4,3,2,4,128]{4,3,2,1,0:T(4,128)S(1)} %broadcast.419, f32[4,3,2,1,128]{4,3,2,1,0:T(1,128)S(1)} %bitcast.108, f32[4,3,2,1,128]{4,3,2,1,0:T(1,128)S(1)} %bitcast.107, f32[4,3,2,1,128]{4,3,2,1,0:T(1,128)S(1)} %bitcast.106, ...), dimensions={3} | concatenate | bytes 1966080 | tf_op jit(solution)/shard_map/concatenate | solution.py:350
  85.4 8.8 %shard_map.96 = f32[4,3,2,80,128]{4,3,2,1,0:T(8,128)} custom-call(f32[4,3,2,80,128]{4,3,2,1,0:T(8,128)} %concatenate.34.field_ref, f32[4,3,2,8,128]{4,3,2,1,0:T(8,128)} %broadcast_27_below_ref_above_ref.2.below_ref.above_ref, f32[4,3,2,8,128]{4,3,2,1,0:T(8,128)} %broadcast_27_below_ref_above_ref.2.below_ref.above_ref, ...), custom_call_target="tpu_custom_call" | custom-call | flops 127795200 | bytes 4259840 | tf_op jit(solution)/shard_map/pallas_call | solution.py:262
  94.6 0.8 copy-done.3
  95.4 1.2 %divide_select_fusion = (f32[4,3,2,80,128]{4,3,2,1,0:T(8,128)}, f32[4,3,2,80,128]{4,3,2,1,0:T(8,128)S(1)}) fusion(f32[3,2,80,128]{3,2,1,0:T(8,128)S(1)} %broadcast_multiply_fusion, pred[80]{0:T(512)(128)(4,1)S(1)} %get-tuple-element.63, f32[4,3,2,80,128]{4,3,2,1,0:T(8,128)S(1)} %concatenate.33, f32[4,3,2,80,128]{4,3,2,1,0:T(8,128)S(1)} %copy-done.3), kind=kLoop, calls=%fused_computation.11 | loop fusion | flops 737280 | bytes 4178000 | tf_op jit(solution)/shard_map/jit(_where)/select_n | solution.py:381
  96.6 8.9 %shard_map.97 = f32[4,3,2,80,128]{4,3,2,1,0:T(8,128)} custom-call(f32[4,3,2,80,128]{4,3,2,1,0:T(8,128)} %get-tuple-element.16.field_ref, f32[4,3,2,8,128]{4,3,2,1,0:T(8,128)} %broadcast_27_below_ref_above_ref.2.below_ref.above_ref, f32[4,3,2,8,128]{4,3,2,1,0:T(8,128)} %broadcast_27_below_ref_above_ref.2.below_ref.above_ref, ...), custom_call_target="tpu_custom_call" | custom-call | flops 127795200 | bytes 4259840 | tf_op jit(solution)/shard_map/pallas_call | solution.py:262
  105.5 2.5 %add_select_fusion = (f32[4,3,2,80,128]{4,3,2,1,0:T(8,128)}, f32[4,3,2,80,128]{4,3,2,1,0:T(8,128)S(1)}) fusion(f32[4,3,2,80,128]{4,3,2,1,0:T(8,128)S(1)} %copy-done.1, f32[3,2,80,128]{3,2,1,0:T(8,128)S(1)} %copy-done.10, f32[]{:T(128)S(6)} %div.95, f32[]{:T(128)S(6)} %mul.49, pred[80]{0:T(512)(128)(4,1)S(1)} %get-tuple-element.62, ...), kind=kLoop, calls=%fused_computation.10 | loop fusion | flops 1474560 | bytes 5161048 | tf_op jit(solution)/shard_map/jit(_where)/select_n | solution.py:383
  108.0 8.9 %shard_map.98 = f32[4,3,2,80,128]{4,3,2,1,0:T(8,128)} custom-call(f32[4,3,2,80,128]{4,3,2,1,0:T(8,128)} %get-tuple-element.14.field_ref, f32[4,3,2,8,128]{4,3,2,1,0:T(8,128)} %broadcast_27_below_ref_above_ref.2.below_ref.above_ref, f32[4,3,2,8,128]{4,3,2,1,0:T(8,128)} %broadcast_27_below_ref_above_ref.2.below_ref.above_ref, ...), custom_call_target="tpu_custom_call" | custom-call | flops 127795200 | bytes 4259840 | tf_op jit(solution)/shard_map/pallas_call | solution.py:262
  116.8 1.4 %fusion.1 = f32[4,3,64,2,128]{4,2,3,1,0:T(8,128)S(1)} fusion(f32[4,3,2,80,128]{4,3,2,1,0:T(8,128)S(1)} %copy-done.2, f32[4,3,2,80,128]{4,3,2,1,0:T(8,128)S(1)} %copy-done.1, f32[4,3,64,2,128]{4,3,2,1,0:T(2,128)} %param.9), kind=kLoop, calls=%fused_computation.15 | loop fusion | flops 393216 | bytes 3145728 | tf_op jit(solution)/shard_map/transpose | solution.py:390
  118.4 1.5 %copy.46 = f32[4,3,64,2,128]{4,3,2,1,0:T(2,128)} copy(f32[4,3,64,2,128]{4,2,3,1,0:T(8,128)S(1)} %fusion) | data formatting | bytes 1572864
  119.9 1.5 %copy.45 = f32[4,3,64,2,128]{4,3,2,1,0:T(2,128)} copy(f32[4,3,64,2,128]{4,2,3,1,0:T(8,128)S(1)} %fusion.1) | data formatting | bytes 1572864
  (81 shorter events, 7.1 us)
Async XLA Ops:
  0.6 1.9 %copy-start = (s32[2,128]{1,0:T(2,128)S(1)}, s32[2,128]{1,0:T(2,128)}, u32[]{:S(2)}) copy-start(s32[2,128]{1,0:T(2,128)} %param.13) | copy-start | bytes 3076
  0.6 6.3 %copy-start.13 = (f32[8]{0:T(128)S(1)}, f32[8]{0:T(128)}, u32[]{:S(2)}) copy-start(f32[8]{0:T(128)} %param.11) | copy-start | bytes 100
  0.7 7.0 %copy-start.12 = (s32[64,2,128]{2,1,0:T(2,128)S(1)}, s32[64,2,128]{2,1,0:T(2,128)}, u32[]{:S(2)}) copy-start(s32[64,2,128]{2,1,0:T(2,128)} %param.10) | copy-start | bytes 196612
  0.7 12.0 %copy-start.11 = (f32[4,3,64,2,128]{4,3,2,1,0:T(2,128)S(1)}, f32[4,3,64,2,128]{4,3,2,1,0:T(2,128)}, u32[]{:S(2)}) copy-start(f32[4,3,64,2,128]{4,3,2,1,0:T(2,128)} %param.8) | copy-start | bytes 2359300
  0.7 13.0 %copy-start.9 = (f32[4,3,64,2,128]{4,3,2,1,0:T(2,128)S(1)}, f32[4,3,64,2,128]{4,3,2,1,0:T(2,128)}, u32[]{:S(2)}) copy-start(f32[4,3,64,2,128]{4,3,2,1,0:T(2,128)} %param.9) | copy-start | bytes 2359300
  12.8 0.9 copy-start.6
  13.8 14.8 %copy-start.4 = (f32[4,3,64,2,128]{4,2,3,1,0:T(8,128)}, f32[4,3,64,2,128]{4,2,3,1,0:T(8,128)S(1)}, u32[]{:S(2)}) copy-start(f32[4,3,64,2,128]{4,2,3,1,0:T(8,128)S(1)} %copy.53) | copy-start | bytes 2359300
  36.1 45.6 %copy-start.5 = (f32[4,3,64,2,128]{4,2,3,1,0:T(8,128)S(1)}, f32[4,3,64,2,128]{4,2,3,1,0:T(8,128)}, u32[]{:S(2)}) copy-start(f32[4,3,64,2,128]{4,2,3,1,0:T(8,128)} %copy-done.4) | copy-start | bytes 2359300
  36.1 38.5 %all-to-all-start = ((f32[16,2,16128]{2,1,0:T(2,128)}), f32[16,2,16128]{2,1,0:T(2,128)S(1)}, u32[]{:S(2)}, u32[]{:S(2)}) async-start(f32[16,2,16128]{2,1,0:T(2,128)} %copy.44), calls=%async_computation | async-start | bytes 4128768 | tf_op jit(solution)/shard_map/all_to_all | solution.py:306
  85.4 8.9 %copy-start.7 = (f32[4,3,64,2,128]{4,2,3,1,0:T(8,128)S(1)}, f32[4,3,64,2,128]{4,2,3,1,0:T(8,128)}, u32[]{:S(2)}) copy-start(f32[4,3,64,2,128]{4,2,3,1,0:T(8,128)} %copy-done.6) | copy-start | bytes 2359300
  94.2 1.2 copy-start.3
  96.6 8.9 %copy-start.1 = (f32[4,3,2,80,128]{4,3,2,1,0:T(8,128)S(1)}, f32[4,3,2,80,128]{4,3,2,1,0:T(8,128)}, u32[]{:S(2)}) copy-start(f32[4,3,2,80,128]{4,3,2,1,0:T(8,128)} %get-tuple-element.16.field_ref) | copy-start | bytes 2949124
  96.6 8.9 %copy-start.10 = (f32[3,2,80,128]{3,2,1,0:T(8,128)S(1)}, f32[3,2,80,128]{3,2,1,0:T(8,128)}, u32[]{:S(2)}) copy-start(f32[3,2,80,128]{3,2,1,0:T(8,128)} %get-tuple-element.7) | copy-start | bytes 737284
  108.0 8.9 %copy-start.2 = (f32[4,3,2,80,128]{4,3,2,1,0:T(8,128)S(1)}, f32[4,3,2,80,128]{4,3,2,1,0:T(8,128)}, u32[]{:S(2)}) copy-start(f32[4,3,2,80,128]{4,3,2,1,0:T(8,128)} %get-tuple-element.14.field_ref) | copy-start | bytes 2949124
  116.8 1.4 %copy-start.8 = (f32[4,3,2,80,128]{4,3,2,1,0:T(8,128)S(1)}, f32[4,3,2,80,128]{4,3,2,1,0:T(8,128)}, u32[]{:S(2)}) copy-start(f32[4,3,2,80,128]{4,3,2,1,0:T(8,128)} %shard_map.98) | copy-start | bytes 2949124

commit v3 on v2

--- a/solution.py
+++ b/solution.py
@@ -135,6 +135,9 @@
         ),
         in_specs=[vmem, vmem, vmem],
         out_specs=(vmem, vmem, vmem),
+        cost_estimate=pl.CostEstimate(
+            flops=26 * 8 * modulus.size, bytes_accessed=4 * 31 * modulus.size, transcendentals=0
+        ),
     )(modulus, halo_below, halo_above)
 
 
@@ -351,41 +354,84 @@
             [jnp.stack(rows, axis=axis), own, jnp.stack(tail, axis=axis)], axis=axis
         )
 
-    md_ext = extend(modal_disp, md_below, md_above, 3)
-    loads_ext = extend(loads, ld_below, ld_above, 3)
-    mod_ext = extend(modulus, mod_below, mod_above, 1)
     low_on = low_dev[col_grp_index()] != col_grp_index()
     up_on = up_dev[col_grp_index()] != col_grp_index()
     zero_mod = jnp.zeros((rows_y, width), jnp.float32)
-    edges, centre_mod, jacobi = edges_and_diagonal(mod_ext, zero_mod, zero_mod)
-
-    row = lax.broadcasted_iota(jnp.int32, (depth + 16,), 0) - 8
-
-    def valid(reach):
-        keep = (row >= 0) & (row < depth)
-        keep = keep | (low_on & (row >= -reach) & (row < 0))
-        keep = keep | (up_on & (row >= depth) & (row < depth + reach))
-        return keep.reshape(depth + 16, 1)
-
     zero_plane = jnp.zeros(plane, jnp.float32)
-
-    def apply(field):
-        return stiffness(field, zero_plane, zero_plane, edges, centre_mod)
 
     theta = (high_bound[0] + low_bound[0]) / 2.0
     half = (high_bound[0] - low_bound[0]) / 2.0
     sigma = theta / half
     rho0 = 1.0 / sigma
     rho1 = 1.0 / (2.0 * sigma - rho0)
-    start = loads_ext - apply(md_ext)
-    step0 = jnp.where(valid(2), start / (theta * jacobi), jnp.float32(0.0))
-    residual1 = start - apply(step0)
-    step1 = jnp.where(
-        valid(1), rho1 * rho0 * step0 + 2.0 * rho1 / half * residual1 / jacobi, jnp.float32(0.0)
+
+    def chain(md, ld, mod, valid):
+        edges, centre_mod, jacobi = edges_and_diagonal(mod, zero_mod, zero_mod)
+
+        def apply(field):
+            return stiffness(field, zero_plane, zero_plane, edges, centre_mod)
+
+        start = ld - apply(md)
+        step0 = start / (theta * jacobi)
+        if valid is not None:
+            step0 = jnp.where(valid(2), step0, jnp.float32(0.0))
+        residual1 = start - apply(step0)
+        step1 = rho1 * rho0 * step0 + 2.0 * rho1 / half * residual1 / jacobi
+        if valid is not None:
+            step1 = jnp.where(valid(1), step1, jnp.float32(0.0))
+        displacement = md + step0 + step1
+        residual = residual1 - apply(step1)
+        return displacement, residual
+
+    disp_local, res_local = chain(modal_disp, loads, modulus, None)
+
+    edge_rows = 16
+    head = slice(0, edge_rows)
+    tail = slice(depth - edge_rows, depth)
+
+    def window(own, lower, upper, axis):
+        zero = jnp.zeros_like(lower[0])
+        rows = [zero] * (8 - len(lower)) + list(lower)
+        after = list(upper) + [zero] * (8 - len(upper))
+        index = [slice(None)] * own.ndim
+        index[axis] = head
+        own_head = own[tuple(index)]
+        index[axis] = tail
+        own_tail = own[tuple(index)]
+        return jnp.concatenate(
+            [jnp.stack(rows, axis=axis), own_head, own_tail, jnp.stack(after, axis=axis)], axis=axis
+        )
+
+    md_win = window(modal_disp, md_below, md_above, 3)
+    ld_win = window(loads, ld_below, ld_above, 3)
+    mod_win = window(modulus, mod_below, mod_above, 1)
+    logical = jnp.concatenate(
+        [
+            jnp.arange(-8, edge_rows, dtype=jnp.int32),
+            jnp.arange(depth - edge_rows, depth + 8, dtype=jnp.int32),
+        ]
     )
-    inner = slice(8, 8 + depth)
-    displacement = modal_disp + step0[:, :, :, inner] + step1[:, :, :, inner]
-    residual = residual1[:, :, :, inner] - apply(step1)[:, :, :, inner]
+
+    def valid(reach):
+        keep = (logical >= 0) & (logical < depth)
+        keep = keep | (low_on & (logical >= -reach) & (logical < 0))
+        keep = keep | (up_on & (logical >= depth) & (logical < depth + reach))
+        return keep.reshape(-1, 1)
+
+    disp_win, res_win = chain(md_win, ld_win, mod_win, valid)
+
+    def merge(local, win):
+        return jnp.concatenate(
+            [
+                win[:, :, :, 8:16],
+                local[:, :, :, 8 : depth - 8],
+                win[:, :, :, 8 + 2 * edge_rows - 8 : 8 + 2 * edge_rows],
+            ],
+            axis=3,
+        )
+
+    displacement = merge(disp_local, disp_win)
+    residual = merge(res_local, res_win)
     return (
         jnp.transpose(displacement, (0, 1, 3, 2, 4)),
         jnp.transpose(residual, (0, 1, 3, 2, 4)),

time: 122 us -> 135 us (1.11); the launches traced: 121 us -> 133 us
  waiting for transfers between devices: 21.4 us -> 0.01 us
  Pallas kernels: 30 us -> 45.6 us
  other arithmetic: 12.7 us -> 23.5 us
  local copies, waits for them, and re-layouts: 26 us -> 32.8 us
    all_to_all x1, waiting for transfers between devices: 21.4 us -> 0.01 us  [exchange(): got = lax.all_to_all(slots, 'col', 0, 0, tiled=True)]
    pallas_call x3 -> x6, Pallas kernels: 26.6 us -> 39.9 us  [stiffness(): pl.pallas_call(stencil_kernel, out_shape=jax.ShapeDtypeStruct(field.shape...]
    add x0 -> x3, other arithmetic: none -> 4.58 us  [the longest x1 2.35 us: chain(): step1 = rho1 * rho0 * step0 + 2.0 * rho1 / half * residual1 / jacobi]
    sub x0 -> x2, other arithmetic: none -> 3.6 us  [chain(): residual = residual1 - apply(step1)]
    concatenate x3, local copies, waits for them, and re-layouts: 5.23 us -> 8.76 us  [window(): jnp.concatenate([jnp.stack(rows, axis=axis), own_head, own_tail, jnp.stac...]
    slice x0 -> x5, local copies, waits for them, and re-layouts: none -> 2.48 us  [the longest x3 2.45 us: window(): own_tail = own[tuple(index)]]
    div x0 -> x1, other arithmetic: none -> 2.26 us  [chain(): step0 = start / (theta * jacobi)]
    pallas_call x1 -> x2, Pallas kernels: 3.48 us -> 5.65 us  [edges_and_diagonal(): pl.pallas_call(edges_kernel, out_shape=(jax.ShapeDtypeStruct((len(OFFSETS...]
  transfers between devices with their start and end apart: 1 -> 1, of which waited for: 1 -> 0; matrix products, arithmetic and copies ran while one was open for 1% -> 10% of each run, Pallas kernels for 0% -> 19%
where the time goes in v3:
time: 135 us; the launch traced here: 133 us
  Pallas kernels  45.6 us (34%)
  local copies, waits for them, and re-layouts  32.8 us (24%)
  other arithmetic  23.5 us (17%)
  blocking collectives  14.3 us (11%)
  between operations  8.69 us (6%)
  starting transfers between devices  7.93 us (6%)
    pallas_call x6, Pallas kernels, stiffness(): pl.pallas_call(stencil_kernel, out_shape=jax.ShapeDtypeStruct(field.shape...  39.9 us
    all_gather x1, blocking collectives, exchange(): held = lax.all_gather(pack, 'grp', axis=0, tiled=True)  14.3 us
    concatenate x3, local copies, waits for them, and re-layouts, window(): jnp.concatenate([jnp.stack(rows, axis=axis), own_head, own_tail, jnp.stac...  8.76 us
    all_to_all x1, starting transfers between devices, exchange(): got = lax.all_to_all(slots, 'col', 0, 0, tiled=True)  7.93 us
    pallas_call x2, Pallas kernels, edges_and_diagonal(): pl.pallas_call(edges_kernel, out_shape=(jax.ShapeDtypeStruct((len(OFFSETS...  5.65 us
    transpose x1, other arithmetic, on_device(): modulus = jnp.transpose(lookup_modulus(material, moduli), (1, 0, 2))  5 us
    unnamed x58, local copies, waits for them, and re-layouts  3.99 us
    sub x2, other arithmetic, chain(): residual = residual1 - apply(step1)  3.6 us
  transfers between devices with their start and end apart: 1, of which 0 were waited for; matrix products, arithmetic and copies ran while one was open for 10% of the time, Pallas kernels for 19%

profile of v3, /device:TPU:0, one launch (start us, length us, event | category | flops | bytes accessed | tf_op | source)
XLA Modules:
  0.0 132.7 jit_solution(14230367829425229422)
XLA Ops:
  2.5 1.5 %gather_fusion.1 = s32[128]{0:T(128)S(1)} fusion(s32[2,128]{1,0:T(2,128)S(1)} %copy-done, s32[128]{0:T(128)S(1)} %get-tuple-element.27), kind=kCustom, calls=%fused_computation.1 | custom fusion | bytes 2048 | tf_op jit(solution)/shard_map/gather | solution.py:286
  4.0 1.5 %gather_fusion = s32[128]{0:T(128)S(1)} fusion(s32[2,128]{1,0:T(2,128)S(1)} %copy-done, s32[128]{0:T(128)S(1)} %fusion.16), kind=kCustom, calls=%fused_computation | custom fusion | bytes 2048 | tf_op jit(solution)/shard_map/gather | solution.py:287
  7.6 5.0 %add_bitcast_fusion.mod_ref = f32[2,64,128]{2,1,0:T(8,128)S(1)} fusion(s32[64,2,128]{2,1,0:T(2,128)S(1)} %copy-done.18, f32[]{:T(128)} %bitcast.20, f32[]{:T(128)} %bitcast.19, f32[]{:T(128)} %bitcast.18, f32[]{:T(128)} %bitcast.17, f32[]{:T(128)} %bitcast.16, f32[]{:T(128)} %bitcast.15, f32[]{:T(128)} %bitcast.14, f32[]{:T(128)} %bitcast.13), kind=kLoop, calls=%fused_computation.27 | loop fusion | flops 376832 | bytes 131104 | tf_op jit(solution)/shard_map/transpose | solution.py:324
  14.0 14.3 %all-gather.1 = f32[8,2,16128]{2,1,0:T(2,128)S(1)} all-gather(f32[1,2,16128]{2,1,0:T(2,128)S(1)} %maximum_bitcast_fusion.2), channel_id=2, replica_groups=mesh['col'=16,'grp'=8] {'grp'}, dimensions={0}, use_global_device_ids=true | all-gather | bytes 1161216 | tf_op jit(solution)/shard_map/all_gather | solution.py:297
  28.3 3.0 %gather_fusion.3 = f32[16,16128]{1,0:T(8,128)} fusion(f32[8,2,16128]{2,1,0:T(2,128)S(1)} %all-gather.1, s32[16]{0:T(128)S(1)} %get-tuple-element.83), kind=kCustom, calls=%fused_computation.3 | custom fusion | bytes 2064512 | tf_op jit(solution)/shard_map/gather | solution.py:303
  31.2 3.0 %gather_fusion.5 = f32[16,16128]{1,0:T(8,128)} fusion(f32[8,2,16128]{2,1,0:T(2,128)S(1)} %all-gather.1, s32[16]{0:T(128)S(1)} %get-tuple-element.84), kind=kCustom, calls=%fused_computation.5 | custom fusion | bytes 2064512 | tf_op jit(solution)/shard_map/gather | solution.py:304
  36.0 2.9 %copy.44 = f32[16,2,16128]{2,1,0:T(2,128)} copy(f32[16,2,16128]{2,0,1:T(8,128)S(1)} %pad_maximum_fusion) | data formatting | bytes 4128768 | tf_op jit(solution)/shard_map/stack | solution.py:308
  38.9 7.9 %all-to-all-start = ((f32[16,2,16128]{2,1,0:T(2,128)}), f32[16,2,16128]{2,1,0:T(2,128)}, u32[]{:S(2)}, u32[]{:S(2)}) async-start(f32[16,2,16128]{2,1,0:T(2,128)} %copy.44), calls=%async_computation | async-start | bytes 4128768 | tf_op jit(solution)/shard_map/all_to_all | solution.py:309
  48.8 3.0 %shard_map.98 = (f32[26,2,64,128]{3,2,1,0:T(8,128)}, f32[2,64,128]{2,1,0:T(8,128)}, f32[3,2,64,128]{3,2,1,0:T(8,128)}) custom-call(f32[2,64,128]{2,1,0:T(8,128)} %copy-done.16, f32[2,8,128]{2,1,0:T(8,128)} %broadcast_37_below_ref_above_ref.2.below_ref.above_ref, f32[2,8,128]{2,1,0:T(8,128)} %broadcast_37_below_ref_above_ref.2.below_ref.above_ref), custom_call_target="tpu_custom_call" | custom-call | flops 3407872 | bytes 2031616 | tf_op jit(solution)/shard_map/pallas_call | solution.py:129
  60.8 7.3 %shard_map.99 = f32[4,3,2,64,128]{4,3,2,1,0:T(8,128)} custom-call(f32[4,3,2,64,128]{4,3,2,1,0:T(8,128)} %bitcast.101, f32[4,3,2,8,128]{4,3,2,1,0:T(8,128)} %broadcast_36_below_ref_above_ref.2.below_ref.above_ref, f32[4,3,2,8,128]{4,3,2,1,0:T(8,128)} %broadcast_36_below_ref_above_ref.2.below_ref.above_ref, f32[26,2,64,128]{3,2,1,0:T(8,128)} %get-tuple-element.11.edge_ref, ...), custom_call_target="tpu_custom_call" | custom-call | flops 102236160 | bytes 3407872 | tf_op jit(solution)/shard_map/pallas_call | solution.py:265
  68.1 2.3 %broadcast_divide_fusion.field_ref = f32[4,3,2,64,128]{4,3,2,1,0:T(8,128)} fusion(f32[3,2,64,128]{3,2,1,0:T(8,128)S(1)} %broadcast_multiply_fusion, f32[4,3,2,64,128]{4,3,2,1,0:T(8,128)} %shard_map.99, f32[4,3,64,2,128]{4,3,2,1,0:T(2,128)S(1)} %copy-done.5), kind=kLoop, calls=%fused_computation.21 | loop fusion | flops 393216 | bytes 2555904 | tf_op jit(solution)/shard_map/div | solution.py:375
  70.4 7.4 %shard_map.100 = f32[4,3,2,64,128]{4,3,2,1,0:T(8,128)} custom-call(f32[4,3,2,64,128]{4,3,2,1,0:T(8,128)} %broadcast_divide_fusion.field_ref, f32[4,3,2,8,128]{4,3,2,1,0:T(8,128)} %broadcast_36_below_ref_above_ref.2.below_ref.above_ref, f32[4,3,2,8,128]{4,3,2,1,0:T(8,128)} %broadcast_36_below_ref_above_ref.2.below_ref.above_ref, ...), custom_call_target="tpu_custom_call" | custom-call | flops 102236160 | bytes 3407872 | tf_op jit(solution)/shard_map/pallas_call | solution.py:265
  77.8 2.4 %divide_add_fusion = (f32[4,3,2,64,128]{4,3,2,1,0:T(8,128)}, f32[4,3,2,64,128]{4,3,2,1,0:T(8,128)S(1)}) fusion(f32[4,3,2,64,128]{4,3,2,1,0:T(8,128)S(1)} %copy-done.1, f32[3,2,64,128]{3,2,1,0:T(8,128)S(1)} %copy-done.14, f32[]{:T(128)S(6)} %div.112, f32[]{:T(128)S(6)} %mul.69, f32[4,3,2,64,128]{4,3,2,1,0:T(8,128)} %shard_map.100, ...), kind=kLoop, calls=%fused_computation.14 | loop fusion | flops 1179648 | bytes 4915208 | tf_op jit(solution)/shard_map/add | solution.py:379
  80.2 7.4 %shard_map.102 = f32[4,3,2,64,128]{4,3,2,1,0:T(8,128)} custom-call(f32[4,3,2,64,128]{4,3,2,1,0:T(8,128)} %get-tuple-element.20.field_ref, f32[4,3,2,8,128]{4,3,2,1,0:T(8,128)} %broadcast_36_below_ref_above_ref.2.below_ref.above_ref, f32[4,3,2,8,128]{4,3,2,1,0:T(8,128)} %broadcast_36_below_ref_above_ref.2.below_ref.above_ref, ...), custom_call_target="tpu_custom_call" | custom-call | flops 102236160 | bytes 3407872 | tf_op jit(solution)/shard_map/pallas_call | solution.py:265
  90.2 2.4 %slice_subtract_fusion = (f32[4,3,2,48,128]{4,3,2,1,0:T(8,128)}, f32[4,3,2,48,128]{4,3,2,1,0:T(8,128)}) fusion(f32[4,3,2,64,128]{4,3,2,1,0:T(8,128)} %shard_map.102, f32[4,3,2,64,128]{4,3,2,1,0:T(8,128)S(1)} %get-tuple-element.21, f32[4,3,2,64,128]{4,3,2,1,0:T(8,128)S(1)} %copy-done.6, f32[4,3,2,64,128]{4,3,2,1,0:T(8,128)S(1)} %copy-done.1, ...), kind=kLoop, calls=%fused_computation.15 | loop fusion | flops 442368 | bytes 4128768 | tf_op jit(solution)/shard_map/sub | solution.py:383
  93.8 3.9 %concatenate.45.mod_ref = f32[2,48,128]{2,1,0:T(8,128)} concatenate(f32[2,1,128]{2,1,0:T(1,128)S(1)} %broadcast.432, f32[2,4,128]{2,1,0:T(4,128)S(1)} %broadcast.433, f32[2,1,128]{2,1,0:T(1,128)S(1)} %get-tuple-element.72, f32[2,1,128]{2,1,0:T(1,128)S(1)} %get-tuple-element.71, f32[2,1,128]{2,1,0:T(1,128)S(1)} %get-tuple-element.70, f32[2,16,128]{2,1,0:T(8,128)} %get-tuple-element.50, ...), dimensions={1} | concatenate | bytes 98304 | tf_op jit(solution)/shard_map/concatenate | solution.py:401
  97.7 2.6 %shard_map.95 = (f32[26,2,48,128]{3,2,1,0:T(8,128)}, f32[2,48,128]{2,1,0:T(8,128)}, f32[3,2,48,128]{3,2,1,0:T(8,128)}) custom-call(f32[2,48,128]{2,1,0:T(8,128)} %concatenate.45.mod_ref, f32[2,8,128]{2,1,0:T(8,128)} %broadcast_37_below_ref_above_ref.2.below_ref.above_ref, f32[2,8,128]{2,1,0:T(8,128)} %broadcast_37_below_ref_above_ref.2.below_ref.above_ref), custom_call_target="tpu_custom_call" | custom-call | flops 2555904 | bytes 1523712 | tf_op jit(solution)/shard_map/pallas_call | solution.py:129
  101.2 4.7 %concatenate.42.field_ref = f32[4,3,2,48,128]{4,3,2,1,0:T(8,128)} concatenate(f32[4,3,2,1,128]{4,3,2,1,0:T(1,128)S(1)} %broadcast.418, f32[4,3,2,4,128]{4,3,2,1,0:T(4,128)S(1)} %broadcast.419, f32[4,3,2,1,128]{4,3,2,1,0:T(1,128)S(1)} %bitcast.115, f32[4,3,2,1,128]{4,3,2,1,0:T(1,128)S(1)} %bitcast.114, f32[4,3,2,1,128]{4,3,2,1,0:T(1,128)S(1)} %bitcast.113, ...), dimensions={3} | concatenate | bytes 1179648 | tf_op jit(solution)/shard_map/concatenate | solution.py:401
  105.9 5.9 %shard_map.96 = f32[4,3,2,48,128]{4,3,2,1,0:T(8,128)} custom-call(f32[4,3,2,48,128]{4,3,2,1,0:T(8,128)} %concatenate.42.field_ref, f32[4,3,2,8,128]{4,3,2,1,0:T(8,128)} %broadcast_36_below_ref_above_ref.2.below_ref.above_ref, f32[4,3,2,8,128]{4,3,2,1,0:T(8,128)} %broadcast_36_below_ref_above_ref.2.below_ref.above_ref, ...), custom_call_target="tpu_custom_call" | custom-call | flops 76677120 | bytes 2555904 | tf_op jit(solution)/shard_map/pallas_call | solution.py:265
  112.0 2.2 %divide_select_fusion = (f32[4,3,2,48,128]{4,3,2,1,0:T(8,128)}, f32[4,3,2,48,128]{4,3,2,1,0:T(8,128)S(1)}) fusion(f32[3,2,48,128]{3,2,1,0:T(8,128)S(1)} %broadcast_multiply_fusion.1, pred[48]{0:T(512)(128)(4,1)S(1)} %get-tuple-element.74, f32[4,3,2,48,128]{4,3,2,1,0:T(8,128)S(1)} %concatenate.44, f32[4,3,2,48,128]{4,3,2,1,0:T(8,128)} %shard_map.96), kind=kLoop, calls=%fused_computation.20 | loop fusion | flops 442368 | bytes 2506800 | tf_op jit(solution)/shard_map/jit(_where)/select_n | solution.py:377
  114.2 5.9 %shard_map.97 = f32[4,3,2,48,128]{4,3,2,1,0:T(8,128)} custom-call(f32[4,3,2,48,128]{4,3,2,1,0:T(8,128)} %get-tuple-element.25.field_ref, f32[4,3,2,8,128]{4,3,2,1,0:T(8,128)} %broadcast_36_below_ref_above_ref.2.below_ref.above_ref, f32[4,3,2,8,128]{4,3,2,1,0:T(8,128)} %broadcast_36_below_ref_above_ref.2.below_ref.above_ref, ...), custom_call_target="tpu_custom_call" | custom-call | flops 76677120 | bytes 2555904 | tf_op jit(solution)/shard_map/pallas_call | solution.py:265
  120.2 2.2 %add_add_fusion = (f32[4,3,2,48,128]{4,3,2,1,0:T(8,128)S(1)}, f32[4,3,2,48,128]{4,3,2,1,0:T(8,128)}, f32[4,3,2,48,128]{4,3,2,1,0:T(8,128)S(1)}) fusion(f32[4,3,2,48,128]{4,3,2,1,0:T(8,128)S(1)} %copy-done.7, f32[4,3,2,48,128]{4,3,2,1,0:T(8,128)S(1)} %copy-done.8, f32[3,2,48,128]{3,2,1,0:T(8,128)S(1)} %copy-done.15, f32[]{:T(128)S(6)} %div.112, f32[]{:T(128)S(6)} %mul.69, ...), kind=kLoop, calls=%fused_computation.19 | loop fusion | flops 1179648 | bytes 4276280 | tf_op jit(solution)/shard_map/add | solution.py:382
  122.4 5.9 %shard_map.101 = f32[4,3,2,48,128]{4,3,2,1,0:T(8,128)} custom-call(f32[4,3,2,48,128]{4,3,2,1,0:T(8,128)} %get-tuple-element.23.field_ref, f32[4,3,2,8,128]{4,3,2,1,0:T(8,128)} %broadcast_36_below_ref_above_ref.2.below_ref.above_ref, f32[4,3,2,8,128]{4,3,2,1,0:T(8,128)} %broadcast_36_below_ref_above_ref.2.below_ref.above_ref, ...), custom_call_target="tpu_custom_call" | custom-call | flops 76677120 | bytes 2555904 | tf_op jit(solution)/shard_map/pallas_call | solution.py:265
  131.2 1.5 %copy.45 = f32[4,3,64,2,128]{4,3,2,1,0:T(2,128)} copy(f32[4,3,64,2,128]{4,2,3,1,0:T(8,128)S(1)} %maximum_bitcast_fusion) | data formatting | bytes 1572864
  (108 shorter events, 17.9 us)
Async XLA Ops:
  0.6 1.8 %copy-start = (s32[2,128]{1,0:T(2,128)S(1)}, s32[2,128]{1,0:T(2,128)}, u32[]{:S(2)}) copy-start(s32[2,128]{1,0:T(2,128)} %param.13) | copy-start | bytes 3076
  0.6 6.2 %copy-start.19 = (f32[8]{0:T(128)S(1)}, f32[8]{0:T(128)}, u32[]{:S(2)}) copy-start(f32[8]{0:T(128)} %param.11) | copy-start | bytes 100
  0.7 6.9 %copy-start.18 = (s32[64,2,128]{2,1,0:T(2,128)S(1)}, s32[64,2,128]{2,1,0:T(2,128)}, u32[]{:S(2)}) copy-start(s32[64,2,128]{2,1,0:T(2,128)} %param.10) | copy-start | bytes 196612
  0.7 11.9 %copy-start.13 = (f32[4,3,64,2,128]{4,3,2,1,0:T(2,128)S(1)}, f32[4,3,64,2,128]{4,3,2,1,0:T(2,128)}, u32[]{:S(2)}) copy-start(f32[4,3,64,2,128]{4,3,2,1,0:T(2,128)} %param.9) | copy-start | bytes 2359300
  2.5 10.3 %copy-start.5 = (f32[4,3,64,2,128]{4,3,2,1,0:T(2,128)S(1)}, f32[4,3,64,2,128]{4,3,2,1,0:T(2,128)}, u32[]{:S(2)}) copy-start(f32[4,3,64,2,128]{4,3,2,1,0:T(2,128)} %param.8) | copy-start | bytes 2359300
  12.6 1.4 %copy-start.16 = (f32[2,64,128]{2,1,0:T(8,128)}, f32[2,64,128]{2,1,0:T(8,128)S(1)}, u32[]{:S(2)}) copy-start(f32[2,64,128]{2,1,0:T(8,128)S(1)} %add_bitcast_fusion.mod_ref) | copy-start | bytes 196612
  12.7 18.5 %copy-start.2 = (f32[4,3,64,2,128]{4,2,3,1,0:T(8,128)}, f32[4,3,64,2,128]{4,2,3,1,0:T(8,128)S(1)}, u32[]{:S(2)}) copy-start(f32[4,3,64,2,128]{4,2,3,1,0:T(8,128)S(1)} %copy.58) | copy-start | bytes 2359300
  12.9 0.9 copy-start.12
  34.2 1.5 %copy-start.9 = (f32[16,16128]{1,0:T(8,128)S(1)}, f32[16,16128]{1,0:T(8,128)}, u32[]{:S(2)}) copy-start(f32[16,16128]{1,0:T(8,128)} %gather_fusion.3) | copy-start | bytes 3096580
  38.9 53.7 %all-to-all-start = ((f32[16,2,16128]{2,1,0:T(2,128)}), f32[16,2,16128]{2,1,0:T(2,128)}, u32[]{:S(2)}, u32[]{:S(2)}) async-start(f32[16,2,16128]{2,1,0:T(2,128)} %copy.44), calls=%async_computation | async-start | bytes 4128768 | tf_op jit(solution)/shard_map/all_to_all | solution.py:309
  70.4 7.4 %copy-start.1 = (f32[4,3,2,64,128]{4,3,2,1,0:T(8,128)S(1)}, f32[4,3,2,64,128]{4,3,2,1,0:T(8,128)}, u32[]{:S(2)}) copy-start(f32[4,3,2,64,128]{4,3,2,1,0:T(8,128)} %broadcast_divide_fusion.field_ref) | copy-start | bytes 2359300
  70.4 7.4 %copy-start.4 = (f32[4,3,2,64,128]{4,3,2,1,0:T(8,128)S(1)}, f32[4,3,2,64,128]{4,3,2,1,0:T(8,128)}, u32[]{:S(2)}) copy-start(f32[4,3,2,64,128]{4,3,2,1,0:T(8,128)} %shard_map.99) | copy-start | bytes 2359300
  70.4 7.4 %copy-start.14 = (f32[3,2,64,128]{3,2,1,0:T(8,128)S(1)}, f32[3,2,64,128]{3,2,1,0:T(8,128)}, u32[]{:S(2)}) copy-start(f32[3,2,64,128]{3,2,1,0:T(8,128)} %get-tuple-element.13) | copy-start | bytes 589828
  80.2 7.5 %copy-start.17 = (f32[2,64,128]{2,1,0:T(8,128)S(1)}, f32[2,64,128]{2,1,0:T(8,128)}, u32[]{:S(2)}) copy-start(f32[2,64,128]{2,1,0:T(8,128)} %copy-done.16) | copy-start | bytes 196612
  80.2 8.1 %copy-start.3 = (f32[4,3,64,2,128]{4,2,3,1,0:T(8,128)S(1)}, f32[4,3,64,2,128]{4,2,3,1,0:T(8,128)}, u32[]{:S(2)}) copy-start(f32[4,3,64,2,128]{4,2,3,1,0:T(8,128)} %copy-done.2) | copy-start | bytes 2359300
  80.2 10.0 %copy-start.6 = (f32[4,3,2,64,128]{4,3,2,1,0:T(8,128)S(1)}, f32[4,3,2,64,128]{4,3,2,1,0:T(8,128)}, u32[]{:S(2)}) copy-start(f32[4,3,2,64,128]{4,3,2,1,0:T(8,128)} %get-tuple-element.20.field_ref) | copy-start | bytes 2359300
  112.0 8.2 %copy-start.7 = (f32[4,3,2,48,128]{4,3,2,1,0:T(8,128)S(1)}, f32[4,3,2,48,128]{4,3,2,1,0:T(8,128)}, u32[]{:S(2)}) copy-start(f32[4,3,2,48,128]{4,3,2,1,0:T(8,128)} %concatenate.42.field_ref) | copy-start | bytes 1769476
  112.0 8.1 %copy-start.15 = (f32[3,2,48,128]{3,2,1,0:T(8,128)S(1)}, f32[3,2,48,128]{3,2,1,0:T(8,128)}, u32[]{:S(2)}) copy-start(f32[3,2,48,128]{3,2,1,0:T(8,128)} %get-tuple-element.10) | copy-start | bytes 442372
  114.2 6.0 %copy-start.8 = (f32[4,3,2,48,128]{4,3,2,1,0:T(8,128)S(1)}, f32[4,3,2,48,128]{4,3,2,1,0:T(8,128)}, u32[]{:S(2)}) copy-start(f32[4,3,2,48,128]{4,3,2,1,0:T(8,128)} %get-tuple-element.25.field_ref) | copy-start | bytes 1769476
  122.4 7.2 %copy-start.11 = (f32[4,3,2,48,128]{4,3,2,1,0:T(8,128)S(1)}, f32[4,3,2,48,128]{4,3,2,1,0:T(8,128)}, u32[]{:S(2)}) copy-start(f32[4,3,2,48,128]{4,3,2,1,0:T(8,128)} %get-tuple-element.89) | copy-start | bytes 1769476
  129.5 1.6 %copy-start.10 = (f32[4,3,2,48,128]{4,3,2,1,0:T(8,128)S(1)}, f32[4,3,2,48,128]{4,3,2,1,0:T(8,128)}, u32[]{:S(2)}) copy-start(f32[4,3,2,48,128]{4,3,2,1,0:T(8,128)} %get-tuple-element.90) | copy-start | bytes 1769476

commit v4 on v3

--- a/solution.py
+++ b/solution.py
@@ -385,7 +385,7 @@
 
     disp_local, res_local = chain(modal_disp, loads, modulus, None)
 
-    edge_rows = 16
+    edge_rows = 8
     head = slice(0, edge_rows)
     tail = slice(depth - edge_rows, depth)
 
@@ -420,15 +420,13 @@
 
     disp_win, res_win = chain(md_win, ld_win, mod_win, valid)
 
+    reach = 3
+    sub_row = lax.broadcasted_iota(jnp.int32, (8, 1), 0)
+
     def merge(local, win):
-        return jnp.concatenate(
-            [
-                win[:, :, :, 8:16],
-                local[:, :, :, 8 : depth - 8],
-                win[:, :, :, 8 + 2 * edge_rows - 8 : 8 + 2 * edge_rows],
-            ],
-            axis=3,
-        )
+        top = jnp.where(sub_row < reach, win[:, :, :, 8:16], local[:, :, :, 0:8])
+        bottom = jnp.where(sub_row >= 8 - reach, win[:, :, :, 16:24], local[:, :, :, depth - 8 : depth])
+        return jnp.concatenate([top, local[:, :, :, 8 : depth - 8], bottom], axis=3)
 
     displacement = merge(disp_local, disp_win)
     residual = merge(res_local, res_win)

time: 135 us -> 129 us (0.956)
  Pallas kernels: 45.6 us -> 40.8 us
    pallas_call x6, Pallas kernels: 39.9 us -> 35.6 us  [stiffness(): pl.pallas_call(stencil_kernel, out_shape=jax.ShapeDtypeStruct(field.shape...]
    concatenate x3, local copies, waits for them, and re-layouts: 8.76 us -> 5.37 us  [window(): jnp.concatenate([jnp.stack(rows, axis=axis), own_head, own_tail, jnp.stac...]
    add x1 -> x2, other arithmetic: 2.23 us -> 4.82 us  [chain(): displacement = md + step0 + step1]
    add x1 -> x0, other arithmetic: 2.35 us -> none  [chain(): step1 = rho1 * rho0 * step0 + 2.0 * rho1 / half * residual1 / jacobi]
    unnamed x58 -> x56, local copies, waits for them, and re-layouts: 3.99 us -> 5.99 us
  transfers between devices with their start and end apart: 1 -> 1, of which waited for: 0 -> 0; matrix products, arithmetic and copies ran while one was open for 10% -> 11% of each run, Pallas kernels for 19% -> 20%
where the time goes in v4:
time: 129 us; the launch traced here: 127 us
  Pallas kernels  40.8 us (32%)
  local copies, waits for them, and re-layouts  32.4 us (25%)
  other arithmetic  22.6 us (18%)
  blocking collectives  14.3 us (11%)
  between operations  8.71 us (7%)
  starting transfers between devices  7.93 us (6%)
    pallas_call x6, Pallas kernels, stiffness(): pl.pallas_call(stencil_kernel, out_shape=jax.ShapeDtypeStruct(field.shape...  35.6 us
    all_gather x1, blocking collectives, exchange(): held = lax.all_gather(pack, 'grp', axis=0, tiled=True)  14.3 us
    all_to_all x1, starting transfers between devices, exchange(): got = lax.all_to_all(slots, 'col', 0, 0, tiled=True)  7.93 us
    unnamed x56, local copies, waits for them, and re-layouts  5.99 us
    transpose x1, other arithmetic, on_device(): modulus = jnp.transpose(lookup_modulus(material, moduli), (1, 0, 2))  5.84 us
    concatenate x3, local copies, waits for them, and re-layouts, window(): jnp.concatenate([jnp.stack(rows, axis=axis), own_head, own_tail, jnp.stac...  5.37 us
    pallas_call x2, Pallas kernels, edges_and_diagonal(): pl.pallas_call(edges_kernel, out_shape=(jax.ShapeDtypeStruct((len(OFFSETS...  5.21 us
    add x2, other arithmetic, chain(): displacement = md + step0 + step1  4.82 us
  transfers between devices with their start and end apart: 1, of which 0 were waited for; matrix products, arithmetic and copies ran while one was open for 11% of the time, Pallas kernels for 20%

profile of v4, /device:TPU:0, one launch (start us, length us, event | category | flops | bytes accessed | tf_op | source)
XLA Modules:
  0.0 126.7 jit_solution(3054352077125266523)
XLA Ops:
  0.7 1.6 %fusion.33 = (f32[1]{0:T(128)}, f32[1]{0:T(128)}, f32[1]{0:T(128)}, f32[1]{0:T(128)}, f32[1]{0:T(128)}, /*index=5*/f32[1]{0:T(128)}, f32[1]{0:T(128)}, f32[1]{0:T(128)}) fusion(f32[8]{0:T(128)} %param.11), kind=kLoop, calls=%fused_computation.120 | loop fusion | bytes 64 | tf_op jit(solution)/shard_map/slice | solution.py:277
  2.3 5.8 %add_bitcast_fusion.mod_ref = f32[2,64,128]{2,1,0:T(8,128)S(1)} fusion(s32[64,2,128]{2,1,0:T(2,128)} %param.10, f32[]{:T(128)} %bitcast.20, f32[]{:T(128)} %bitcast.19, f32[]{:T(128)} %bitcast.18, f32[]{:T(128)} %bitcast.17, f32[]{:T(128)} %bitcast.16, f32[]{:T(128)} %bitcast.15, f32[]{:T(128)} %bitcast.14, f32[]{:T(128)} %bitcast.13), kind=kLoop, calls=%fused_computation.28 | loop fusion | flops 376832 | bytes 131104 | tf_op jit(solution)/shard_map/transpose | solution.py:324
  10.7 14.3 %all-gather.1 = f32[8,2,16128]{2,1,0:T(2,128)S(1)} all-gather(f32[1,2,16128]{2,1,0:T(2,128)S(1)} %maximum_bitcast_fusion.2), channel_id=2, replica_groups=mesh['col'=16,'grp'=8] {'grp'}, dimensions={0}, use_global_device_ids=true | all-gather | bytes 1161216 | tf_op jit(solution)/shard_map/all_gather | solution.py:297
  26.1 1.5 %gather_fusion = s32[128]{0:T(128)S(1)} fusion(s32[2,128]{1,0:T(2,128)S(1)} %copy-done, s32[128]{0:T(128)S(1)} %fusion.16), kind=kCustom, calls=%fused_computation | custom fusion | bytes 2048 | tf_op jit(solution)/shard_map/gather | solution.py:287
  27.6 1.5 %gather_fusion.1 = s32[128]{0:T(128)S(1)} fusion(s32[2,128]{1,0:T(2,128)S(1)} %copy-done, s32[128]{0:T(128)S(1)} %get-tuple-element.25), kind=kCustom, calls=%fused_computation.1 | custom fusion | bytes 2048 | tf_op jit(solution)/shard_map/gather | solution.py:286
  30.5 3.0 %gather_fusion.3 = f32[16,16128]{1,0:T(8,128)} fusion(f32[8,2,16128]{2,1,0:T(2,128)S(1)} %all-gather.1, s32[16]{0:T(128)S(1)} %get-tuple-element.85), kind=kCustom, calls=%fused_computation.3 | custom fusion | bytes 2064512 | tf_op jit(solution)/shard_map/gather | solution.py:303
  33.4 2.1 %gather_fusion.5 = f32[16,16128]{1,0:T(8,128)S(1)} fusion(f32[8,2,16128]{2,1,0:T(2,128)S(1)} %all-gather.1, s32[16]{0:T(128)S(1)} %get-tuple-element.86), kind=kCustom, calls=%fused_computation.5 | custom fusion | bytes 2064512 | tf_op jit(solution)/shard_map/gather | solution.py:304
  37.2 2.9 %copy.44 = f32[16,2,16128]{2,1,0:T(2,128)} copy(f32[16,2,16128]{2,0,1:T(8,128)S(1)} %pad_maximum_fusion) | data formatting | bytes 4128768 | tf_op jit(solution)/shard_map/stack | solution.py:308
  40.1 7.9 %all-to-all-start = ((f32[16,2,16128]{2,1,0:T(2,128)}), f32[16,2,16128]{2,1,0:T(2,128)}, u32[]{:S(2)}, u32[]{:S(2)}) async-start(f32[16,2,16128]{2,1,0:T(2,128)} %copy.44), calls=%async_computation | async-start | bytes 4128768 | tf_op jit(solution)/shard_map/all_to_all | solution.py:309
  57.3 3.0 %shard_map.98 = (f32[26,2,64,128]{3,2,1,0:T(8,128)}, f32[2,64,128]{2,1,0:T(8,128)}, f32[3,2,64,128]{3,2,1,0:T(8,128)}) custom-call(f32[2,64,128]{2,1,0:T(8,128)} %copy-done.17, f32[2,8,128]{2,1,0:T(8,128)} %broadcast_41_below_ref_above_ref.2.below_ref.above_ref, f32[2,8,128]{2,1,0:T(8,128)} %broadcast_41_below_ref_above_ref.2.below_ref.above_ref), custom_call_target="tpu_custom_call" | custom-call | flops 3407872 | bytes 2031616 | tf_op jit(solution)/shard_map/pallas_call | solution.py:129
  61.9 7.3 %shard_map.99 = f32[4,3,2,64,128]{4,3,2,1,0:T(8,128)} custom-call(f32[4,3,2,64,128]{4,3,2,1,0:T(8,128)} %bitcast.106, f32[4,3,2,8,128]{4,3,2,1,0:T(8,128)} %broadcast_40_below_ref_above_ref.2.below_ref.above_ref, f32[4,3,2,8,128]{4,3,2,1,0:T(8,128)} %broadcast_40_below_ref_above_ref.2.below_ref.above_ref, f32[26,2,64,128]{3,2,1,0:T(8,128)} %get-tuple-element.11.edge_ref, ...), custom_call_target="tpu_custom_call" | custom-call | flops 102236160 | bytes 3407872 | tf_op jit(solution)/shard_map/pallas_call | solution.py:265
  69.2 2.3 %broadcast_divide_fusion.field_ref = f32[4,3,2,64,128]{4,3,2,1,0:T(8,128)} fusion(f32[3,2,64,128]{3,2,1,0:T(8,128)S(1)} %broadcast_multiply_fusion, f32[4,3,2,64,128]{4,3,2,1,0:T(8,128)} %shard_map.99, f32[4,3,64,2,128]{4,3,2,1,0:T(2,128)S(1)} %copy-done.2), kind=kLoop, calls=%fused_computation.16 | loop fusion | flops 393216 | bytes 2555904 | tf_op jit(solution)/shard_map/div | solution.py:375
  71.5 7.4 %shard_map.100 = f32[4,3,2,64,128]{4,3,2,1,0:T(8,128)} custom-call(f32[4,3,2,64,128]{4,3,2,1,0:T(8,128)} %broadcast_divide_fusion.field_ref, f32[4,3,2,8,128]{4,3,2,1,0:T(8,128)} %broadcast_40_below_ref_above_ref.2.below_ref.above_ref, f32[4,3,2,8,128]{4,3,2,1,0:T(8,128)} %broadcast_40_below_ref_above_ref.2.below_ref.above_ref, ...), custom_call_target="tpu_custom_call" | custom-call | flops 102236160 | bytes 3407872 | tf_op jit(solution)/shard_map/pallas_call | solution.py:265
  78.9 2.7 %add_add_fusion = (f32[4,3,2,64,128]{4,3,2,1,0:T(8,128)}, f32[4,3,2,64,128]{4,3,2,1,0:T(8,128)}) fusion(f32[4,3,2,64,128]{4,3,2,1,0:T(8,128)S(1)} %copy-done.3, f32[4,3,64,2,128]{4,3,2,1,0:T(2,128)S(1)} %copy-done.8, f32[3,2,64,128]{3,2,1,0:T(8,128)S(1)} %copy-done.15, f32[4,3,2,64,128]{4,3,2,1,0:T(8,128)} %shard_map.100, ...), kind=kLoop, calls=%fused_computation.15 | loop fusion | flops 1572864 | bytes 5701640 | tf_op jit(solution)/shard_map/add | solution.py:382
  81.6 7.4 %shard_map.102 = f32[4,3,2,64,128]{4,3,2,1,0:T(8,128)} custom-call(f32[4,3,2,64,128]{4,3,2,1,0:T(8,128)} %get-tuple-element.28.field_ref, f32[4,3,2,8,128]{4,3,2,1,0:T(8,128)} %broadcast_40_below_ref_above_ref.2.below_ref.above_ref, f32[4,3,2,8,128]{4,3,2,1,0:T(8,128)} %broadcast_40_below_ref_above_ref.2.below_ref.above_ref, ...), custom_call_target="tpu_custom_call" | custom-call | flops 102236160 | bytes 3407872 | tf_op jit(solution)/shard_map/pallas_call | solution.py:265
  96.2 2.4 %concatenate.45.mod_ref = f32[2,32,128]{2,1,0:T(8,128)} concatenate(f32[2,1,128]{2,1,0:T(1,128)S(1)} %broadcast.451, f32[2,4,128]{2,1,0:T(4,128)S(1)} %broadcast.452, f32[2,1,128]{2,1,0:T(1,128)S(1)} %get-tuple-element.72, f32[2,1,128]{2,1,0:T(1,128)S(1)} %get-tuple-element.71, f32[2,1,128]{2,1,0:T(1,128)S(1)} %get-tuple-element.70, f32[2,8,128]{2,1,0:T(8,128)S(1)} %get-tuple-element.50, ...), dimensions={1} | concatenate | bytes 65536 | tf_op jit(solution)/shard_map/concatenate | solution.py:401
  98.7 2.2 %shard_map.95 = (f32[26,2,32,128]{3,2,1,0:T(8,128)}, f32[2,32,128]{2,1,0:T(8,128)}, f32[3,2,32,128]{3,2,1,0:T(8,128)}) custom-call(f32[2,32,128]{2,1,0:T(8,128)} %concatenate.45.mod_ref, f32[2,8,128]{2,1,0:T(8,128)} %broadcast_41_below_ref_above_ref.2.below_ref.above_ref, f32[2,8,128]{2,1,0:T(8,128)} %broadcast_41_below_ref_above_ref.2.below_ref.above_ref), custom_call_target="tpu_custom_call" | custom-call | flops 1703936 | bytes 1015808 | tf_op jit(solution)/shard_map/pallas_call | solution.py:129
  101.8 2.8 %concatenate.42.field_ref = f32[4,3,2,32,128]{4,3,2,1,0:T(8,128)} concatenate(f32[4,3,2,1,128]{4,3,2,1,0:T(1,128)S(1)} %broadcast.437, f32[4,3,2,4,128]{4,3,2,1,0:T(4,128)S(1)} %broadcast.438, f32[4,3,2,1,128]{4,3,2,1,0:T(1,128)S(1)} %bitcast.126, f32[4,3,2,1,128]{4,3,2,1,0:T(1,128)S(1)} %bitcast.125, f32[4,3,2,1,128]{4,3,2,1,0:T(1,128)S(1)} %bitcast.124, ...), dimensions={3} | concatenate | bytes 786432 | tf_op jit(solution)/shard_map/concatenate | solution.py:401
  104.5 4.4 %shard_map.96 = f32[4,3,2,32,128]{4,3,2,1,0:T(8,128)} custom-call(f32[4,3,2,32,128]{4,3,2,1,0:T(8,128)} %concatenate.42.field_ref, f32[4,3,2,8,128]{4,3,2,1,0:T(8,128)} %broadcast_40_below_ref_above_ref.2.below_ref.above_ref, f32[4,3,2,8,128]{4,3,2,1,0:T(8,128)} %broadcast_40_below_ref_above_ref.2.below_ref.above_ref, ...), custom_call_target="tpu_custom_call" | custom-call | flops 51118080 | bytes 1703936 | tf_op jit(solution)/shard_map/pallas_call | solution.py:265
  109.2 2.0 %divide_select_fusion = (f32[4,3,2,32,128]{4,3,2,1,0:T(8,128)}, f32[4,3,2,32,128]{4,3,2,1,0:T(8,128)S(1)}) fusion(f32[3,2,32,128]{3,2,1,0:T(8,128)S(1)} %broadcast_multiply_fusion.1, pred[32]{0:T(512)(128)(4,1)S(1)} %get-tuple-element.76, f32[4,3,2,32,128]{4,3,2,1,0:T(8,128)S(1)} %concatenate.44, f32[4,3,2,32,128]{4,3,2,1,0:T(8,128)} %shard_map.96), kind=kLoop, calls=%fused_computation.19 | loop fusion | flops 294912 | bytes 1671200 | tf_op jit(solution)/shard_map/jit(_where)/select_n | solution.py:377
  111.1 4.5 %shard_map.97 = f32[4,3,2,32,128]{4,3,2,1,0:T(8,128)} custom-call(f32[4,3,2,32,128]{4,3,2,1,0:T(8,128)} %get-tuple-element.23.field_ref, f32[4,3,2,8,128]{4,3,2,1,0:T(8,128)} %broadcast_40_below_ref_above_ref.2.below_ref.above_ref, f32[4,3,2,8,128]{4,3,2,1,0:T(8,128)} %broadcast_40_below_ref_above_ref.2.below_ref.above_ref, ...), custom_call_target="tpu_custom_call" | custom-call | flops 51118080 | bytes 1703936 | tf_op jit(solution)/shard_map/pallas_call | solution.py:265
  115.6 2.2 %add_add_fusion.1 = (f32[4,3,2,32,128]{4,3,2,1,0:T(8,128)}, f32[4,3,2,32,128]{4,3,2,1,0:T(8,128)}, f32[4,3,2,32,128]{4,3,2,1,0:T(8,128)S(1)}) fusion(f32[4,3,2,32,128]{4,3,2,1,0:T(8,128)S(1)} %copy-done.6, f32[4,3,2,32,128]{4,3,2,1,0:T(8,128)S(1)} %copy-done.7, f32[3,2,32,128]{3,2,1,0:T(8,128)S(1)} %copy-done.16, f32[]{:T(128)S(6)} %div.112, f32[]{:T(128)S(6)} %mul.69, ...), kind=kLoop, calls=%fused_computation.18 | loop fusion | flops 786432 | bytes 2850856 | tf_op jit(solution)/shard_map/add | solution.py:382
  117.8 4.5 %shard_map.101 = f32[4,3,2,32,128]{4,3,2,1,0:T(8,128)} custom-call(f32[4,3,2,32,128]{4,3,2,1,0:T(8,128)} %get-tuple-element.21.field_ref, f32[4,3,2,8,128]{4,3,2,1,0:T(8,128)} %broadcast_40_below_ref_above_ref.2.below_ref.above_ref, f32[4,3,2,8,128]{4,3,2,1,0:T(8,128)} %broadcast_40_below_ref_above_ref.2.below_ref.above_ref, ...), custom_call_target="tpu_custom_call" | custom-call | flops 51118080 | bytes 1703936 | tf_op jit(solution)/shard_map/pallas_call | solution.py:265
  123.7 1.5 %copy.46 = f32[4,3,64,2,128]{4,3,2,1,0:T(2,128)} copy(f32[4,3,64,2,128]{4,2,3,1,0:T(8,128)S(1)} %maximum_bitcast_fusion.1) | data formatting | bytes 1572864
  (109 shorter events, 20.8 us)
Async XLA Ops:
  0.6 25.4 %copy-start = (s32[2,128]{1,0:T(2,128)S(1)}, s32[2,128]{1,0:T(2,128)}, u32[]{:S(2)}) copy-start(s32[2,128]{1,0:T(2,128)} %param.13) | copy-start | bytes 3076
  0.6 8.8 %copy-start.2 = (f32[4,3,64,2,128]{4,3,2,1,0:T(2,128)S(1)}, f32[4,3,64,2,128]{4,3,2,1,0:T(2,128)}, u32[]{:S(2)}) copy-start(f32[4,3,64,2,128]{4,3,2,1,0:T(2,128)} %param.8) | copy-start | bytes 2359300
  8.1 2.6 %copy-start.17 = (f32[2,64,128]{2,1,0:T(8,128)}, f32[2,64,128]{2,1,0:T(8,128)S(1)}, u32[]{:S(2)}) copy-start(f32[2,64,128]{2,1,0:T(8,128)S(1)} %add_bitcast_fusion.mod_ref) | copy-start | bytes 196612
  9.4 18.2 %copy-start.5 = (f32[4,3,64,2,128]{4,2,3,1,0:T(8,128)}, f32[4,3,64,2,128]{4,2,3,1,0:T(8,128)S(1)}, u32[]{:S(2)}) copy-start(f32[4,3,64,2,128]{4,2,3,1,0:T(8,128)S(1)} %copy.64) | copy-start | bytes 2359300
  9.4 15.6 %copy-start.18 = (s32[128]{0:T(128)S(1)}, s32[128]{0:T(128)}, u32[]{:S(2)}) copy-start(s32[128]{0:T(128)} %param.12) | copy-start | bytes 1540
  9.6 1.0 copy-start.13
  40.1 55.0 %all-to-all-start = ((f32[16,2,16128]{2,1,0:T(2,128)}), f32[16,2,16128]{2,1,0:T(2,128)}, u32[]{:S(2)}, u32[]{:S(2)}) async-start(f32[16,2,16128]{2,1,0:T(2,128)} %copy.44), calls=%async_computation | async-start | bytes 4128768 | tf_op jit(solution)/shard_map/all_to_all | solution.py:309
  71.5 7.4 %copy-start.1 = (f32[4,3,2,64,128]{4,3,2,1,0:T(8,128)S(1)}, f32[4,3,2,64,128]{4,3,2,1,0:T(8,128)}, u32[]{:S(2)}) copy-start(f32[4,3,2,64,128]{4,3,2,1,0:T(8,128)} %shard_map.99) | copy-start | bytes 2359300
  71.5 7.4 %copy-start.3 = (f32[4,3,2,64,128]{4,3,2,1,0:T(8,128)S(1)}, f32[4,3,2,64,128]{4,3,2,1,0:T(8,128)}, u32[]{:S(2)}) copy-start(f32[4,3,2,64,128]{4,3,2,1,0:T(8,128)} %broadcast_divide_fusion.field_ref) | copy-start | bytes 2359300
  71.5 7.4 %copy-start.8 = (f32[4,3,64,2,128]{4,3,2,1,0:T(2,128)S(1)}, f32[4,3,64,2,128]{4,3,2,1,0:T(2,128)}, u32[]{:S(2)}) copy-start(f32[4,3,64,2,128]{4,3,2,1,0:T(2,128)} %param.9) | copy-start | bytes 2359300
  71.5 7.4 %copy-start.15 = (f32[3,2,64,128]{3,2,1,0:T(8,128)S(1)}, f32[3,2,64,128]{3,2,1,0:T(8,128)}, u32[]{:S(2)}) copy-start(f32[3,2,64,128]{3,2,1,0:T(8,128)} %get-tuple-element.13) | copy-start | bytes 589828
  81.6 7.4 %copy-start.4 = (f32[4,3,2,64,128]{4,3,2,1,0:T(8,128)S(1)}, f32[4,3,2,64,128]{4,3,2,1,0:T(8,128)}, u32[]{:S(2)}) copy-start(f32[4,3,2,64,128]{4,3,2,1,0:T(8,128)} %shard_map.100) | copy-start | bytes 2359300
  89.0 2.4 %copy-start.9 = (f32[4,3,2,64,128]{4,3,2,1,0:T(8,128)S(1)}, f32[4,3,2,64,128]{4,3,2,1,0:T(8,128)}, u32[]{:S(2)}) copy-start(f32[4,3,2,64,128]{4,3,2,1,0:T(8,128)} %get-tuple-element.27) | copy-start | bytes 2359300
  90.5 0.9 copy-start.10
  109.0 6.7 %copy-start.6 = (f32[4,3,2,32,128]{4,3,2,1,0:T(8,128)S(1)}, f32[4,3,2,32,128]{4,3,2,1,0:T(8,128)}, u32[]{:S(2)}) copy-start(f32[4,3,2,32,128]{4,3,2,1,0:T(8,128)} %concatenate.42.field_ref) | copy-start | bytes 1179652
  109.0 6.7 %copy-start.16 = (f32[3,2,32,128]{3,2,1,0:T(8,128)S(1)}, f32[3,2,32,128]{3,2,1,0:T(8,128)}, u32[]{:S(2)}) copy-start(f32[3,2,32,128]{3,2,1,0:T(8,128)} %get-tuple-element.10) | copy-start | bytes 294916
  111.1 4.5 %copy-start.7 = (f32[4,3,2,32,128]{4,3,2,1,0:T(8,128)S(1)}, f32[4,3,2,32,128]{4,3,2,1,0:T(8,128)}, u32[]{:S(2)}) copy-start(f32[4,3,2,32,128]{4,3,2,1,0:T(8,128)} %get-tuple-element.23.field_ref) | copy-start | bytes 1179652
  117.8 5.6 %copy-start.11 = (f32[4,3,2,64,128]{4,3,2,1,0:T(8,128)S(1)}, f32[4,3,2,64,128]{4,3,2,1,0:T(8,128)}, u32[]{:S(2)}) copy-start(f32[4,3,2,64,128]{4,3,2,1,0:T(8,128)} %copy-done.10) | copy-start | bytes 2359300
  117.8 5.6 %copy-start.14 = (f32[4,3,2,32,128]{4,3,2,1,0:T(8,128)S(1)}, f32[4,3,2,32,128]{4,3,2,1,0:T(8,128)}, u32[]{:S(2)}) copy-start(f32[4,3,2,32,128]{4,3,2,1,0:T(8,128)} %get-tuple-element.20) | copy-start | bytes 1179652
  117.8 5.8 %slice-start = ((f32[4,3,2,64,128]{4,3,2,1,0:T(8,128)}), f32[4,3,2,48,128]{4,3,2,1,0:T(8,128)S(1)}, s32[]{:S(2)}) async-start(f32[4,3,2,64,128]{4,3,2,1,0:T(8,128)} %copy-done.10), calls=%async_computation.1 | async-start | bytes 1179648 | tf_op jit(solution)/shard_map/slice | solution.py:429
  123.4 1.7 %copy-start.12 = (f32[4,3,2,48,128]{4,3,2,1,0:T(8,128)S(1)}, f32[4,3,2,48,128]{4,3,2,1,0:T(8,128)}, u32[]{:S(2)}) copy-start(f32[4,3,2,48,128]{4,3,2,1,0:T(8,128)} %slice.356) | copy-start | bytes 1769476

commit v5 on v4

--- a/solution.py
+++ b/solution.py
@@ -53,23 +53,22 @@
     return jnp.stack(comps, axis=0)
 
 
-def edges_kernel(mod_ref, below_ref, above_ref, edge_ref, centre_ref, diag_ref):
+def edges_body(mod_ref, edge_ref, centre_ref, diag_ref):
     rows_y, depth, width = mod_ref.shape
     chunks = depth // 8
     sub = lax.broadcasted_iota(jnp.int32, (8, width), 0)
     lane = lax.broadcasted_iota(jnp.int32, (8, width), 1)
+    zero = jnp.zeros((8, width), jnp.float32)
 
     def body(it, carry):
         r = pl.multiple_of(it * 8, 8)
         centre = [mod_ref[y, pl.ds(r, 8), :] for y in range(rows_y)]
         prev = [
-            jnp.where(it == 0, below_ref[y], mod_ref[y, pl.ds(jnp.maximum(r - 8, 0), 8), :])
+            jnp.where(it == 0, zero, mod_ref[y, pl.ds(jnp.maximum(r - 8, 0), 8), :])
             for y in range(rows_y)
         ]
         nxt = [
-            jnp.where(
-                it == chunks - 1, above_ref[y], mod_ref[y, pl.ds(jnp.minimum(r + 8, depth - 8), 8), :]
-            )
+            jnp.where(it == chunks - 1, zero, mod_ref[y, pl.ds(jnp.minimum(r + 8, depth - 8), 8), :])
             for y in range(rows_y)
         ]
         comps = [[GAMMA * centre[y] for y in range(rows_y)] for c in range(3)]
@@ -104,7 +103,7 @@
                         if 0 <= source < rows_y:
                             other = shifted[off_z][source]
                         else:
-                            other = jnp.zeros_like(centre[y])
+                            other = zero
                         edge = EDGE_WEIGHTS[norm_sq] * 0.5 * (centre[y] + other)
                         edge_ref[index, y, pl.ds(r, 8), :] = edge
                         for c in range(3):
@@ -121,48 +120,29 @@
     lax.fori_loop(0, chunks, body, 0)
 
 
-def edges_and_diagonal(modulus, below, above):
-    rows_y, depth, width = modulus.shape
-    vmem = pl.BlockSpec(memory_space=pltpu.VMEM)
-    halo_below = jnp.broadcast_to(below[:, None], (rows_y, 8, width))
-    halo_above = jnp.broadcast_to(above[:, None], (rows_y, 8, width))
-    return pl.pallas_call(
-        edges_kernel,
-        out_shape=(
-            jax.ShapeDtypeStruct((len(OFFSETS), rows_y, depth, width), jnp.float32),
-            jax.ShapeDtypeStruct((rows_y, depth, width), jnp.float32),
-            jax.ShapeDtypeStruct((3, rows_y, depth, width), jnp.float32),
-        ),
-        in_specs=[vmem, vmem, vmem],
-        out_specs=(vmem, vmem, vmem),
-        cost_estimate=pl.CostEstimate(
-            flops=26 * 8 * modulus.size, bytes_accessed=4 * 31 * modulus.size, transcendentals=0
-        ),
-    )(modulus, halo_below, halo_above)
-
-
-def stencil_kernel(field_ref, below_ref, above_ref, edge_ref, cm_ref, out_ref):
+def stencil_body(field_ref, edge_ref, cm_ref, out_ref):
     samples, _, rows_y, depth, width = field_ref.shape
     chunks = depth // 8
     sub = lax.broadcasted_iota(jnp.int32, (8, width), 0)
     lane = lax.broadcasted_iota(jnp.int32, (8, width), 1)
+    zero = jnp.zeros((8, width), jnp.float32)
 
     def body(it, carry):
         s = it // chunks
-        r = pl.multiple_of((it % chunks) * 8, 8)
-
-        first = (it % chunks) == 0
-        last = (it % chunks) == chunks - 1
+        part = it % chunks
+        r = pl.multiple_of(part * 8, 8)
 
         def rows(c, y, off):
             if off == 0:
                 return field_ref[s, c, y, pl.ds(r, 8), :]
             if off < 0:
                 return jnp.where(
-                    first, below_ref[s, c, y], field_ref[s, c, y, pl.ds(jnp.maximum(r - 8, 0), 8), :]
+                    part == 0, zero, field_ref[s, c, y, pl.ds(jnp.maximum(r - 8, 0), 8), :]
                 )
             return jnp.where(
-                last, above_ref[s, c, y], field_ref[s, c, y, pl.ds(jnp.minimum(r + 8, depth - 8), 8), :]
+                part == chunks - 1,
+                zero,
+                field_ref[s, c, y, pl.ds(jnp.minimum(r + 8, depth - 8), 8), :],
             )
 
         centre = [[rows(c, y, 0) for y in range(rows_y)] for c in range(3)]
@@ -198,26 +178,18 @@
                     ]
                     for c in range(3)
                 ]
-            shifted = {}
-            for off_z in (-1, 0, 1):
-                if off_z == 0:
-                    shifted[off_z] = shifted_x
-                elif off_z < 0:
-                    shifted[off_z] = [
-                        [
-                            jnp.where(lane == 0, jnp.float32(0.0), pltpu.roll(v, 1, 1))
-                            for v in per_c
-                        ]
-                        for per_c in shifted_x
-                    ]
-                else:
-                    shifted[off_z] = [
-                        [
-                            jnp.where(lane == width - 1, jnp.float32(0.0), pltpu.roll(v, width - 1, 1))
-                            for v in per_c
-                        ]
-                        for per_c in shifted_x
-                    ]
+            shifted = {0: shifted_x}
+            shifted[-1] = [
+                [jnp.where(lane == 0, jnp.float32(0.0), pltpu.roll(v, 1, 1)) for v in per_c]
+                for per_c in shifted_x
+            ]
+            shifted[1] = [
+                [
+                    jnp.where(lane == width - 1, jnp.float32(0.0), pltpu.roll(v, width - 1, 1))
+                    for v in per_c
+                ]
+                for per_c in shifted_x
+            ]
             for off_y in (-1, 0, 1):
                 for off_z in (-1, 0, 1):
                     if (off_x, off_y, off_z) == (0, 0, 0):
@@ -255,20 +227,80 @@
     lax.fori_loop(0, samples * chunks, body, 0)
 
 
-def stiffness(field, below, above, edges, centre_mod):
-    samples, _, rows_y, depth, width = field.shape
-    halo_shape = (samples, 3, rows_y, 8, width)
-    halo_below = jnp.broadcast_to(below[:, :, :, None], halo_shape)
-    halo_above = jnp.broadcast_to(above[:, :, :, None], halo_shape)
+def chain_kernel(
+    scal_ref, mask_ref, md_ref, ld_ref, mod_ref, disp_ref, res_ref,
+    edge_s, cm_s, jac_s, k_s, a_s, step0_s, step1_s,
+):
+    samples, _, rows_y, depth, width = md_ref.shape
+    theta = scal_ref[0]
+    c1 = scal_ref[1]
+    c2 = scal_ref[2]
+    edges_body(mod_ref, edge_s, cm_s, jac_s)
+    stencil_body(md_ref, edge_s, cm_s, k_s)
+    keep0 = mask_ref[0] > 0.0
+    keep1 = mask_ref[1] > 0.0
+
+    def first(it, carry):
+        s = it // 3
+        c = it % 3
+        for y in range(rows_y):
+            start = ld_ref[s, c, y] - k_s[s, c, y]
+            a_s[s, c, y] = start
+            step0_s[s, c, y] = jnp.where(keep0, start / (theta * jac_s[c, y]), jnp.float32(0.0))
+        return carry
+
+    lax.fori_loop(0, samples * 3, first, 0)
+    stencil_body(step0_s, edge_s, cm_s, k_s)
+
+    def second(it, carry):
+        s = it // 3
+        c = it % 3
+        for y in range(rows_y):
+            residual1 = a_s[s, c, y] - k_s[s, c, y]
+            a_s[s, c, y] = residual1
+            step0 = step0_s[s, c, y]
+            step1 = jnp.where(
+                keep1, c1 * step0 + c2 * residual1 / jac_s[c, y], jnp.float32(0.0)
+            )
+            step1_s[s, c, y] = step1
+            disp_ref[s, c, y] = md_ref[s, c, y] + step0 + step1
+        return carry
+
+    lax.fori_loop(0, samples * 3, second, 0)
+    stencil_body(step1_s, edge_s, cm_s, k_s)
+
+    def third(it, carry):
+        s = it // 3
+        c = it % 3
+        for y in range(rows_y):
+            res_ref[s, c, y] = a_s[s, c, y] - k_s[s, c, y]
+        return carry
+
+    lax.fori_loop(0, samples * 3, third, 0)
+
+
+def run_chain(scalars, masks, md, ld, mod):
+    samples, _, rows_y, depth, width = md.shape
     vmem = pl.BlockSpec(memory_space=pltpu.VMEM)
-    size = samples * 3 * rows_y * depth * width
+    smem = pl.BlockSpec(memory_space=pltpu.SMEM)
+    field = jax.ShapeDtypeStruct(md.shape, jnp.float32)
+    size = md.size
     return pl.pallas_call(
-        stencil_kernel,
-        out_shape=jax.ShapeDtypeStruct(field.shape, jnp.float32),
-        in_specs=[vmem] * 5,
-        out_specs=vmem,
-        cost_estimate=pl.CostEstimate(flops=26 * 20 * size, bytes_accessed=4 * (2 * size + 28 * size // samples // 3), transcendentals=0),
-    )(field, halo_below, halo_above, edges, centre_mod)
+        chain_kernel,
+        out_shape=(field, field),
+        in_specs=[smem, vmem, vmem, vmem, vmem],
+        out_specs=(vmem, vmem),
+        scratch_shapes=[
+            pltpu.VMEM((len(OFFSETS), rows_y, depth, width), jnp.float32),
+            pltpu.VMEM((rows_y, depth, width), jnp.float32),
+            pltpu.VMEM((3, rows_y, depth, width), jnp.float32),
+        ]
+        + [pltpu.VMEM(md.shape, jnp.float32)] * 4,
+        compiler_params=pltpu.CompilerParams(vmem_limit_bytes=48 * 1024 * 1024),
+        cost_estimate=pl.CostEstimate(
+            flops=3 * 26 * 20 * size, bytes_accessed=4 * 5 * size, transcendentals=0
+        ),
+    )(scalars, masks, md, ld, mod)
 
 
 def lookup_modulus(material, moduli):
@@ -365,25 +397,12 @@
     rho0 = 1.0 / sigma
     rho1 = 1.0 / (2.0 * sigma - rho0)
 
-    def chain(md, ld, mod, valid):
-        edges, centre_mod, jacobi = edges_and_diagonal(mod, zero_mod, zero_mod)
-
-        def apply(field):
-            return stiffness(field, zero_plane, zero_plane, edges, centre_mod)
-
-        start = ld - apply(md)
-        step0 = start / (theta * jacobi)
-        if valid is not None:
-            step0 = jnp.where(valid(2), step0, jnp.float32(0.0))
-        residual1 = start - apply(step0)
-        step1 = rho1 * rho0 * step0 + 2.0 * rho1 / half * residual1 / jacobi
-        if valid is not None:
-            step1 = jnp.where(valid(1), step1, jnp.float32(0.0))
-        displacement = md + step0 + step1
-        residual = residual1 - apply(step1)
-        return displacement, residual
-
-    disp_local, res_local = chain(modal_disp, loads, modulus, None)
+    scalars = jnp.stack([theta, rho1 * rho0, 2.0 * rho1 / half]).astype(jnp.float32)
+
+    def chain(md, ld, mod, masks):
+        return run_chain(scalars, masks, md, ld, mod)
+
+    disp_local, res_local = chain(modal_disp, loads, modulus, jnp.ones((2, depth, width), jnp.float32))
 
     edge_rows = 8
     head = slice(0, edge_rows)
@@ -416,9 +435,10 @@
         keep = (logical >= 0) & (logical < depth)
         keep = keep | (low_on & (logical >= -reach) & (logical < 0))
         keep = keep | (up_on & (logical >= depth) & (logical < depth + reach))
-        return keep.reshape(-1, 1)
-
-    disp_win, res_win = chain(md_win, ld_win, mod_win, valid)
+        return jnp.broadcast_to(keep.astype(jnp.float32)[:, None], (logical.shape[0], width))
+
+    masks = jnp.stack([valid(2), valid(1)], axis=0)
+    disp_win, res_win = chain(md_win, ld_win, mod_win, masks)
 
     reach = 3
     sub_row = lax.broadcasted_iota(jnp.int32, (8, 1), 0)

time: 129 us -> 94.6 us (0.73); the launches traced: 127 us -> 94.1 us
  Pallas kernels: 40.8 us -> 25 us
  other arithmetic: 22.6 us -> 10.6 us
  local copies, waits for them, and re-layouts: 32.4 us -> 24.3 us
  waiting for transfers between devices: 0.01 us -> 2.92 us
    pallas_call x8 -> x2, Pallas kernels: 40.8 us -> 25 us  [run_chain(): pl.pallas_call(chain_kernel, out_shape=(field, field), in_specs=[smem, vm...]
    concatenate x3, local copies, waits for them, and re-layouts: 5.37 us -> 0.46 us  [window(): jnp.concatenate([jnp.stack(rows, axis=axis), own_head, own_tail, jnp.stac...]
    add x2 -> x0, other arithmetic: 4.82 us -> none  [chain(): displacement = md + step0 + step1]
    all_to_all x1, waiting for transfers between devices: 0.01 us -> 2.92 us  [exchange(): got = lax.all_to_all(slots, 'col', 0, 0, tiled=True)]
    unnamed x56 -> x24, local copies, waits for them, and re-layouts: 5.99 us -> 3.15 us
    slice x3, local copies, waits for them, and re-layouts: 2.63 us -> 0.03 us  [window(): own_tail = own[tuple(index)]]
    sub x2 -> x0, other arithmetic: 2.57 us -> none  [chain(): residual = residual1 - apply(step1)]
    div x1 -> x0, other arithmetic: 2.27 us -> none  [chain(): step0 = start / (theta * jacobi)]
  transfers between devices with their start and end apart: 1 -> 1, of which waited for: 0 -> 1; matrix products, arithmetic and copies ran while one was open for 11% -> 3% of each run, Pallas kernels for 20% -> 17%
where the time goes in v5:
time: 94.6 us; the launch traced here: 94.1 us
  Pallas kernels  25 us (26%)
  local copies, waits for them, and re-layouts  24.3 us (26%)
  blocking collectives  14.3 us (15%)
  other arithmetic  10.6 us (11%)
  between operations  9.08 us (10%)
  starting transfers between devices  7.93 us (8%)
  waiting for transfers between devices  2.92 us (3%)
    pallas_call x2, Pallas kernels, run_chain(): pl.pallas_call(chain_kernel, out_shape=(field, field), in_specs=[smem, vm...  25 us
    all_gather x1, blocking collectives, exchange(): held = lax.all_gather(pack, 'grp', axis=0, tiled=True)  14.3 us
    all_to_all x1, starting transfers between devices, exchange(): got = lax.all_to_all(slots, 'col', 0, 0, tiled=True)  7.93 us
    transpose x1, other arithmetic, on_device(): modulus = jnp.transpose(lookup_modulus(material, moduli), (1, 0, 2))  6.04 us
    unnamed x24, local copies, waits for them, and re-layouts  3.15 us
    gather x1, local copies, waits for them, and re-layouts, exchange(): from_low = held[t_low % GROUP, 1]  2.99 us
    gather x1, local copies, waits for them, and re-layouts, exchange(): from_up = held[t_up % GROUP, 0]  2.96 us
    all_to_all x1, waiting for transfers between devices, exchange(): got = lax.all_to_all(slots, 'col', 0, 0, tiled=True)  2.92 us
  transfers between devices with their start and end apart: 1, of which 1 were waited for; matrix products, arithmetic and copies ran while one was open for 3% of the time, Pallas kernels for 17%

profile of v5, /device:TPU:0, one launch (start us, length us, event | category | flops | bytes accessed | tf_op | source)
XLA Modules:
  0.0 94.1 jit_solution(234176666461290651)
XLA Ops:
  0.6 1.6 %fusion.30 = (f32[1]{0:T(128)}, f32[1]{0:T(128)}, f32[1]{0:T(128)}, f32[1]{0:T(128)}, f32[1]{0:T(128)}, /*index=5*/f32[1]{0:T(128)}, f32[1]{0:T(128)}, f32[1]{0:T(128)}) fusion(f32[8]{0:T(128)} %param.11), kind=kLoop, calls=%fused_computation.111 | loop fusion | bytes 64 | tf_op jit(solution)/shard_map/slice | solution.py:309
  2.3 6.0 %add_bitcast_fusion.mod_ref = f32[2,64,128]{2,1,0:T(8,128)S(1)} fusion(s32[64,2,128]{2,1,0:T(2,128)} %param.10, f32[]{:T(128)} %bitcast.25, f32[]{:T(128)} %bitcast.24, f32[]{:T(128)} %bitcast.23, f32[]{:T(128)} %bitcast.22, f32[]{:T(128)} %bitcast.21, f32[]{:T(128)} %bitcast.20, f32[]{:T(128)} %bitcast.19, f32[]{:T(128)} %bitcast.18), kind=kLoop, calls=%fused_computation.21 | loop fusion | flops 376832 | bytes 131104 | tf_op jit(solution)/shard_map/transpose | solution.py:356
  8.4 1.6 %copy_bitcast_fusion = (f32[4,3,2,64,128]{4,3,2,1,0:T(8,128)S(1)}, f32[4,3,2,64,128]{4,3,2,1,0:T(8,128)S(1)}) fusion(f32[4,3,64,2,128]{4,3,2,1,0:T(2,128)} %param.8, f32[4,3,64,2,128]{4,3,2,1,0:T(2,128)} %param.9), kind=kLoop, calls=%fused_computation.12 | loop fusion | bytes 3145728 | tf_op jit(solution)/shard_map/transpose | solution.py:354
  10.5 14.3 %all-gather.1 = f32[8,2,16128]{2,1,0:T(2,128)S(1)} all-gather(f32[1,2,16128]{2,1,0:T(2,128)S(1)} %maximum_bitcast_fusion.2), channel_id=2, replica_groups=mesh['col'=16,'grp'=8] {'grp'}, dimensions={0}, use_global_device_ids=true | all-gather | bytes 1161216 | tf_op jit(solution)/shard_map/all_gather | solution.py:329
  24.8 1.0 %scatter_custom_fusion = s32[128]{0:T(128)S(1)} fusion(s32[128]{0:T(128)S(1)} %compare_select_fusion.5, s32[128]{0:T(128)S(1)} %iota.34, s32[]{:T(128)} %constant.120.clone.1), kind=kCustom, calls=%fused_computation.101 | custom fusion | bytes 516 | tf_op jit(solution)/shard_map/scatter | solution.py:316
  25.8 1.5 %gather_fusion.1 = s32[128]{0:T(128)S(1)} fusion(s32[2,128]{1,0:T(2,128)S(1)} %copy-done, s32[128]{0:T(128)S(1)} %fusion.19), kind=kCustom, calls=%fused_computation.1 | custom fusion | bytes 2048 | tf_op jit(solution)/shard_map/gather | solution.py:318
  27.3 1.5 %gather_fusion = s32[128]{0:T(128)S(1)} fusion(s32[2,128]{1,0:T(2,128)S(1)} %copy-done, s32[128]{0:T(128)S(1)} %get-tuple-element.16), kind=kCustom, calls=%fused_computation | custom fusion | bytes 2048 | tf_op jit(solution)/shard_map/gather | solution.py:319
  28.9 0.7 gather_fusion.2
  29.5 0.7 gather_fusion.4
  30.2 3.0 %gather_fusion.3 = f32[16,16128]{1,0:T(8,128)} fusion(f32[8,2,16128]{2,1,0:T(2,128)S(1)} %all-gather.1, s32[16]{0:T(128)S(1)} %get-tuple-element.76), kind=kCustom, calls=%fused_computation.3 | custom fusion | bytes 2064512 | tf_op jit(solution)/shard_map/gather | solution.py:335
  33.2 3.0 %gather_fusion.5 = f32[16,16128]{1,0:T(8,128)} fusion(f32[8,2,16128]{2,1,0:T(2,128)S(1)} %all-gather.1, s32[16]{0:T(128)S(1)} %get-tuple-element.77), kind=kCustom, calls=%fused_computation.5 | custom fusion | bytes 2064512 | tf_op jit(solution)/shard_map/gather | solution.py:336
  36.2 1.4 %bitcast_select_fusion.1 = f32[16,1,16128]{2,0,1:T(8,128)S(1)} fusion(f32[16,16128]{1,0:T(8,128)} %gather_fusion.3, pred[16]{0:T(512)(128)(4,1)S(1)} %get-tuple-element.79), kind=kLoop, calls=%fused_computation.9 | loop fusion | flops 258048 | bytes 2064400 | tf_op jit(solution)/shard_map/jit(_where)/select_n | solution.py:338
  38.0 2.9 %copy.44 = f32[16,2,16128]{2,1,0:T(2,128)} copy(f32[16,2,16128]{2,0,1:T(8,128)S(1)} %pad_maximum_fusion) | data formatting | bytes 4128768 | tf_op jit(solution)/shard_map/stack | solution.py:340
  40.9 7.9 %all-to-all-start = ((f32[16,2,16128]{2,1,0:T(2,128)}), f32[16,2,16128]{2,1,0:T(2,128)}, u32[]{:S(2)}, u32[]{:S(2)}) async-start(f32[16,2,16128]{2,1,0:T(2,128)} %copy.44), calls=%async_computation | async-start | bytes 4128768 | tf_op jit(solution)/shard_map/all_to_all | solution.py:341
  51.4 0.6 dynamic_slice.14
  58.1 16.3 %shard_map.96 = (f32[4,3,2,64,128]{4,3,2,1,0:T(8,128)S(1)}, f32[4,3,2,64,128]{4,3,2,1,0:T(8,128)S(1)}) custom-call(f32[3]{0:T(128)S(1)} %pad_maximum_fusion.2.scal_ref, f32[2,64,128]{2,1,0:T(8,128)S(1)} %broadcast_in_dim.123.mask_ref, f32[4,3,2,64,128]{4,3,2,1,0:T(8,128)S(1)} %get-tuple-element.75.md_ref, ...), custom_call_target="tpu_custom_call" | custom-call | flops 306708480 | bytes 3932160 | tf_op jit(solution)/shard_map/pallas_call | solution.py:288
  74.4 0.9 slice.301
  75.3 0.9 slice.296
  76.4 2.9 %all-to-all-done = f32[16,2,16128]{2,1,0:T(2,128)} async-done(((f32[16,2,16128]{2,1,0:T(2,128)}), f32[16,2,16128]{2,1,0:T(2,128)}, u32[]{:S(2)}, u32[]{:S(2)}) %all-to-all-start) | async-done | bytes 2064416 | tf_op jit(solution)/shard_map/all_to_all | solution.py:341
  79.3 1.1 %broadcast_select_fusion = (f32[1,1,16128]{2,1,0:T(1,128)S(1)}, f32[1,1,16128]{2,1,0:T(1,128)S(1)}) fusion(pred[]{:T(512)S(6)} %ne.108, f32[16,2,16128]{2,1,0:T(2,128)} %all-to-all-done, s32[]{:T(128)S(6)} %select_n.253, s32[]{:T(128)S(6)} %select_n.249, pred[]{:T(512)S(6)} %ne.107), kind=kLoop, calls=%fused_computation.15 | loop fusion | flops 32256 | bytes 258058 | tf_op jit(solution)/shard_map/jit(_where)/select_n | solution.py:346
  81.0 8.7 %shard_map.95 = (f32[4,3,2,32,128]{4,3,2,1,0:T(8,128)S(1)}, f32[4,3,2,32,128]{4,3,2,1,0:T(8,128)S(1)}) custom-call(f32[3]{0:T(128)S(1)} %pad_maximum_fusion.2.scal_ref, f32[2,32,128]{2,1,0:T(8,128)S(1)} %pad_maximum_fusion.1.mask_ref, f32[4,3,2,32,128]{4,3,2,1,0:T(8,128)S(1)} %concatenate.43.md_ref, f32[4,3,2,32,128]{4,3,2,1,0:T(8,128)S(1)} %concatenate.44.ld_ref, ...), custom_call_target="tpu_custom_call" | custom-call | flops 153354240 | bytes 1966080 | tf_op jit(solution)/shard_map/pallas_call | solution.py:288
  89.8 1.2 %maximum_bitcast_fusion.1 = f32[4,3,64,2,128]{4,2,3,1,0:T(8,128)S(1)} fusion(f32[4,3,2,8,128]{4,3,2,1,0:T(8,128)S(1)} %get-tuple-element.62, f32[4,3,2,48,128]{4,3,2,1,0:T(8,128)} %slice.301, f32[4,3,2,8,128]{4,3,2,1,0:T(8,128)S(1)} %get-tuple-element.63), kind=kLoop, calls=%fused_computation.11 | loop fusion | flops 393216 | bytes 1572864 | tf_op jit(solution)/shard_map/transpose | solution.py:455
  91.0 1.5 %copy.46 = f32[4,3,64,2,128]{4,3,2,1,0:T(2,128)} copy(f32[4,3,64,2,128]{4,2,3,1,0:T(8,128)S(1)} %maximum_bitcast_fusion.1) | data formatting | bytes 1572864
  92.6 1.5 %copy.45 = f32[4,3,64,2,128]{4,3,2,1,0:T(2,128)} copy(f32[4,3,64,2,128]{4,2,3,1,0:T(8,128)S(1)} %maximum_bitcast_fusion) | data formatting | bytes 1572864
  (66 shorter events, 2.5 us)
Async XLA Ops:
  0.6 25.2 %copy-start = (s32[2,128]{1,0:T(2,128)S(1)}, s32[2,128]{1,0:T(2,128)}, u32[]{:S(2)}) copy-start(s32[2,128]{1,0:T(2,128)} %param.13) | copy-start | bytes 3076
  8.3 16.4 %copy-start.3 = (s32[128]{0:T(128)S(1)}, s32[128]{0:T(128)}, u32[]{:S(2)}) copy-start(s32[128]{0:T(128)} %param.12) | copy-start | bytes 1540
  36.2 1.5 %copy-start.1 = (f32[16,16128]{1,0:T(8,128)S(1)}, f32[16,16128]{1,0:T(8,128)}, u32[]{:S(2)}) copy-start(f32[16,16128]{1,0:T(8,128)} %gather_fusion.5) | copy-start | bytes 3096580
  40.9 38.4 %all-to-all-start = ((f32[16,2,16128]{2,1,0:T(2,128)}), f32[16,2,16128]{2,1,0:T(2,128)}, u32[]{:S(2)}, u32[]{:S(2)}) async-start(f32[16,2,16128]{2,1,0:T(2,128)} %copy.44), calls=%async_computation | async-start | bytes 4128768 | tf_op jit(solution)/shard_map/all_to_all | solution.py:341
  89.7 2.8 %copy-start.2 = (f32[4,3,2,48,128]{4,3,2,1,0:T(8,128)S(1)}, f32[4,3,2,48,128]{4,3,2,1,0:T(8,128)}, u32[]{:S(2)}) copy-start(f32[4,3,2,48,128]{4,3,2,1,0:T(8,128)} %slice.296) | copy-start | bytes 1769476

commit v6 on v5

--- a/solution.py
+++ b/solution.py
@@ -313,10 +313,11 @@
 def neighbour_devices(part_device, partners):
     count = part_device.shape[0]
     ids = jnp.arange(count, dtype=jnp.int32)
-    place = jnp.zeros((count,), jnp.int32).at[part_device].set(ids)
-    parity = place % 2
-    up_dev = partners[parity, ids]
-    low_dev = partners[1 - parity, ids]
+    hit = part_device[None, :] == ids[:, None]
+    place = jnp.sum(jnp.where(hit, ids[None, :], 0), axis=1)
+    upper = place % 2 == 0
+    up_dev = jnp.where(upper, partners[0], partners[1])
+    low_dev = jnp.where(upper, partners[1], partners[0])
     return up_dev, low_dev
 
 
@@ -327,22 +328,22 @@
     cols = up_dev.shape[0] // GROUP
     pack = jnp.stack([first, last], axis=0)[None]
     held = lax.all_gather(pack, "grp", axis=0, tiled=True)
-    targets = jnp.arange(cols, dtype=jnp.int32) * GROUP + grp
-    t_up = up_dev[targets]
-    t_low = low_dev[targets]
-    up_here = (t_up // GROUP) == col
-    low_here = (t_low // GROUP) == col
-    from_up = held[t_up % GROUP, 0]
-    from_low = held[t_low % GROUP, 1]
-    shape = (cols,) + (1,) * (from_up.ndim - 1)
-    from_up = jnp.where(up_here.reshape(shape), from_up, jnp.float32(0.0))
-    from_low = jnp.where(low_here.reshape(shape), from_low, jnp.float32(0.0))
+    pick = (jnp.arange(GROUP, dtype=jnp.int32) == grp)[None, :]
+    t_up = jnp.sum(jnp.where(pick, up_dev.reshape(cols, GROUP), 0), axis=1)
+    t_low = jnp.sum(jnp.where(pick, low_dev.reshape(cols, GROUP), 0), axis=1)
+    up_at = jnp.where(t_up // GROUP == col, t_up % GROUP, -1)[:, None]
+    low_at = jnp.where(t_low // GROUP == col, t_low % GROUP, -1)[:, None]
+    from_up = jnp.zeros((cols, first.shape[0]), jnp.float32)
+    from_low = jnp.zeros((cols, first.shape[0]), jnp.float32)
+    for k in range(GROUP):
+        from_up = jnp.where(up_at == k, held[k, 0][None, :], from_up)
+        from_low = jnp.where(low_at == k, held[k, 1][None, :], from_low)
     slots = jnp.stack([from_up, from_low], axis=1)
     got = lax.all_to_all(slots, "col", 0, 0, tiled=True)
     my_up = up_dev[me]
     my_low = low_dev[me]
-    above = got[my_up // GROUP, 0]
-    below = got[my_low // GROUP, 1]
+    above = lax.dynamic_index_in_dim(got, my_up // GROUP, axis=0, keepdims=False)[0]
+    below = lax.dynamic_index_in_dim(got, my_low // GROUP, axis=0, keepdims=False)[1]
     above = jnp.where(my_up != me, above, jnp.float32(0.0))
     below = jnp.where(my_low != me, below, jnp.float32(0.0))
     return below, above
@@ -353,7 +354,7 @@
     samples, _, depth, rows_y, width = loads.shape
     loads = jnp.transpose(loads, (0, 1, 3, 2, 4))
     modal_disp = jnp.transpose(modal_disp, (0, 1, 3, 2, 4))
-    modulus = jnp.transpose(lookup_modulus(material, moduli), (1, 0, 2))
+    modulus = lookup_modulus(jnp.transpose(material, (1, 0, 2)), moduli)
     plane = (samples, 3, rows_y, width)
     plane_size = samples * 3 * rows_y * width
     mod_size = rows_y * width

time: 94.6 us -> 98.5 us (1.041)
  other arithmetic: 10.6 us -> 25.9 us
  local copies, waits for them, and re-layouts: 24.3 us -> 13 us
    select_n x4, other arithmetic: 1.59 us -> 13.7 us  [the longest x1 6.94 us: exchange(): from_up = jnp.where(up_at == k, held[k, 0][None, :], from_up)]
    gather x6 -> x0, local copies, waits for them, and re-layouts: 10.3 us -> none  [the longest x1 2.99 us: exchange(): from_low = held[t_low % GROUP, 1]]
    transpose x1 -> x0, other arithmetic: 6.04 us -> none  [on_device(): modulus = jnp.transpose(lookup_modulus(material, moduli), (1, 0, 2))]
    add x0 -> x1, other arithmetic: none -> 5.92 us  [lookup_modulus(): modulus + jnp.where(material == index, moduli[index], jnp.float32(0.0))]
    another operation x1, other arithmetic: 0.14 us -> 3.15 us  [exchange(): slots = jnp.stack([from_up, from_low], axis=1)]
    another operation x6 -> x5, local copies, waits for them, and re-layouts: 2.91 us -> 0.03 us  [the longest x1 2.88 us: exchange(): slots = jnp.stack([from_up, from_low], axis=1)]
    slice x0 -> x2, local copies, waits for them, and re-layouts: none -> 2.69 us  [the longest x1 2.67 us: exchange(): from_up = jnp.where(up_at == k, held[k, 0][None, :], from_up)]
    unnamed x24 -> x22, local copies, waits for them, and re-layouts: 3.15 us -> 3.07 us
where the time goes in v6:
time: 98.5 us; the launch traced here: 98 us
  other arithmetic  25.9 us (26%)
  Pallas kernels  25 us (25%)
  blocking collectives  14.3 us (15%)
  local copies, waits for them, and re-layouts  13 us (13%)
  between operations  9.06 us (9%)
  starting transfers between devices  7.93 us (8%)
  waiting for transfers between devices  2.87 us (3%)
    pallas_call x2, Pallas kernels, run_chain(): pl.pallas_call(chain_kernel, out_shape=(field, field), in_specs=[smem, vm...  25 us
    all_gather x1, blocking collectives, exchange(): held = lax.all_gather(pack, 'grp', axis=0, tiled=True)  14.3 us
    all_to_all x1, starting transfers between devices, exchange(): got = lax.all_to_all(slots, 'col', 0, 0, tiled=True)  7.93 us
    select_n x1, other arithmetic, exchange(): from_up = jnp.where(up_at == k, held[k, 0][None, :], from_up)  6.94 us
    select_n x1, other arithmetic, exchange(): from_low = jnp.where(low_at == k, held[k, 1][None, :], from_low)  6.76 us
    add x1, other arithmetic, lookup_modulus(): modulus + jnp.where(material == index, moduli[index], jnp.float32(0.0))  5.92 us
    another operation x1, other arithmetic, exchange(): slots = jnp.stack([from_up, from_low], axis=1)  3.15 us
    unnamed x22, local copies, waits for them, and re-layouts  3.07 us
  transfers between devices with their start and end apart: 1, of which 1 were waited for; matrix products, arithmetic and copies ran while one was open for 3% of the time, Pallas kernels for 17%

profile of v6, /device:TPU:0, one launch (start us, length us, event | category | flops | bytes accessed | tf_op | source)
XLA Modules:
  0.0 98.0 jit_solution(10952795260605509417)
XLA Ops:
  0.6 1.6 %fusion.11 = (f32[1]{0:T(128)}, f32[1]{0:T(128)}, f32[1]{0:T(128)}, f32[1]{0:T(128)}, f32[1]{0:T(128)}, /*index=5*/f32[1]{0:T(128)}, f32[1]{0:T(128)}, f32[1]{0:T(128)}) fusion(f32[8]{0:T(128)} %param.11), kind=kLoop, calls=%fused_computation.132 | loop fusion | bytes 64 | tf_op jit(solution)/shard_map/slice | solution.py:309
  2.3 5.9 %add_bitcast_fusion.mod_ref = f32[2,64,128]{2,1,0:T(8,128)S(1)} fusion(s32[64,2,128]{2,1,0:T(2,128)} %param.10, f32[]{:T(128)} %bitcast.22, f32[]{:T(128)} %bitcast.21, f32[]{:T(128)} %bitcast.20, f32[]{:T(128)} %bitcast.19, f32[]{:T(128)} %bitcast.18, f32[]{:T(128)} %bitcast.17, f32[]{:T(128)} %bitcast.16, f32[]{:T(128)} %bitcast.15), kind=kLoop, calls=%fused_computation.28 | loop fusion | flops 376832 | bytes 131104 | tf_op jit(solution)/shard_map/add | solution.py:309
  8.2 1.6 %copy_bitcast_fusion = (f32[4,3,2,64,128]{4,3,2,1,0:T(8,128)S(1)}, f32[4,3,2,64,128]{4,3,2,1,0:T(8,128)S(1)}) fusion(f32[4,3,64,2,128]{4,3,2,1,0:T(2,128)} %param.8, f32[4,3,64,2,128]{4,3,2,1,0:T(2,128)} %param.9), kind=kLoop, calls=%fused_computation.19 | loop fusion | bytes 3145728 | tf_op jit(solution)/shard_map/transpose | solution.py:355
  10.2 0.1 maximum_bitcast_fusion.2
  10.3 14.3 %all-gather.1 = f32[8,2,16128]{2,1,0:T(2,128)S(1)} all-gather(f32[1,2,16128]{2,1,0:T(2,128)S(1)} %maximum_bitcast_fusion.2), channel_id=2, replica_groups=mesh['col'=16,'grp'=8] {'grp'}, dimensions={0}, use_global_device_ids=true | all-gather | bytes 1161216 | tf_op jit(solution)/shard_map/all_gather | solution.py:330
  24.6 2.7 %slice_reduce_fusion.15 = (f32[16128]{0:T(1024)S(1)}, f32[16128]{0:T(1024)S(1)}, f32[16128]{0:T(1024)S(1)}, f32[16128]{0:T(1024)S(1)}, f32[16128]{0:T(1024)S(1)}...) fusion(f32[8,2,16128]{2,1,0:T(2,128)S(1)} %all-gather.1), kind=kLoop, calls=%fused_computation.46 | loop fusion | bytes 2064384 | tf_op jit(solution)/shard_map/slice | solution.py:339
  27.7 0.1 select_reduce_fusion.2
  27.9 6.9 %broadcast_select_fusion.13 = f32[16,1,16128]{2,1,0:T(1,128)S(1)} fusion(pred[16]{0:T(512)(128)(4,1)S(1)} %get-tuple-element.116, pred[16]{0:T(512)(128)(4,1)S(1)} %get-tuple-element.117, pred[16]{0:T(512)(128)(4,1)S(1)} %get-tuple-element.121, pred[16]{0:T(512)(128)(4,1)S(1)} %get-tuple-element.120, pred[16]{0:T(512)(128)(4,1)S(1)} %get-tuple-element.119, ...), kind=kLoop, calls=%fused_computation.14 | loop fusion | flops 2064384 | bytes 1548416 | tf_op jit(solution)/shard_map/jit(_where)/select_n | solution.py:339
  34.9 6.8 %broadcast_select_fusion.6 = f32[16,1,16128]{2,1,0:T(1,128)S(1)} fusion(pred[16]{0:T(512)(128)(4,1)S(1)} %get-tuple-element.105, pred[16]{0:T(512)(128)(4,1)S(1)} %get-tuple-element.104, pred[16]{0:T(512)(128)(4,1)S(1)} %get-tuple-element.100, pred[16]{0:T(512)(128)(4,1)S(1)} %get-tuple-element.101, pred[16]{0:T(512)(128)(4,1)S(1)} %get-tuple-element.102, ...), kind=kLoop, calls=%fused_computation.7 | loop fusion | flops 2064384 | bytes 1548416 | tf_op jit(solution)/shard_map/jit(_where)/select_n | solution.py:340
  41.6 3.1 %pad_maximum_fusion = f32[16,2,16128]{2,1,0:T(2,128)} fusion(f32[16,1,16128]{2,1,0:T(1,128)S(1)} %broadcast_select_fusion.6, f32[16,1,16128]{2,1,0:T(1,128)S(1)} %broadcast_select_fusion.13), kind=kLoop, calls=%fused_computation | loop fusion | flops 516096 | bytes 4128768 | tf_op jit(solution)/shard_map/stack | solution.py:341
  44.8 7.9 %all-to-all-start = ((f32[16,2,16128]{2,1,0:T(2,128)}), f32[16,2,16128]{2,1,0:T(2,128)}, u32[]{:S(2)}, u32[]{:S(2)}) async-start(f32[16,2,16128]{2,1,0:T(2,128)} %pad_maximum_fusion), calls=%async_computation | async-start | bytes 4128768 | tf_op jit(solution)/shard_map/all_to_all | solution.py:342
  52.8 0.6 dynamic_slice.16
  55.3 0.6 dynamic_slice.15
  62.0 16.3 %shard_map.96 = (f32[4,3,2,64,128]{4,3,2,1,0:T(8,128)S(1)}, f32[4,3,2,64,128]{4,3,2,1,0:T(8,128)S(1)}) custom-call(f32[3]{0:T(128)S(1)} %pad_maximum_fusion.2.scal_ref, f32[2,64,128]{2,1,0:T(8,128)S(1)} %broadcast_in_dim.368.mask_ref, f32[4,3,2,64,128]{4,3,2,1,0:T(8,128)S(1)} %get-tuple-element.115.md_ref, ...), custom_call_target="tpu_custom_call" | custom-call | flops 306708480 | bytes 3932160 | tf_op jit(solution)/shard_map/pallas_call | solution.py:288
  78.4 0.9 slice.385
  79.2 0.9 slice.380
  80.4 2.9 %all-to-all-done = f32[16,2,16128]{2,1,0:T(2,128)} async-done(((f32[16,2,16128]{2,1,0:T(2,128)}), f32[16,2,16128]{2,1,0:T(2,128)}, u32[]{:S(2)}, u32[]{:S(2)}) %all-to-all-start) | async-done | bytes 2064416 | tf_op jit(solution)/shard_map/all_to_all | solution.py:342
  83.2 1.1 %broadcast_select_fusion.16 = (f32[1,1,16128]{2,1,0:T(1,128)S(1)}, f32[1,1,16128]{2,1,0:T(1,128)S(1)}) fusion(pred[]{:T(512)S(6)} %ne.282, f32[16,2,16128]{2,1,0:T(2,128)} %all-to-all-done, s32[]{:T(128)S(6)} %select_n.580, s32[]{:T(128)S(6)} %select_n.576, s32[]{:T(128)S(6)} %add.232, pred[]{:T(512)S(6)} %ne.281), kind=kLoop, calls=%fused_computation.22 | loop fusion | flops 32256 | bytes 258062 | tf_op jit(solution)/shard_map/jit(_where)/select_n | solution.py:347
  84.4 0.2 concatenate.28.ld_ref
  84.6 0.2 concatenate.27.md_ref
  84.9 8.7 %shard_map.95 = (f32[4,3,2,32,128]{4,3,2,1,0:T(8,128)S(1)}, f32[4,3,2,32,128]{4,3,2,1,0:T(8,128)S(1)}) custom-call(f32[3]{0:T(128)S(1)} %pad_maximum_fusion.2.scal_ref, f32[2,32,128]{2,1,0:T(8,128)S(1)} %pad_maximum_fusion.1.mask_ref, f32[4,3,2,32,128]{4,3,2,1,0:T(8,128)S(1)} %concatenate.27.md_ref, f32[4,3,2,32,128]{4,3,2,1,0:T(8,128)S(1)} %concatenate.28.ld_ref, ...), custom_call_target="tpu_custom_call" | custom-call | flops 153354240 | bytes 1966080 | tf_op jit(solution)/shard_map/pallas_call | solution.py:288
  93.7 1.2 %maximum_bitcast_fusion.1 = f32[4,3,64,2,128]{4,2,3,1,0:T(8,128)S(1)} fusion(f32[4,3,2,8,128]{4,3,2,1,0:T(8,128)S(1)} %get-tuple-element.88, f32[4,3,2,48,128]{4,3,2,1,0:T(8,128)} %slice.385, f32[4,3,2,8,128]{4,3,2,1,0:T(8,128)S(1)} %get-tuple-element.89), kind=kLoop, calls=%fused_computation.18 | loop fusion | flops 393216 | bytes 1572864 | tf_op jit(solution)/shard_map/transpose | solution.py:456
  94.9 1.5 %copy.57 = f32[4,3,64,2,128]{4,3,2,1,0:T(2,128)} copy(f32[4,3,64,2,128]{4,2,3,1,0:T(8,128)S(1)} %maximum_bitcast_fusion.1) | data formatting | bytes 1572864
  96.5 1.5 %copy.56 = f32[4,3,64,2,128]{4,3,2,1,0:T(2,128)} copy(f32[4,3,64,2,128]{4,2,3,1,0:T(8,128)S(1)} %maximum_bitcast_fusion) | data formatting | bytes 1572864
  (61 shorter events, 1.4 us)
Async XLA Ops:
  9.8 17.5 %copy-start.1 = (s32[2,128]{1,0:T(2,128)S(1)}, s32[2,128]{1,0:T(2,128)}, u32[]{:S(2)}) copy-start(s32[2,128]{1,0:T(2,128)} %param.13) | copy-start | bytes 3076
  9.9 17.6 %copy-start.2 = (s32[128]{0:T(128)S(1)}, s32[128]{0:T(128)}, u32[]{:S(2)}) copy-start(s32[128]{0:T(128)} %param.12) | copy-start | bytes 1540
  44.8 38.4 %all-to-all-start = ((f32[16,2,16128]{2,1,0:T(2,128)}), f32[16,2,16128]{2,1,0:T(2,128)}, u32[]{:S(2)}, u32[]{:S(2)}) async-start(f32[16,2,16128]{2,1,0:T(2,128)} %pad_maximum_fusion), calls=%async_computation | async-start | bytes 4128768 | tf_op jit(solution)/shard_map/all_to_all | solution.py:342
  93.6 2.8 %copy-start = (f32[4,3,2,48,128]{4,3,2,1,0:T(8,128)S(1)}, f32[4,3,2,48,128]{4,3,2,1,0:T(8,128)}, u32[]{:S(2)}) copy-start(f32[4,3,2,48,128]{4,3,2,1,0:T(8,128)} %slice.380) | copy-start | bytes 1769476

commit v7 on v6

--- a/solution.py
+++ b/solution.py
@@ -333,11 +333,13 @@
     t_low = jnp.sum(jnp.where(pick, low_dev.reshape(cols, GROUP), 0), axis=1)
     up_at = jnp.where(t_up // GROUP == col, t_up % GROUP, -1)[:, None]
     low_at = jnp.where(t_low // GROUP == col, t_low % GROUP, -1)[:, None]
-    from_up = jnp.zeros((cols, first.shape[0]), jnp.float32)
-    from_low = jnp.zeros((cols, first.shape[0]), jnp.float32)
+    up_at = up_at[:, :, None]
+    low_at = low_at[:, :, None]
+    from_up = jnp.zeros((cols,) + first.shape, jnp.float32)
+    from_low = jnp.zeros((cols,) + first.shape, jnp.float32)
     for k in range(GROUP):
-        from_up = jnp.where(up_at == k, held[k, 0][None, :], from_up)
-        from_low = jnp.where(low_at == k, held[k, 1][None, :], from_low)
+        from_up = jnp.where(up_at == k, held[k, 0][None], from_up)
+        from_low = jnp.where(low_at == k, held[k, 1][None], from_low)
     slots = jnp.stack([from_up, from_low], axis=1)
     got = lax.all_to_all(slots, "col", 0, 0, tiled=True)
     my_up = up_dev[me]
@@ -354,7 +356,8 @@
     samples, _, depth, rows_y, width = loads.shape
     loads = jnp.transpose(loads, (0, 1, 3, 2, 4))
     modal_disp = jnp.transpose(modal_disp, (0, 1, 3, 2, 4))
-    modulus = lookup_modulus(jnp.transpose(material, (1, 0, 2)), moduli)
+    flat_mod = lookup_modulus(material.reshape(depth, rows_y * width), moduli)
+    modulus = jnp.stack([flat_mod[:, y * width : (y + 1) * width] for y in range(rows_y)], axis=0)
     plane = (samples, 3, rows_y, width)
     plane_size = samples * 3 * rows_y * width
     mod_size = rows_y * width
@@ -363,11 +366,14 @@
         parts = [modal_disp[:, :, :, r].reshape(-1) for r in md_rows]
         parts += [loads[:, :, :, r].reshape(-1) for r in load_rows]
         parts += [modulus[:, r].reshape(-1) for r in md_rows]
-        return jnp.concatenate(parts)
+        flat = jnp.concatenate(parts)
+        return flat.reshape(flat.shape[0] // width, width)
 
     first = pack((0, 1, 2), (0, 1))
     last = pack((depth - 3, depth - 2, depth - 1), (depth - 2, depth - 1))
     below, above = exchange(first, last, up_dev, low_dev)
+    below = below.reshape(-1)
+    above = above.reshape(-1)
 
     def planes_of(got, count, start, size, shape):
         return [got[start + i * size : start + (i + 1) * size].reshape(shape) for i in range(count)]

time: 98.5 us -> 95.7 us (0.972)
  local copies, waits for them, and re-layouts: 13 us -> 11.4 us
  other arithmetic: 25.9 us -> 24.6 us
    slice x2 -> x1, local copies, waits for them, and re-layouts: 2.68 us -> 1.08 us  [exchange(): lax.dynamic_index_in_dim(got, my_up // GROUP, axis=0, keepdims=False)[0]]
    select_n x1, other arithmetic: 1.1 us -> 0.01 us  [exchange(): above = jnp.where(my_up != me, above, jnp.float32(0.0))]
    select_n x2 -> x3, other arithmetic: 13.7 us -> 13.5 us  [the longest x1 6.76 us: exchange(): from_up = jnp.where(up_at == k, held[k, 0][None], from_up)]
    unnamed x22 -> x23, local copies, waits for them, and re-layouts: 3.07 us -> 3.08 us
where the time goes in v7:
time: 95.7 us; the launch traced here: 95.2 us
  Pallas kernels  25 us (26%)
  other arithmetic  24.6 us (26%)
  blocking collectives  14.3 us (15%)
  local copies, waits for them, and re-layouts  11.4 us (12%)
  between operations  9.09 us (9%)
  starting transfers between devices  7.93 us (8%)
  waiting for transfers between devices  2.86 us (3%)
    pallas_call x2, Pallas kernels, run_chain(): pl.pallas_call(chain_kernel, out_shape=(field, field), in_specs=[smem, vm...  25 us
    all_gather x1, blocking collectives, exchange(): held = lax.all_gather(pack, 'grp', axis=0, tiled=True)  14.3 us
    all_to_all x1, starting transfers between devices, exchange(): got = lax.all_to_all(slots, 'col', 0, 0, tiled=True)  7.93 us
    select_n x1, other arithmetic, exchange(): from_up = jnp.where(up_at == k, held[k, 0][None], from_up)  6.76 us
    select_n x1, other arithmetic, exchange(): from_low = jnp.where(low_at == k, held[k, 1][None], from_low)  6.76 us
    add x1, other arithmetic, lookup_modulus(): modulus + jnp.where(material == index, moduli[index], jnp.float32(0.0))  6.06 us
    another operation x1, other arithmetic, exchange(): slots = jnp.stack([from_up, from_low], axis=1)  3.16 us
    unnamed x23, local copies, waits for them, and re-layouts  3.08 us
  transfers between devices with their start and end apart: 1, of which 1 were waited for; matrix products, arithmetic and copies ran while one was open for 3% of the time, Pallas kernels for 17%

profile of v7, /device:TPU:0, one launch (start us, length us, event | category | flops | bytes accessed | tf_op | source)
XLA Modules:
  0.0 95.2 jit_solution(13371669887418661555)
XLA Ops:
  0.6 1.6 %fusion.26 = (f32[1]{0:T(128)}, f32[1]{0:T(128)}, f32[1]{0:T(128)}, f32[1]{0:T(128)}, f32[1]{0:T(128)}, /*index=5*/f32[1]{0:T(128)}, f32[1]{0:T(128)}, f32[1]{0:T(128)}) fusion(f32[8]{0:T(128)} %param.11), kind=kLoop, calls=%fused_computation.170 | loop fusion | bytes 64 | tf_op jit(solution)/shard_map/slice | solution.py:309
  2.3 6.1 %fusion.6 = f32[64,2,128]{2,1,0:T(2,128)S(1)} fusion(s32[64,2,128]{2,1,0:T(2,128)} %param.10, f32[]{:T(128)} %bitcast.22, f32[]{:T(128)} %bitcast.21, f32[]{:T(128)} %bitcast.20, f32[]{:T(128)} %bitcast.19, f32[]{:T(128)} %bitcast.18, f32[]{:T(128)} %bitcast.17, f32[]{:T(128)} %bitcast.16, f32[]{:T(128)} %bitcast.15), kind=kLoop, calls=%fused_computation.57 | loop fusion | flops 376832 | bytes 131104 | tf_op jit(solution)/shard_map/add | solution.py:309
  8.4 1.6 %copy_bitcast_fusion = (f32[4,3,2,64,128]{4,3,2,1,0:T(8,128)S(1)}, f32[4,3,2,64,128]{4,3,2,1,0:T(8,128)S(1)}) fusion(f32[4,3,64,2,128]{4,3,2,1,0:T(2,128)} %param.8, f32[4,3,64,2,128]{4,3,2,1,0:T(2,128)} %param.9), kind=kLoop, calls=%fused_computation.19 | loop fusion | bytes 3145728 | tf_op jit(solution)/shard_map/transpose | solution.py:357
  10.3 14.3 %all-gather = f32[16,126,128]{2,1,0:T(8,128)S(1)} all-gather(f32[2,126,128]{2,1,0:T(8,128)S(1)} %pad_maximum_fusion.2), channel_id=2, replica_groups=mesh['col'=16,'grp'=8] {'grp'}, dimensions={0}, use_global_device_ids=true | all-gather | bytes 1161216 | tf_op jit(solution)/shard_map/all_gather | solution.py:330
  24.9 0.1 select_reduce_fusion
  25.1 0.1 select_reduce_fusion.2
  25.3 6.8 %broadcast_select_fusion.13 = f32[16,1,126,128]{3,1,2,0:T(1,128)S(1)} fusion(pred[16]{0:T(512)(128)(4,1)S(1)} %get-tuple-element.118, pred[16]{0:T(512)(128)(4,1)S(1)} %get-tuple-element.119, pred[16]{0:T(512)(128)(4,1)S(1)} %get-tuple-element.123, pred[16]{0:T(512)(128)(4,1)S(1)} %get-tuple-element.122, pred[16]{0:T(512)(128)(4,1)S(1)} %get-tuple-element.121, ...), kind=kLoop, calls=%fused_computation.14 | loop fusion | flops 2064384 | bytes 1548416 | tf_op jit(solution)/shard_map/jit(_where)/select_n | solution.py:341
  32.0 6.8 %broadcast_select_fusion.6 = f32[16,1,126,128]{3,1,2,0:T(1,128)S(1)} fusion(pred[16]{0:T(512)(128)(4,1)S(1)} %get-tuple-element.107, pred[16]{0:T(512)(128)(4,1)S(1)} %get-tuple-element.106, pred[16]{0:T(512)(128)(4,1)S(1)} %get-tuple-element.102, pred[16]{0:T(512)(128)(4,1)S(1)} %get-tuple-element.103, pred[16]{0:T(512)(128)(4,1)S(1)} %get-tuple-element.104, ...), kind=kLoop, calls=%fused_computation.7 | loop fusion | flops 2064384 | bytes 1548416 | tf_op jit(solution)/shard_map/jit(_where)/select_n | solution.py:342
  38.8 3.2 %pad_maximum_fusion = f32[16,2,126,128]{3,1,2,0:T(2,128)} fusion(f32[16,1,126,128]{3,1,2,0:T(1,128)S(1)} %broadcast_select_fusion.6, f32[16,1,126,128]{3,1,2,0:T(1,128)S(1)} %broadcast_select_fusion.13), kind=kLoop, calls=%fused_computation | loop fusion | flops 516096 | bytes 4128768 | tf_op jit(solution)/shard_map/stack | solution.py:343
  42.0 7.9 %all-to-all-start = ((f32[16,2,126,128]{3,1,2,0:T(2,128)}), f32[16,2,126,128]{3,1,2,0:T(2,128)}, u32[]{:S(2)}, u32[]{:S(2)}) async-start(f32[16,2,126,128]{3,1,2,0:T(2,128)} %pad_maximum_fusion), calls=%async_computation | async-start | bytes 4128768 | tf_op jit(solution)/shard_map/all_to_all | solution.py:344
  50.0 0.6 dynamic_slice.16
  52.5 0.6 dynamic_slice.15
  59.2 16.3 %shard_map.96 = (f32[4,3,2,64,128]{4,3,2,1,0:T(8,128)S(1)}, f32[4,3,2,64,128]{4,3,2,1,0:T(8,128)S(1)}) custom-call(f32[3]{0:T(128)S(1)} %pad_maximum_fusion.4.scal_ref, f32[2,64,128]{2,1,0:T(8,128)S(1)} %broadcast_in_dim.366.mask_ref, f32[4,3,2,64,128]{4,3,2,1,0:T(8,128)S(1)} %get-tuple-element.117.md_ref, ...), custom_call_target="tpu_custom_call" | custom-call | flops 306708480 | bytes 3932160 | tf_op jit(solution)/shard_map/pallas_call | solution.py:288
  75.5 0.9 slice.345
  76.4 0.9 slice.340
  77.6 2.9 %all-to-all-done = f32[16,2,126,128]{3,1,2,0:T(2,128)} async-done(((f32[16,2,126,128]{3,1,2,0:T(2,128)}), f32[16,2,126,128]{3,1,2,0:T(2,128)}, u32[]{:S(2)}, u32[]{:S(2)}) %all-to-all-start) | async-done | bytes 2064416 | tf_op jit(solution)/shard_map/all_to_all | solution.py:344
  80.4 1.1 %constant_dynamic-slice_fusion = (f32[1,1,126,128]{3,1,2,0:T(1,128)S(1)}, f32[1,1,126,128]{3,1,2,0:T(1,128)S(1)}) fusion(f32[16,2,126,128]{3,1,2,0:T(2,128)} %all-to-all-done, s32[]{:T(128)S(6)} %select_n.538, s32[]{:T(128)S(6)} %select_n.534, s32[]{:T(128)S(6)} %add.216), kind=kLoop, calls=%fused_computation.139 | loop fusion | bytes 258060 | tf_op jit(solution)/shard_map/slice | solution.py:347
  81.6 0.2 concatenate.28.ld_ref
  81.8 0.2 concatenate.27.md_ref
  82.1 8.7 %shard_map.95 = (f32[4,3,2,32,128]{4,3,2,1,0:T(8,128)S(1)}, f32[4,3,2,32,128]{4,3,2,1,0:T(8,128)S(1)}) custom-call(f32[3]{0:T(128)S(1)} %pad_maximum_fusion.4.scal_ref, f32[2,32,128]{2,1,0:T(8,128)S(1)} %pad_maximum_fusion.3.mask_ref, f32[4,3,2,32,128]{4,3,2,1,0:T(8,128)S(1)} %concatenate.27.md_ref, f32[4,3,2,32,128]{4,3,2,1,0:T(8,128)S(1)} %concatenate.28.ld_ref, ...), custom_call_target="tpu_custom_call" | custom-call | flops 153354240 | bytes 1966080 | tf_op jit(solution)/shard_map/pallas_call | solution.py:288
  90.8 0.1 slice_select_fusion.3
  90.9 1.2 %maximum_bitcast_fusion.1 = f32[4,3,64,2,128]{4,2,3,1,0:T(8,128)S(1)} fusion(f32[4,3,2,8,128]{4,3,2,1,0:T(8,128)S(1)} %get-tuple-element.90, f32[4,3,2,48,128]{4,3,2,1,0:T(8,128)} %slice.345, f32[4,3,2,8,128]{4,3,2,1,0:T(8,128)S(1)} %get-tuple-element.91), kind=kLoop, calls=%fused_computation.18 | loop fusion | flops 393216 | bytes 1572864 | tf_op jit(solution)/shard_map/transpose | solution.py:462
  92.1 1.5 %copy.89 = f32[4,3,64,2,128]{4,3,2,1,0:T(2,128)} copy(f32[4,3,64,2,128]{4,2,3,1,0:T(8,128)S(1)} %maximum_bitcast_fusion.1) | data formatting | bytes 1572864
  93.7 1.5 %copy.88 = f32[4,3,64,2,128]{4,3,2,1,0:T(2,128)} copy(f32[4,3,64,2,128]{4,2,3,1,0:T(8,128)S(1)} %maximum_bitcast_fusion) | data formatting | bytes 1572864
  (64 shorter events, 1.2 us)
Async XLA Ops:
  9.9 14.7 %copy-start.1 = (s32[2,128]{1,0:T(2,128)S(1)}, s32[2,128]{1,0:T(2,128)}, u32[]{:S(2)}) copy-start(s32[2,128]{1,0:T(2,128)} %param.13) | copy-start | bytes 3076
  10.0 14.9 %copy-start.2 = (s32[128]{0:T(128)S(1)}, s32[128]{0:T(128)}, u32[]{:S(2)}) copy-start(s32[128]{0:T(128)} %param.12) | copy-start | bytes 1540
  42.0 38.4 %all-to-all-start = ((f32[16,2,126,128]{3,1,2,0:T(2,128)}), f32[16,2,126,128]{3,1,2,0:T(2,128)}, u32[]{:S(2)}, u32[]{:S(2)}) async-start(f32[16,2,126,128]{3,1,2,0:T(2,128)} %pad_maximum_fusion), calls=%async_computation | async-start | bytes 4128768 | tf_op jit(solution)/shard_map/all_to_all | solution.py:344
  90.8 2.8 %copy-start = (f32[4,3,2,48,128]{4,3,2,1,0:T(8,128)S(1)}, f32[4,3,2,48,128]{4,3,2,1,0:T(8,128)}, u32[]{:S(2)}) copy-start(f32[4,3,2,48,128]{4,3,2,1,0:T(8,128)} %slice.340) | copy-start | bytes 1769476

commit v8 on v7

--- a/solution.py
+++ b/solution.py
@@ -326,7 +326,8 @@
     grp = lax.axis_index("grp")
     me = col * GROUP + grp
     cols = up_dev.shape[0] // GROUP
-    pack = jnp.stack([first, last], axis=0)[None]
+    rows = first.shape[0]
+    pack = jnp.concatenate([first, last], axis=0)[None]
     held = lax.all_gather(pack, "grp", axis=0, tiled=True)
     pick = (jnp.arange(GROUP, dtype=jnp.int32) == grp)[None, :]
     t_up = jnp.sum(jnp.where(pick, up_dev.reshape(cols, GROUP), 0), axis=1)
@@ -338,14 +339,15 @@
     from_up = jnp.zeros((cols,) + first.shape, jnp.float32)
     from_low = jnp.zeros((cols,) + first.shape, jnp.float32)
     for k in range(GROUP):
-        from_up = jnp.where(up_at == k, held[k, 0][None], from_up)
-        from_low = jnp.where(low_at == k, held[k, 1][None], from_low)
-    slots = jnp.stack([from_up, from_low], axis=1)
+        from_up = jnp.where(up_at == k, held[k, :rows][None], from_up)
+        from_low = jnp.where(low_at == k, held[k, rows:][None], from_low)
+    rows = first.shape[0]
+    slots = jnp.concatenate([from_up, from_low], axis=1)
     got = lax.all_to_all(slots, "col", 0, 0, tiled=True)
     my_up = up_dev[me]
     my_low = low_dev[me]
-    above = lax.dynamic_index_in_dim(got, my_up // GROUP, axis=0, keepdims=False)[0]
-    below = lax.dynamic_index_in_dim(got, my_low // GROUP, axis=0, keepdims=False)[1]
+    above = lax.dynamic_index_in_dim(got, my_up // GROUP, axis=0, keepdims=False)[:rows]
+    below = lax.dynamic_index_in_dim(got, my_low // GROUP, axis=0, keepdims=False)[rows:]
     above = jnp.where(my_up != me, above, jnp.float32(0.0))
     below = jnp.where(my_low != me, below, jnp.float32(0.0))
     return below, above

time: 95.7 us -> 82.7 us (0.86)
  other arithmetic: 24.6 us -> 12.4 us
  local copies, waits for them, and re-layouts: 11.4 us -> 10.3 us
    select_n x3 -> x2, other arithmetic: 13.5 us -> 2 us  [the longest x1 1 us: exchange(): from_up = jnp.where(up_at == k, held[k, :rows][None], from_up)]
    another operation x2 -> x0, other arithmetic: 3.17 us -> none  [the longest x1 3.16 us: exchange(): slots = jnp.stack([from_up, from_low], axis=1)]
    concatenate x0 -> x1, other arithmetic: none -> 1.52 us  [exchange(): slots = jnp.concatenate([from_up, from_low], axis=1)]
    slice x1 -> x0, local copies, waits for them, and re-layouts: 1.08 us -> none  [exchange(): lax.dynamic_index_in_dim(got, my_up // GROUP, axis=0, keepdims=False)[0]]
  transfers between devices with their start and end apart: 1 -> 1, of which waited for: 1 -> 1; matrix products, arithmetic and copies ran while one was open for 3% -> 4% of each run, Pallas kernels for 17% -> 20%
where the time goes in v8:
time: 82.7 us; the launch traced here: 82.2 us
  Pallas kernels  25 us (30%)
  blocking collectives  14.3 us (17%)
  other arithmetic  12.4 us (15%)
  local copies, waits for them, and re-layouts  10.3 us (12%)
  between operations  9.07 us (11%)
  starting transfers between devices  7.93 us (10%)
  waiting for transfers between devices  3.2 us (4%)
    pallas_call x2, Pallas kernels, run_chain(): pl.pallas_call(chain_kernel, out_shape=(field, field), in_specs=[smem, vm...  25 us
    all_gather x1, blocking collectives, exchange(): held = lax.all_gather(pack, 'grp', axis=0, tiled=True)  14.3 us
    all_to_all x1, starting transfers between devices, exchange(): got = lax.all_to_all(slots, 'col', 0, 0, tiled=True)  7.93 us
    add x1, other arithmetic, lookup_modulus(): modulus + jnp.where(material == index, moduli[index], jnp.float32(0.0))  6.06 us
    all_to_all x1, waiting for transfers between devices, exchange(): got = lax.all_to_all(slots, 'col', 0, 0, tiled=True)  3.2 us
    unnamed x23, local copies, waits for them, and re-layouts  3.08 us
    slice x2, local copies, waits for them, and re-layouts, merge(): return jnp.concatenate([top, local[:, :, :, 8:depth - 8], bottom], axis=3)  1.73 us
  transfers between devices with their start and end apart: 1, of which 1 were waited for; matrix products, arithmetic and copies ran while one was open for 4% of the time, Pallas kernels for 20%

profile of v8, /device:TPU:0, one launch (start us, length us, event | category | flops | bytes accessed | tf_op | source)
XLA Modules:
  0.0 82.2 jit_solution(14679083568855802734)
XLA Ops:
  0.6 1.6 %fusion.26 = (f32[1]{0:T(128)}, f32[1]{0:T(128)}, f32[1]{0:T(128)}, f32[1]{0:T(128)}, f32[1]{0:T(128)}, /*index=5*/f32[1]{0:T(128)}, f32[1]{0:T(128)}, f32[1]{0:T(128)}) fusion(f32[8]{0:T(128)} %param.11), kind=kLoop, calls=%fused_computation.154 | loop fusion | bytes 64 | tf_op jit(solution)/shard_map/slice | solution.py:309
  2.3 6.1 %fusion.6 = f32[64,2,128]{2,1,0:T(2,128)S(1)} fusion(s32[64,2,128]{2,1,0:T(2,128)} %param.10, f32[]{:T(128)} %bitcast.22, f32[]{:T(128)} %bitcast.21, f32[]{:T(128)} %bitcast.20, f32[]{:T(128)} %bitcast.19, f32[]{:T(128)} %bitcast.18, f32[]{:T(128)} %bitcast.17, f32[]{:T(128)} %bitcast.16, f32[]{:T(128)} %bitcast.15), kind=kLoop, calls=%fused_computation.43 | loop fusion | flops 376832 | bytes 131104 | tf_op jit(solution)/shard_map/add | solution.py:309
  8.4 1.6 %copy_bitcast_fusion = (f32[4,3,2,64,128]{4,3,2,1,0:T(8,128)S(1)}, f32[4,3,2,64,128]{4,3,2,1,0:T(8,128)S(1)}) fusion(f32[4,3,64,2,128]{4,3,2,1,0:T(2,128)} %param.8, f32[4,3,64,2,128]{4,3,2,1,0:T(2,128)} %param.9), kind=kLoop, calls=%fused_computation.5 | loop fusion | bytes 3145728 | tf_op jit(solution)/shard_map/transpose | solution.py:359
  10.3 14.3 %all-gather.1 = f32[8,252,128]{2,1,0:T(8,128)S(1)} all-gather(f32[1,252,128]{2,1,0:T(8,128)S(1)} %maximum_bitcast_fusion.2), channel_id=2, replica_groups=mesh['col'=16,'grp'=8] {'grp'}, dimensions={0}, use_global_device_ids=true | all-gather | bytes 1161216 | tf_op jit(solution)/shard_map/all_gather | solution.py:331
  24.9 0.1 select_reduce_fusion
  25.1 0.1 select_reduce_fusion.2
  25.3 1.0 %select_select_fusion.1 = f32[16,126,128]{2,1,0:T(8,128)S(1)} fusion(f32[126,128]{1,0:T(8,128)S(1)} %get-tuple-element.42, f32[126,128]{1,0:T(8,128)S(1)} %get-tuple-element.43, f32[126,128]{1,0:T(8,128)S(1)} %get-tuple-element.44, f32[126,128]{1,0:T(8,128)S(1)} %get-tuple-element.45, f32[126,128]{1,0:T(8,128)S(1)} %get-tuple-element.46, ...), kind=kLoop, calls=%fused_computation.2 | loop fusion | flops 2064384 | bytes 1548416 | tf_op jit(solution)/shard_map/jit(_where)/select_n | solution.py:342
  26.3 1.0 %select_select_fusion = f32[16,126,128]{2,1,0:T(8,128)S(1)} fusion(f32[126,128]{1,0:T(8,128)S(1)} %get-tuple-element.49, f32[126,128]{1,0:T(8,128)S(1)} %get-tuple-element.35, f32[126,128]{1,0:T(8,128)S(1)} %get-tuple-element.36, f32[126,128]{1,0:T(8,128)S(1)} %get-tuple-element.37, f32[126,128]{1,0:T(8,128)S(1)} %get-tuple-element.38, ...), kind=kLoop, calls=%fused_computation.1 | loop fusion | flops 2064384 | bytes 1548416 | tf_op jit(solution)/shard_map/jit(_where)/select_n | solution.py:343
  27.3 1.5 %pad_maximum_fusion = f32[16,252,128]{2,1,0:T(8,128)} fusion(f32[16,126,128]{2,1,0:T(8,128)S(1)} %select_select_fusion, f32[16,126,128]{2,1,0:T(8,128)S(1)} %select_select_fusion.1), kind=kLoop, calls=%fused_computation | loop fusion | flops 516096 | bytes 4128768 | tf_op jit(solution)/shard_map/concatenate | solution.py:345
  28.8 7.9 %all-to-all-start = ((f32[16,252,128]{2,1,0:T(8,128)}), f32[16,252,128]{2,1,0:T(8,128)}, u32[]{:S(2)}, u32[]{:S(2)}) async-start(f32[16,252,128]{2,1,0:T(8,128)} %pad_maximum_fusion), calls=%async_computation | async-start | bytes 4194304 | tf_op jit(solution)/shard_map/all_to_all | solution.py:346
  36.8 0.6 dynamic_slice.16
  39.4 0.6 dynamic_slice.15
  46.1 16.3 %shard_map.96 = (f32[4,3,2,64,128]{4,3,2,1,0:T(8,128)S(1)}, f32[4,3,2,64,128]{4,3,2,1,0:T(8,128)S(1)}) custom-call(f32[3]{0:T(128)S(1)} %pad_maximum_fusion.3.scal_ref, f32[2,64,128]{2,1,0:T(8,128)S(1)} %broadcast_in_dim.366.mask_ref, f32[4,3,2,64,128]{4,3,2,1,0:T(8,128)S(1)} %get-tuple-element.117.md_ref, ...), custom_call_target="tpu_custom_call" | custom-call | flops 306708480 | bytes 3932160 | tf_op jit(solution)/shard_map/pallas_call | solution.py:288
  62.4 0.9 %slice.345 = f32[4,3,2,48,128]{4,3,2,1,0:T(8,128)} slice(f32[4,3,2,64,128]{4,3,2,1,0:T(8,128)S(1)} %get-tuple-element.9), slice={[0:4], [0:3], [0:2], [8:56], [0:128]} | slice | bytes 1179648 | tf_op jit(solution)/shard_map/slice | solution.py:458
  63.3 0.9 %slice.340 = f32[4,3,2,48,128]{4,3,2,1,0:T(8,128)} slice(f32[4,3,2,64,128]{4,3,2,1,0:T(8,128)S(1)} %get-tuple-element.7), slice={[0:4], [0:3], [0:2], [8:56], [0:128]} | slice | bytes 1179648 | tf_op jit(solution)/shard_map/slice | solution.py:458
  64.4 3.2 %all-to-all-done = f32[16,252,128]{2,1,0:T(8,128)} async-done(((f32[16,252,128]{2,1,0:T(8,128)}), f32[16,252,128]{2,1,0:T(8,128)}, u32[]{:S(2)}, u32[]{:S(2)}) %all-to-all-start) | async-done | bytes 2064416 | tf_op jit(solution)/shard_map/all_to_all | solution.py:346
  67.6 0.9 %dynamic-slice_select_fusion = (f32[1,126,128]{2,1,0:T(8,128)S(1)}, f32[1,126,128]{2,1,0:T(8,128)S(1)}) fusion(f32[16,252,128]{2,1,0:T(8,128)} %all-to-all-done, s32[]{:T(128)S(6)} %select_n.426, pred[]{:T(512)S(6)} %ne.282, s32[]{:T(128)S(6)} %select_n.422, s32[]{:T(128)S(6)} %add.216, pred[]{:T(512)S(6)} %ne.281), kind=kLoop, calls=%fused_computation.45 | loop fusion | flops 32256 | bytes 258062 | tf_op jit(solution)/shard_map/jit(_where)/select_n | solution.py:351
  68.6 0.2 concatenate.36.ld_ref
  68.9 0.2 concatenate.35.md_ref
  69.2 8.7 %shard_map.95 = (f32[4,3,2,32,128]{4,3,2,1,0:T(8,128)S(1)}, f32[4,3,2,32,128]{4,3,2,1,0:T(8,128)S(1)}) custom-call(f32[3]{0:T(128)S(1)} %pad_maximum_fusion.3.scal_ref, f32[2,32,128]{2,1,0:T(8,128)S(1)} %pad_maximum_fusion.2.mask_ref, f32[4,3,2,32,128]{4,3,2,1,0:T(8,128)S(1)} %concatenate.35.md_ref, f32[4,3,2,32,128]{4,3,2,1,0:T(8,128)S(1)} %concatenate.36.ld_ref, ...), custom_call_target="tpu_custom_call" | custom-call | flops 153354240 | bytes 1966080 | tf_op jit(solution)/shard_map/pallas_call | solution.py:288
  77.9 0.1 slice_select_fusion.3
  78.0 1.2 %maximum_bitcast_fusion.1 = f32[4,3,64,2,128]{4,2,3,1,0:T(8,128)S(1)} fusion(f32[4,3,2,8,128]{4,3,2,1,0:T(8,128)S(1)} %get-tuple-element.90, f32[4,3,2,48,128]{4,3,2,1,0:T(8,128)} %slice.345, f32[4,3,2,8,128]{4,3,2,1,0:T(8,128)S(1)} %get-tuple-element.91), kind=kLoop, calls=%fused_computation.4 | loop fusion | flops 393216 | bytes 1572864 | tf_op jit(solution)/shard_map/transpose | solution.py:464
  79.2 1.5 %copy.85 = f32[4,3,64,2,128]{4,3,2,1,0:T(2,128)} copy(f32[4,3,64,2,128]{4,2,3,1,0:T(8,128)S(1)} %maximum_bitcast_fusion.1) | data formatting | bytes 1572864
  80.7 1.5 %copy.84 = f32[4,3,64,2,128]{4,3,2,1,0:T(2,128)} copy(f32[4,3,64,2,128]{4,2,3,1,0:T(8,128)S(1)} %maximum_bitcast_fusion) | data formatting | bytes 1572864
  (62 shorter events, 1.2 us)
Async XLA Ops:
  9.9 14.8 %copy-start.1 = (s32[2,128]{1,0:T(2,128)S(1)}, s32[2,128]{1,0:T(2,128)}, u32[]{:S(2)}) copy-start(s32[2,128]{1,0:T(2,128)} %param.13) | copy-start | bytes 3076
  9.9 15.0 %copy-start.2 = (s32[128]{0:T(128)S(1)}, s32[128]{0:T(128)}, u32[]{:S(2)}) copy-start(s32[128]{0:T(128)} %param.12) | copy-start | bytes 1540
  28.8 38.8 %all-to-all-start = ((f32[16,252,128]{2,1,0:T(8,128)}), f32[16,252,128]{2,1,0:T(8,128)}, u32[]{:S(2)}, u32[]{:S(2)}) async-start(f32[16,252,128]{2,1,0:T(8,128)} %pad_maximum_fusion), calls=%async_computation | async-start | bytes 4194304 | tf_op jit(solution)/shard_map/all_to_all | solution.py:346
  77.8 2.8 %copy-start = (f32[4,3,2,48,128]{4,3,2,1,0:T(8,128)S(1)}, f32[4,3,2,48,128]{4,3,2,1,0:T(8,128)}, u32[]{:S(2)}) copy-start(f32[4,3,2,48,128]{4,3,2,1,0:T(8,128)} %slice.340) | copy-start | bytes 1769476

commit v9 on v8

--- a/solution.py
+++ b/solution.py
@@ -306,7 +306,7 @@
 def lookup_modulus(material, moduli):
     modulus = jnp.zeros(material.shape, jnp.float32)
     for index in range(MATERIALS):
-        modulus = modulus + jnp.where(material == index, moduli[index], jnp.float32(0.0))
+        modulus = modulus + jnp.where(material == float(index), moduli[index], jnp.float32(0.0))
     return modulus
 
 
@@ -358,8 +358,8 @@
     samples, _, depth, rows_y, width = loads.shape
     loads = jnp.transpose(loads, (0, 1, 3, 2, 4))
     modal_disp = jnp.transpose(modal_disp, (0, 1, 3, 2, 4))
-    flat_mod = lookup_modulus(material.reshape(depth, rows_y * width), moduli)
-    modulus = jnp.stack([flat_mod[:, y * width : (y + 1) * width] for y in range(rows_y)], axis=0)
+    ids = lax.optimization_barrier(jnp.transpose(material.astype(jnp.float32), (1, 0, 2)))
+    modulus = lookup_modulus(ids, moduli)
     plane = (samples, 3, rows_y, width)
     plane_size = samples * 3 * rows_y * width
     mod_size = rows_y * width

time: 82.7 us -> 82.6 us (level)
    add x1, other arithmetic: 6.06 us -> 5.08 us  [lookup_modulus(): modulus + jnp.where(material == float(index), moduli[index], jnp.float32(...]
    transpose x0 -> x1, other arithmetic: none -> 0.85 us  [on_device(): jnp.transpose(material.astype(jnp.float32), (1, 0, 2))]
    unnamed x23 -> x22, local copies, waits for them, and re-layouts: 3.08 us -> 3.07 us
where the time goes in v9:
time: 82.6 us; the launch traced here: 82.1 us
  Pallas kernels  25 us (30%)
  blocking collectives  14.3 us (17%)
  other arithmetic  12.3 us (15%)
  local copies, waits for them, and re-layouts  10.3 us (12%)
  between operations  9.06 us (11%)
  starting transfers between devices  7.93 us (10%)
  waiting for transfers between devices  3.21 us (4%)
    pallas_call x2, Pallas kernels, run_chain(): pl.pallas_call(chain_kernel, out_shape=(field, field), in_specs=[smem, vm...  25 us
    all_gather x1, blocking collectives, exchange(): held = lax.all_gather(pack, 'grp', axis=0, tiled=True)  14.3 us
    all_to_all x1, starting transfers between devices, exchange(): got = lax.all_to_all(slots, 'col', 0, 0, tiled=True)  7.93 us
    add x1, other arithmetic, lookup_modulus(): modulus + jnp.where(material == float(index), moduli[index], jnp.float32(...  5.08 us
    all_to_all x1, waiting for transfers between devices, exchange(): got = lax.all_to_all(slots, 'col', 0, 0, tiled=True)  3.21 us
    unnamed x22, local copies, waits for them, and re-layouts  3.07 us
    slice x2, local copies, waits for them, and re-layouts, merge(): return jnp.concatenate([top, local[:, :, :, 8:depth - 8], bottom], axis=3)  1.73 us
  transfers between devices with their start and end apart: 1, of which 1 were waited for; matrix products, arithmetic and copies ran while one was open for 4% of the time, Pallas kernels for 20%

profile of v9, /device:TPU:0, one launch (start us, length us, event | category | flops | bytes accessed | tf_op | source)
XLA Modules:
  0.0 82.1 jit_solution(11819382952589082039)
XLA Ops:
  0.6 1.6 %fusion.14 = (f32[1]{0:T(128)}, f32[1]{0:T(128)}, f32[1]{0:T(128)}, f32[1]{0:T(128)}, f32[1]{0:T(128)}, /*index=5*/f32[1]{0:T(128)}, f32[1]{0:T(128)}, f32[1]{0:T(128)}) fusion(f32[8]{0:T(128)} %param.11), kind=kLoop, calls=%fused_computation.116 | loop fusion | bytes 64 | tf_op jit(solution)/shard_map/slice | solution.py:309
  2.3 0.8 %fusion = f32[2,64,128]{2,1,0:T(8,128)S(1)} fusion(s32[64,2,128]{2,1,0:T(2,128)} %param.10), kind=kLoop, calls=%fused_computation.31 | loop fusion | flops 16384 | bytes 131072 | tf_op jit(solution)/shard_map/transpose | solution.py:361
  3.1 5.1 %select_add_fusion.mod_ref = f32[2,64,128]{2,1,0:T(8,128)S(1)} fusion(f32[2,64,128]{2,1,0:T(8,128)S(1)} %fusion, f32[]{:T(128)} %bitcast.23, f32[]{:T(128)} %bitcast.22, f32[]{:T(128)} %bitcast.21, f32[]{:T(128)} %bitcast.20, f32[]{:T(128)} %bitcast.19, f32[]{:T(128)} %bitcast.18, f32[]{:T(128)} %bitcast.17, f32[]{:T(128)} %bitcast.16), kind=kLoop, calls=%fused_computation.32 | loop fusion | flops 376832 | bytes 131104 | tf_op jit(solution)/shard_map/add | solution.py:309
  8.2 1.6 %copy_bitcast_fusion = (f32[4,3,2,64,128]{4,3,2,1,0:T(8,128)S(1)}, f32[4,3,2,64,128]{4,3,2,1,0:T(8,128)S(1)}) fusion(f32[4,3,64,2,128]{4,3,2,1,0:T(2,128)} %param.8, f32[4,3,64,2,128]{4,3,2,1,0:T(2,128)} %param.9), kind=kLoop, calls=%fused_computation.5 | loop fusion | bytes 3145728 | tf_op jit(solution)/shard_map/transpose | solution.py:359
  10.1 14.3 %all-gather.1 = f32[8,252,128]{2,1,0:T(8,128)S(1)} all-gather(f32[1,252,128]{2,1,0:T(8,128)S(1)} %maximum_bitcast_fusion.2), channel_id=2, replica_groups=mesh['col'=16,'grp'=8] {'grp'}, dimensions={0}, use_global_device_ids=true | all-gather | bytes 1161216 | tf_op jit(solution)/shard_map/all_gather | solution.py:331
  24.9 0.1 select_reduce_fusion.2
  25.2 1.0 %select_select_fusion.1 = f32[16,126,128]{2,1,0:T(8,128)S(1)} fusion(f32[126,128]{1,0:T(8,128)S(1)} %get-tuple-element.42, f32[126,128]{1,0:T(8,128)S(1)} %get-tuple-element.43, f32[126,128]{1,0:T(8,128)S(1)} %get-tuple-element.44, f32[126,128]{1,0:T(8,128)S(1)} %get-tuple-element.45, f32[126,128]{1,0:T(8,128)S(1)} %get-tuple-element.46, ...), kind=kLoop, calls=%fused_computation.2 | loop fusion | flops 2064384 | bytes 1548416 | tf_op jit(solution)/shard_map/jit(_where)/select_n | solution.py:342
  26.2 1.0 %select_select_fusion = f32[16,126,128]{2,1,0:T(8,128)S(1)} fusion(f32[126,128]{1,0:T(8,128)S(1)} %get-tuple-element.49, f32[126,128]{1,0:T(8,128)S(1)} %get-tuple-element.35, f32[126,128]{1,0:T(8,128)S(1)} %get-tuple-element.36, f32[126,128]{1,0:T(8,128)S(1)} %get-tuple-element.37, f32[126,128]{1,0:T(8,128)S(1)} %get-tuple-element.38, ...), kind=kLoop, calls=%fused_computation.1 | loop fusion | flops 2064384 | bytes 1548416 | tf_op jit(solution)/shard_map/jit(_where)/select_n | solution.py:343
  27.2 1.5 %pad_maximum_fusion = f32[16,252,128]{2,1,0:T(8,128)} fusion(f32[16,126,128]{2,1,0:T(8,128)S(1)} %select_select_fusion, f32[16,126,128]{2,1,0:T(8,128)S(1)} %select_select_fusion.1), kind=kLoop, calls=%fused_computation | loop fusion | flops 516096 | bytes 4128768 | tf_op jit(solution)/shard_map/concatenate | solution.py:345
  28.7 7.9 %all-to-all-start = ((f32[16,252,128]{2,1,0:T(8,128)}), f32[16,252,128]{2,1,0:T(8,128)}, u32[]{:S(2)}, u32[]{:S(2)}) async-start(f32[16,252,128]{2,1,0:T(8,128)} %pad_maximum_fusion), calls=%async_computation | async-start | bytes 4194304 | tf_op jit(solution)/shard_map/all_to_all | solution.py:346
  36.7 0.6 dynamic_slice.16
  39.2 0.6 dynamic_slice.15
  45.9 16.3 %shard_map.96 = (f32[4,3,2,64,128]{4,3,2,1,0:T(8,128)S(1)}, f32[4,3,2,64,128]{4,3,2,1,0:T(8,128)S(1)}) custom-call(f32[3]{0:T(128)S(1)} %pad_maximum_fusion.2.scal_ref, f32[2,64,128]{2,1,0:T(8,128)S(1)} %broadcast_49_mask_ref.2.mask_ref, f32[4,3,2,64,128]{4,3,2,1,0:T(8,128)S(1)} %get-tuple-element.115.md_ref, ...), custom_call_target="tpu_custom_call" | custom-call | flops 306708480 | bytes 3932160 | tf_op jit(solution)/shard_map/pallas_call | solution.py:288
  62.2 0.9 %slice.337 = f32[4,3,2,48,128]{4,3,2,1,0:T(8,128)} slice(f32[4,3,2,64,128]{4,3,2,1,0:T(8,128)S(1)} %get-tuple-element.9), slice={[0:4], [0:3], [0:2], [8:56], [0:128]} | slice | bytes 1179648 | tf_op jit(solution)/shard_map/slice | solution.py:458
  63.1 0.9 %slice.332 = f32[4,3,2,48,128]{4,3,2,1,0:T(8,128)} slice(f32[4,3,2,64,128]{4,3,2,1,0:T(8,128)S(1)} %get-tuple-element.7), slice={[0:4], [0:3], [0:2], [8:56], [0:128]} | slice | bytes 1179648 | tf_op jit(solution)/shard_map/slice | solution.py:458
  64.3 3.2 %all-to-all-done = f32[16,252,128]{2,1,0:T(8,128)} async-done(((f32[16,252,128]{2,1,0:T(8,128)}), f32[16,252,128]{2,1,0:T(8,128)}, u32[]{:S(2)}, u32[]{:S(2)}) %all-to-all-start) | async-done | bytes 2064416 | tf_op jit(solution)/shard_map/all_to_all | solution.py:346
  67.5 0.9 %dynamic-slice_select_fusion = (f32[1,126,128]{2,1,0:T(8,128)S(1)}, f32[1,126,128]{2,1,0:T(8,128)S(1)}) fusion(f32[16,252,128]{2,1,0:T(8,128)} %all-to-all-done, s32[]{:T(128)S(6)} %select_n.403, pred[]{:T(512)S(6)} %ne.282, s32[]{:T(128)S(6)} %select_n.399, s32[]{:T(128)S(6)} %add.206, pred[]{:T(512)S(6)} %ne.281), kind=kLoop, calls=%fused_computation.12 | loop fusion | flops 32256 | bytes 258062 | tf_op jit(solution)/shard_map/jit(_where)/select_n | solution.py:351
  68.5 0.2 concatenate.36.ld_ref
  68.7 0.2 concatenate.35.md_ref
  69.0 8.7 %shard_map.95 = (f32[4,3,2,32,128]{4,3,2,1,0:T(8,128)S(1)}, f32[4,3,2,32,128]{4,3,2,1,0:T(8,128)S(1)}) custom-call(f32[3]{0:T(128)S(1)} %pad_maximum_fusion.2.scal_ref, f32[2,32,128]{2,1,0:T(8,128)S(1)} %pad_maximum_fusion.1.mask_ref, f32[4,3,2,32,128]{4,3,2,1,0:T(8,128)S(1)} %concatenate.35.md_ref, f32[4,3,2,32,128]{4,3,2,1,0:T(8,128)S(1)} %concatenate.36.ld_ref, ...), custom_call_target="tpu_custom_call" | custom-call | flops 153354240 | bytes 1966080 | tf_op jit(solution)/shard_map/pallas_call | solution.py:288
  77.7 0.1 slice_select_fusion.3
  77.8 1.2 %maximum_bitcast_fusion.1 = f32[4,3,64,2,128]{4,2,3,1,0:T(8,128)S(1)} fusion(f32[4,3,2,8,128]{4,3,2,1,0:T(8,128)S(1)} %get-tuple-element.88, f32[4,3,2,48,128]{4,3,2,1,0:T(8,128)} %slice.337, f32[4,3,2,8,128]{4,3,2,1,0:T(8,128)S(1)} %get-tuple-element.89), kind=kLoop, calls=%fused_computation.4 | loop fusion | flops 393216 | bytes 1572864 | tf_op jit(solution)/shard_map/transpose | solution.py:464
  79.0 1.5 %copy.89 = f32[4,3,64,2,128]{4,3,2,1,0:T(2,128)} copy(f32[4,3,64,2,128]{4,2,3,1,0:T(8,128)S(1)} %maximum_bitcast_fusion.1) | data formatting | bytes 1572864
  80.6 1.5 %copy.88 = f32[4,3,64,2,128]{4,3,2,1,0:T(2,128)} copy(f32[4,3,64,2,128]{4,2,3,1,0:T(8,128)S(1)} %maximum_bitcast_fusion) | data formatting | bytes 1572864
  (60 shorter events, 1.3 us)
Async XLA Ops:
  9.8 14.8 %copy-start.1 = (s32[2,128]{1,0:T(2,128)S(1)}, s32[2,128]{1,0:T(2,128)}, u32[]{:S(2)}) copy-start(s32[2,128]{1,0:T(2,128)} %param.13) | copy-start | bytes 3076
  9.8 14.9 %copy-start.2 = (s32[128]{0:T(128)S(1)}, s32[128]{0:T(128)}, u32[]{:S(2)}) copy-start(s32[128]{0:T(128)} %param.12) | copy-start | bytes 1540
  28.7 38.8 %all-to-all-start = ((f32[16,252,128]{2,1,0:T(8,128)}), f32[16,252,128]{2,1,0:T(8,128)}, u32[]{:S(2)}, u32[]{:S(2)}) async-start(f32[16,252,128]{2,1,0:T(8,128)} %pad_maximum_fusion), calls=%async_computation | async-start | bytes 4194304 | tf_op jit(solution)/shard_map/all_to_all | solution.py:346
  77.7 2.8 %copy-start = (f32[4,3,2,48,128]{4,3,2,1,0:T(8,128)S(1)}, f32[4,3,2,48,128]{4,3,2,1,0:T(8,128)}, u32[]{:S(2)}) copy-start(f32[4,3,2,48,128]{4,3,2,1,0:T(8,128)} %slice.332) | copy-start | bytes 1769476

commit v10 on v9

--- a/solution.py
+++ b/solution.py
@@ -344,12 +344,14 @@
     rows = first.shape[0]
     slots = jnp.concatenate([from_up, from_low], axis=1)
     got = lax.all_to_all(slots, "col", 0, 0, tiled=True)
-    my_up = up_dev[me]
-    my_low = low_dev[me]
-    above = lax.dynamic_index_in_dim(got, my_up // GROUP, axis=0, keepdims=False)[:rows]
-    below = lax.dynamic_index_in_dim(got, my_low // GROUP, axis=0, keepdims=False)[rows:]
-    above = jnp.where(my_up != me, above, jnp.float32(0.0))
-    below = jnp.where(my_low != me, below, jnp.float32(0.0))
+    mine = jnp.arange(up_dev.shape[0], dtype=jnp.int32) == me
+    my_up = jnp.sum(jnp.where(mine, up_dev, 0))
+    my_low = jnp.sum(jnp.where(mine, low_dev, 0))
+    above = jnp.zeros(first.shape, jnp.float32)
+    below = jnp.zeros(first.shape, jnp.float32)
+    for k in range(cols):
+        above = jnp.where((my_up // GROUP == k) & (my_up != me), got[k, :rows], above)
+        below = jnp.where((my_low // GROUP == k) & (my_low != me), got[k, rows:], below)
     return below, above
 
 
@@ -395,8 +397,9 @@
             [jnp.stack(rows, axis=axis), own, jnp.stack(tail, axis=axis)], axis=axis
         )
 
-    low_on = low_dev[col_grp_index()] != col_grp_index()
-    up_on = up_dev[col_grp_index()] != col_grp_index()
+    mine = jnp.arange(up_dev.shape[0], dtype=jnp.int32) == col_grp_index()
+    low_on = jnp.sum(jnp.where(mine, low_dev, 0)) != col_grp_index()
+    up_on = jnp.sum(jnp.where(mine, up_dev, 0)) != col_grp_index()
     zero_mod = jnp.zeros((rows_y, width), jnp.float32)
     zero_plane = jnp.zeros(plane, jnp.float32)
 

time: 82.6 us -> 84.4 us (1.022)
  other arithmetic: 12.3 us -> 14.6 us
  local copies, waits for them, and re-layouts: 10.3 us -> 9.14 us
    select_n x3 -> x2, other arithmetic: 0.95 us -> 2.73 us  [the longest x1 1.44 us: exchange(): jnp.where((my_low // GROUP == k) & (my_low != me), got[k, rows:], below)]
    dynamic_slice x2 -> x0, local copies, waits for them, and re-layouts: 1.18 us -> none  [the longest x1 0.59 us: on_device(): up_on = up_dev[col_grp_index()] != col_grp_index()]
  transfers between devices with their start and end apart: 1 -> 1, of which waited for: 1 -> 1; matrix products, arithmetic and copies ran while one was open for 4% -> 3% of each run, Pallas kernels for 20% -> 19%
where the time goes in v10:
time: 84.4 us; the launch traced here: 83.8 us
  Pallas kernels  25 us (30%)
  other arithmetic  14.6 us (17%)
  blocking collectives  14.3 us (17%)
  between operations  9.19 us (11%)
  local copies, waits for them, and re-layouts  9.14 us (11%)
  starting transfers between devices  7.93 us (9%)
  waiting for transfers between devices  3.63 us (4%)
    pallas_call x2, Pallas kernels, run_chain(): pl.pallas_call(chain_kernel, out_shape=(field, field), in_specs=[smem, vm...  25 us
    all_gather x1, blocking collectives, exchange(): held = lax.all_gather(pack, 'grp', axis=0, tiled=True)  14.3 us
    all_to_all x1, starting transfers between devices, exchange(): got = lax.all_to_all(slots, 'col', 0, 0, tiled=True)  7.93 us
    add x1, other arithmetic, lookup_modulus(): modulus + jnp.where(material == float(index), moduli[index], jnp.float32(...  5.05 us
    all_to_all x1, waiting for transfers between devices, exchange(): got = lax.all_to_all(slots, 'col', 0, 0, tiled=True)  3.63 us
    unnamed x22, local copies, waits for them, and re-layouts  3.07 us
    slice x2, local copies, waits for them, and re-layouts, merge(): return jnp.concatenate([top, local[:, :, :, 8:depth - 8], bottom], axis=3)  1.73 us
  transfers between devices with their start and end apart: 1, of which 1 were waited for; matrix products, arithmetic and copies ran while one was open for 3% of the time, Pallas kernels for 19%

profile of v10, /device:TPU:0, one launch (start us, length us, event | category | flops | bytes accessed | tf_op | source)
XLA Modules:
  0.0 83.8 jit_solution(2318085576927680811)
XLA Ops:
  0.6 1.6 %fusion.46 = (f32[1]{0:T(128)}, f32[1]{0:T(128)}, f32[1]{0:T(128)}, f32[1]{0:T(128)}, f32[1]{0:T(128)}, /*index=5*/f32[1]{0:T(128)}, f32[1]{0:T(128)}, f32[1]{0:T(128)}) fusion(f32[8]{0:T(128)} %param.11), kind=kLoop, calls=%fused_computation.150 | loop fusion | bytes 64 | tf_op jit(solution)/shard_map/slice | solution.py:309
  2.2 0.8 %fusion.30 = f32[2,64,128]{2,1,0:T(8,128)S(1)} fusion(s32[64,2,128]{2,1,0:T(2,128)} %param.10), kind=kLoop, calls=%fused_computation.61 | loop fusion | flops 16384 | bytes 131072 | tf_op jit(solution)/shard_map/transpose | solution.py:363
  3.1 5.0 %select_add_fusion.mod_ref = f32[2,64,128]{2,1,0:T(8,128)S(1)} fusion(f32[2,64,128]{2,1,0:T(8,128)S(1)} %fusion.30, f32[]{:T(128)} %bitcast.21, f32[]{:T(128)} %bitcast.20, f32[]{:T(128)} %bitcast.19, f32[]{:T(128)} %bitcast.18, f32[]{:T(128)} %bitcast.17, f32[]{:T(128)} %bitcast.16, f32[]{:T(128)} %bitcast.15, f32[]{:T(128)} %bitcast.14), kind=kLoop, calls=%fused_computation.62 | loop fusion | flops 376832 | bytes 131104 | tf_op jit(solution)/shard_map/add | solution.py:309
  8.2 1.6 %copy_bitcast_fusion = (f32[4,3,2,64,128]{4,3,2,1,0:T(8,128)S(1)}, f32[4,3,2,64,128]{4,3,2,1,0:T(8,128)S(1)}) fusion(f32[4,3,64,2,128]{4,3,2,1,0:T(2,128)} %param.8, f32[4,3,64,2,128]{4,3,2,1,0:T(2,128)} %param.9), kind=kLoop, calls=%fused_computation.5 | loop fusion | bytes 3145728 | tf_op jit(solution)/shard_map/transpose | solution.py:361
  10.1 14.3 %all-gather.1 = f32[8,252,128]{2,1,0:T(8,128)S(1)} all-gather(f32[1,252,128]{2,1,0:T(8,128)S(1)} %maximum_bitcast_fusion.2), channel_id=2, replica_groups=mesh['col'=16,'grp'=8] {'grp'}, dimensions={0}, use_global_device_ids=true | all-gather | bytes 1161216 | tf_op jit(solution)/shard_map/all_gather | solution.py:331
  24.9 0.1 select_reduce_fusion.2
  25.1 1.0 %select_select_fusion.1 = f32[16,126,128]{2,1,0:T(8,128)S(1)} fusion(f32[126,128]{1,0:T(8,128)S(1)} %get-tuple-element.40, f32[126,128]{1,0:T(8,128)S(1)} %get-tuple-element.41, f32[126,128]{1,0:T(8,128)S(1)} %get-tuple-element.42, f32[126,128]{1,0:T(8,128)S(1)} %get-tuple-element.43, f32[126,128]{1,0:T(8,128)S(1)} %get-tuple-element.44, ...), kind=kLoop, calls=%fused_computation.2 | loop fusion | flops 2064384 | bytes 1548416 | tf_op jit(solution)/shard_map/jit(_where)/select_n | solution.py:342
  26.1 1.0 %select_select_fusion = f32[16,126,128]{2,1,0:T(8,128)S(1)} fusion(f32[126,128]{1,0:T(8,128)S(1)} %get-tuple-element.47, f32[126,128]{1,0:T(8,128)S(1)} %get-tuple-element.33, f32[126,128]{1,0:T(8,128)S(1)} %get-tuple-element.34, f32[126,128]{1,0:T(8,128)S(1)} %get-tuple-element.35, f32[126,128]{1,0:T(8,128)S(1)} %get-tuple-element.36, ...), kind=kLoop, calls=%fused_computation.1 | loop fusion | flops 2064384 | bytes 1548416 | tf_op jit(solution)/shard_map/jit(_where)/select_n | solution.py:343
  27.1 1.5 %pad_maximum_fusion = f32[16,252,128]{2,1,0:T(8,128)} fusion(f32[16,126,128]{2,1,0:T(8,128)S(1)} %select_select_fusion, f32[16,126,128]{2,1,0:T(8,128)S(1)} %select_select_fusion.1), kind=kLoop, calls=%fused_computation | loop fusion | flops 516096 | bytes 4128768 | tf_op jit(solution)/shard_map/concatenate | solution.py:345
  28.6 7.9 %all-to-all-start = ((f32[16,252,128]{2,1,0:T(8,128)}), f32[16,252,128]{2,1,0:T(8,128)}, u32[]{:S(2)}, u32[]{:S(2)}) async-start(f32[16,252,128]{2,1,0:T(8,128)} %pad_maximum_fusion), calls=%async_computation | async-start | bytes 4194304 | tf_op jit(solution)/shard_map/all_to_all | solution.py:346
  36.6 0.6 fusion.33
  45.4 16.3 %shard_map.96 = (f32[4,3,2,64,128]{4,3,2,1,0:T(8,128)S(1)}, f32[4,3,2,64,128]{4,3,2,1,0:T(8,128)S(1)}) custom-call(f32[3]{0:T(128)S(1)} %pad_maximum_fusion.2.scal_ref, f32[2,64,128]{2,1,0:T(8,128)S(1)} %broadcast_51_mask_ref.2.mask_ref, f32[4,3,2,64,128]{4,3,2,1,0:T(8,128)S(1)} %get-tuple-element.113.md_ref, ...), custom_call_target="tpu_custom_call" | custom-call | flops 306708480 | bytes 3932160 | tf_op jit(solution)/shard_map/pallas_call | solution.py:288
  61.8 0.9 %slice.439 = f32[4,3,2,48,128]{4,3,2,1,0:T(8,128)} slice(f32[4,3,2,64,128]{4,3,2,1,0:T(8,128)S(1)} %get-tuple-element.9), slice={[0:4], [0:3], [0:2], [8:56], [0:128]} | slice | bytes 1179648 | tf_op jit(solution)/shard_map/slice | solution.py:461
  62.6 0.9 %slice.434 = f32[4,3,2,48,128]{4,3,2,1,0:T(8,128)} slice(f32[4,3,2,64,128]{4,3,2,1,0:T(8,128)S(1)} %get-tuple-element.7), slice={[0:4], [0:3], [0:2], [8:56], [0:128]} | slice | bytes 1179648 | tf_op jit(solution)/shard_map/slice | solution.py:461
  63.8 3.6 %all-to-all-done = f32[16,252,128]{2,1,0:T(8,128)} async-done(((f32[16,252,128]{2,1,0:T(8,128)}), f32[16,252,128]{2,1,0:T(8,128)}, u32[]{:S(2)}, u32[]{:S(2)}) %all-to-all-start) | async-done | bytes 2064416 | tf_op jit(solution)/shard_map/all_to_all | solution.py:346
  67.4 1.3 %fusion.14 = f32[1,126,128]{2,1,0:T(8,128)S(1)} fusion(f32[16,252,128]{2,1,0:T(8,128)} %all-to-all-done, pred[]{:T(512)S(6)} %and.431, pred[]{:T(512)S(6)} %and.432, pred[]{:T(512)S(6)} %and.433, pred[]{:T(512)S(6)} %and.434, pred[]{:T(512)S(6)} %and.435, pred[]{:T(512)S(6)} %and.436, pred[]{:T(512)S(6)} %and.437, pred[]{:T(512)S(6)} %and.438, ...), kind=kLoop, calls=%fused_computation.27 | loop fusion | flops 258048 | bytes 1096720 | tf_op jit(solution)/shard_map/jit(_where)/select_n | solution.py:353
  68.7 1.4 %fusion.29 = f32[1,126,128]{2,1,0:T(8,128)S(1)} fusion(f32[16,252,128]{2,1,0:T(8,128)} %all-to-all-done, pred[]{:T(512)S(6)} %and.409, pred[]{:T(512)S(6)} %and.415, pred[]{:T(512)S(6)} %and.416, pred[]{:T(512)S(6)} %and.417, pred[]{:T(512)S(6)} %and.418, pred[]{:T(512)S(6)} %and.419, pred[]{:T(512)S(6)} %and.420, pred[]{:T(512)S(6)} %and.421, ...), kind=kLoop, calls=%fused_computation.43 | loop fusion | flops 258048 | bytes 1096720 | tf_op jit(solution)/shard_map/jit(_where)/select_n | solution.py:354
  70.2 0.2 concatenate.36.ld_ref
  70.4 0.2 concatenate.35.md_ref
  70.7 8.7 %shard_map.95 = (f32[4,3,2,32,128]{4,3,2,1,0:T(8,128)S(1)}, f32[4,3,2,32,128]{4,3,2,1,0:T(8,128)S(1)}) custom-call(f32[3]{0:T(128)S(1)} %pad_maximum_fusion.2.scal_ref, f32[2,32,128]{2,1,0:T(8,128)S(1)} %pad_maximum_fusion.1.mask_ref, f32[4,3,2,32,128]{4,3,2,1,0:T(8,128)S(1)} %concatenate.35.md_ref, f32[4,3,2,32,128]{4,3,2,1,0:T(8,128)S(1)} %concatenate.36.ld_ref, ...), custom_call_target="tpu_custom_call" | custom-call | flops 153354240 | bytes 1966080 | tf_op jit(solution)/shard_map/pallas_call | solution.py:288
  79.4 0.1 slice_select_fusion.3
  79.5 1.2 %maximum_bitcast_fusion.1 = f32[4,3,64,2,128]{4,2,3,1,0:T(8,128)S(1)} fusion(f32[4,3,2,8,128]{4,3,2,1,0:T(8,128)S(1)} %get-tuple-element.86, f32[4,3,2,48,128]{4,3,2,1,0:T(8,128)} %slice.439, f32[4,3,2,8,128]{4,3,2,1,0:T(8,128)S(1)} %get-tuple-element.87), kind=kLoop, calls=%fused_computation.4 | loop fusion | flops 393216 | bytes 1572864 | tf_op jit(solution)/shard_map/transpose | solution.py:467
  80.7 1.5 %copy.89 = f32[4,3,64,2,128]{4,3,2,1,0:T(2,128)} copy(f32[4,3,64,2,128]{4,2,3,1,0:T(8,128)S(1)} %maximum_bitcast_fusion.1) | data formatting | bytes 1572864
  82.3 1.5 %copy.88 = f32[4,3,64,2,128]{4,3,2,1,0:T(2,128)} copy(f32[4,3,64,2,128]{4,2,3,1,0:T(8,128)S(1)} %maximum_bitcast_fusion) | data formatting | bytes 1572864
  (58 shorter events, 1.3 us)
Async XLA Ops:
  9.7 14.8 %copy-start.1 = (s32[2,128]{1,0:T(2,128)S(1)}, s32[2,128]{1,0:T(2,128)}, u32[]{:S(2)}) copy-start(s32[2,128]{1,0:T(2,128)} %param.13) | copy-start | bytes 3076
  9.7 14.9 %copy-start.2 = (s32[128]{0:T(128)S(1)}, s32[128]{0:T(128)}, u32[]{:S(2)}) copy-start(s32[128]{0:T(128)} %param.12) | copy-start | bytes 1540
  28.6 38.8 %all-to-all-start = ((f32[16,252,128]{2,1,0:T(8,128)}), f32[16,252,128]{2,1,0:T(8,128)}, u32[]{:S(2)}, u32[]{:S(2)}) async-start(f32[16,252,128]{2,1,0:T(8,128)} %pad_maximum_fusion), calls=%async_computation | async-start | bytes 4194304 | tf_op jit(solution)/shard_map/all_to_all | solution.py:346
  79.4 2.8 %copy-start = (f32[4,3,2,48,128]{4,3,2,1,0:T(8,128)S(1)}, f32[4,3,2,48,128]{4,3,2,1,0:T(8,128)}, u32[]{:S(2)}) copy-start(f32[4,3,2,48,128]{4,3,2,1,0:T(8,128)} %slice.434) | copy-start | bytes 1769476

commit v11 on v10

--- a/solution.py
+++ b/solution.py
@@ -328,30 +328,27 @@
     cols = up_dev.shape[0] // GROUP
     rows = first.shape[0]
     pack = jnp.concatenate([first, last], axis=0)[None]
-    held = lax.all_gather(pack, "grp", axis=0, tiled=True)
-    pick = (jnp.arange(GROUP, dtype=jnp.int32) == grp)[None, :]
-    t_up = jnp.sum(jnp.where(pick, up_dev.reshape(cols, GROUP), 0), axis=1)
-    t_low = jnp.sum(jnp.where(pick, low_dev.reshape(cols, GROUP), 0), axis=1)
-    up_at = jnp.where(t_up // GROUP == col, t_up % GROUP, -1)[:, None]
-    low_at = jnp.where(t_low // GROUP == col, t_low % GROUP, -1)[:, None]
-    up_at = up_at[:, :, None]
-    low_at = low_at[:, :, None]
-    from_up = jnp.zeros((cols,) + first.shape, jnp.float32)
-    from_low = jnp.zeros((cols,) + first.shape, jnp.float32)
-    for k in range(GROUP):
+    held = lax.all_gather(pack, "col", axis=0, tiled=True)
+    pick = (jnp.arange(cols, dtype=jnp.int32) == col)[:, None]
+    t_up = jnp.sum(jnp.where(pick, up_dev.reshape(cols, GROUP), 0), axis=0)
+    t_low = jnp.sum(jnp.where(pick, low_dev.reshape(cols, GROUP), 0), axis=0)
+    up_at = jnp.where(t_up % GROUP == grp, t_up // GROUP, -1)[:, None, None]
+    low_at = jnp.where(t_low % GROUP == grp, t_low // GROUP, -1)[:, None, None]
+    from_up = jnp.zeros((GROUP,) + first.shape, jnp.float32)
+    from_low = jnp.zeros((GROUP,) + first.shape, jnp.float32)
+    for k in range(cols):
         from_up = jnp.where(up_at == k, held[k, :rows][None], from_up)
         from_low = jnp.where(low_at == k, held[k, rows:][None], from_low)
-    rows = first.shape[0]
     slots = jnp.concatenate([from_up, from_low], axis=1)
-    got = lax.all_to_all(slots, "col", 0, 0, tiled=True)
+    got = lax.all_to_all(slots, "grp", 0, 0, tiled=True)
     mine = jnp.arange(up_dev.shape[0], dtype=jnp.int32) == me
     my_up = jnp.sum(jnp.where(mine, up_dev, 0))
     my_low = jnp.sum(jnp.where(mine, low_dev, 0))
     above = jnp.zeros(first.shape, jnp.float32)
     below = jnp.zeros(first.shape, jnp.float32)
-    for k in range(cols):
-        above = jnp.where((my_up // GROUP == k) & (my_up != me), got[k, :rows], above)
-        below = jnp.where((my_low // GROUP == k) & (my_low != me), got[k, rows:], below)
+    for k in range(GROUP):
+        above = jnp.where((my_up % GROUP == k) & (my_up != me), got[k, :rows], above)
+        below = jnp.where((my_low % GROUP == k) & (my_low != me), got[k, rows:], below)
     return below, above
 
 

time: 84.4 us -> 115 us (1.36)
  waiting for transfers between devices: 3.63 us -> 37.3 us
  blocking collectives: 14.3 us -> 0 us
  between operations: 9.19 us -> 21.2 us
  starting transfers between devices: 7.93 us -> 4.33 us
  local copies, waits for them, and re-layouts: 9.14 us -> 11.8 us
    all_gather x0 -> x1, waiting for transfers between devices: none -> 21.5 us  [exchange(): held = lax.all_gather(pack, 'col', axis=0, tiled=True)]
    all_gather x1 -> x0, blocking collectives: 14.3 us -> none  [exchange(): held = lax.all_gather(pack, 'grp', axis=0, tiled=True)]
    all_to_all x1, waiting for transfers between devices: 3.63 us -> 15.8 us  [exchange(): got = lax.all_to_all(slots, 'grp', 0, 0, tiled=True)]
    all_to_all x1, starting transfers between devices: 7.93 us -> 4.29 us  [exchange(): got = lax.all_to_all(slots, 'grp', 0, 0, tiled=True)]
    broadcast_in_dim x1 -> x2, local copies, waits for them, and re-layouts: 0.09 us -> 2.74 us  [exchange(): from_up = jnp.where(up_at == k, held[k, :rows][None], from_up)]
  transfers between devices with their start and end apart: 1 -> 2, of which waited for: 1 -> 2; matrix products, arithmetic and copies ran while one was open for 3% -> 3% of each run, Pallas kernels for 19% -> 14%
where the time goes in v11:
time: 115 us; the launch traced here: 113 us
  waiting for transfers between devices  37.3 us (32%)
  Pallas kernels  25 us (22%)
  between operations  21.2 us (18%)
  other arithmetic  13.8 us (12%)
  local copies, waits for them, and re-layouts  11.8 us (10%)
  starting transfers between devices  4.33 us (4%)
    pallas_call x2, Pallas kernels, run_chain(): pl.pallas_call(chain_kernel, out_shape=(field, field), in_specs=[smem, vm...  25 us
    all_gather x1, waiting for transfers between devices, exchange(): held = lax.all_gather(pack, 'col', axis=0, tiled=True)  21.5 us
    all_to_all x1, waiting for transfers between devices, exchange(): got = lax.all_to_all(slots, 'grp', 0, 0, tiled=True)  15.8 us
    add x1, other arithmetic, lookup_modulus(): modulus + jnp.where(material == float(index), moduli[index], jnp.float32(...  5.02 us
    all_to_all x1, starting transfers between devices, exchange(): got = lax.all_to_all(slots, 'grp', 0, 0, tiled=True)  4.29 us
    unnamed x22, local copies, waits for them, and re-layouts  3.08 us
    broadcast_in_dim x2, local copies, waits for them, and re-layouts, exchange(): from_up = jnp.where(up_at == k, held[k, :rows][None], from_up)  2.74 us
  transfers between devices with their start and end apart: 2, of which 2 were waited for; matrix products, arithmetic and copies ran while one was open for 3% of the time, Pallas kernels for 14%

profile of v11, /device:TPU:0, one launch (start us, length us, event | category | flops | bytes accessed | tf_op | source)
XLA Modules:
  0.0 113.4 jit_solution(3417666300639532200)
XLA Ops:
  7.2 1.6 %fusion.30 = (f32[1]{0:T(128)}, f32[1]{0:T(128)}, f32[1]{0:T(128)}, f32[1]{0:T(128)}, f32[1]{0:T(128)}, /*index=5*/f32[1]{0:T(128)}, f32[1]{0:T(128)}, f32[1]{0:T(128)}) fusion(f32[8]{0:T(128)} %param.11), kind=kLoop, calls=%fused_computation.166 | loop fusion | bytes 64 | tf_op jit(solution)/shard_map/slice | solution.py:309
  8.8 0.8 fusion.14
  9.7 5.0 %select_add_fusion.mod_ref = f32[2,64,128]{2,1,0:T(8,128)S(1)} fusion(f32[2,64,128]{2,1,0:T(8,128)S(1)} %fusion.14, f32[]{:T(128)} %bitcast.21, f32[]{:T(128)} %bitcast.20, f32[]{:T(128)} %bitcast.19, f32[]{:T(128)} %bitcast.18, f32[]{:T(128)} %bitcast.17, f32[]{:T(128)} %bitcast.16, f32[]{:T(128)} %bitcast.15, f32[]{:T(128)} %bitcast.14), kind=kLoop, calls=%fused_computation.62 | loop fusion | flops 376832 | bytes 131104 | tf_op jit(solution)/shard_map/add | solution.py:309
  14.8 1.6 %copy_bitcast_fusion = (f32[4,3,2,64,128]{4,3,2,1,0:T(8,128)S(1)}, f32[4,3,2,64,128]{4,3,2,1,0:T(8,128)S(1)}) fusion(f32[4,3,64,2,128]{4,3,2,1,0:T(2,128)} %param.8, f32[4,3,64,2,128]{4,3,2,1,0:T(2,128)} %param.9), kind=kLoop, calls=%fused_computation.3 | loop fusion | bytes 3145728 | tf_op jit(solution)/shard_map/transpose | solution.py:358
  16.6 0.7 maximum_bitcast_fusion.2
  17.5 0.6 fusion.17
  25.2 16.3 %shard_map.96 = (f32[4,3,2,64,128]{4,3,2,1,0:T(8,128)S(1)}, f32[4,3,2,64,128]{4,3,2,1,0:T(8,128)S(1)}) custom-call(f32[3]{0:T(128)S(1)} %pad_maximum_fusion.2.scal_ref, f32[2,64,128]{2,1,0:T(8,128)S(1)} %broadcast_67_mask_ref.2.mask_ref, f32[4,3,2,64,128]{4,3,2,1,0:T(8,128)S(1)} %get-tuple-element.145.md_ref, ...), custom_call_target="tpu_custom_call" | custom-call | flops 306708480 | bytes 3932160 | tf_op jit(solution)/shard_map/pallas_call | solution.py:288
  41.5 0.9 slice.439
  42.4 0.9 slice.434
  43.4 21.5 %all-gather.4.cloned.1.call-done = f32[16,252,128]{2,1,0:T(8,128)} async-done(((f32[1,252,128]{2,1,0:T(8,128)}), f32[16,252,128]{2,1,0:T(8,128)}) %all-gather.4.cloned.1.call-update) | async-done | bytes 2064400 | tf_op jit(solution)/shard_map/all_gather | solution.py:331
  65.0 1.4 %slice_bitcast_fusion.31 = (f32[126,128]{1,0:T(8,128)S(1)}, f32[126,128]{1,0:T(8,128)S(1)}, f32[126,128]{1,0:T(8,128)S(1)}, f32[126,128]{1,0:T(8,128)S(1)}, f32[...) fusion(f32[16,252,128]{2,1,0:T(8,128)} %all-gather.4.cloned.1.c, ...), kind=kLoop, calls=%fused_computation.59 | loop fusion | bytes 2451456 | tf_op jit(solution)/shard_map/jit(_where)/broadcast_in_dim | solution.py:340
  66.4 1.3 %slice_bitcast_fusion.30 = (f32[126,128]{1,0:T(8,128)S(1)}, f32[126,128]{1,0:T(8,128)S(1)}, f32[126,128]{1,0:T(8,128)S(1)}, f32[126,128]{1,0:T(8,128)S(1)}, f32[...) fusion(f32[16,252,128]{2,1,0:T(8,128)} %all-gather.4.cloned.1.c, ...), kind=kLoop, calls=%fused_computation.58 | loop fusion | bytes 1677312 | tf_op jit(solution)/shard_map/jit(_where)/broadcast_in_dim | solution.py:340
  67.7 0.7 select_select_fusion.1
  68.5 0.7 select_select_fusion
  69.2 1.1 pad_maximum_fusion
  70.3 4.3 %all-to-all-start = ((f32[8,252,128]{2,1,0:T(8,128)}), f32[8,252,128]{2,1,0:T(8,128)}, u32[]{:S(2)}, u32[]{:S(2)}) async-start(f32[8,252,128]{2,1,0:T(8,128)} %pad_maximum_fusion), calls=%async_computation | async-start | bytes 2097152 | tf_op jit(solution)/shard_map/all_to_all | solution.py:343
  74.9 15.8 %all-to-all-done = f32[8,252,128]{2,1,0:T(8,128)} async-done(((f32[8,252,128]{2,1,0:T(8,128)}), f32[8,252,128]{2,1,0:T(8,128)}, u32[]{:S(2)}, u32[]{:S(2)}) %all-to-all-start) | async-done | bytes 1032224 | tf_op jit(solution)/shard_map/all_to_all | solution.py:343
  90.7 1.1 fusion.6
  91.8 1.2 %fusion.13 = f32[1,126,128]{2,1,0:T(8,128)S(1)} fusion(f32[8,252,128]{2,1,0:T(8,128)} %all-to-all-done, pred[]{:T(512)S(6)} %and.521, pred[]{:T(512)S(6)} %and.527, pred[]{:T(512)S(6)} %and.528, pred[]{:T(512)S(6)} %and.529, pred[]{:T(512)S(6)} %and.533, pred[]{:T(512)S(6)} %and.532, pred[]{:T(512)S(6)} %and.531, pred[]{:T(512)S(6)} %and.530), kind=kLoop, calls=%fused_computation.27 | loop fusion | flops 129024 | bytes 580616 | tf_op jit(solution)/shard_map/jit(_where)/select_n | solution.py:351
  93.2 0.2 concatenate.35.md_ref
  93.5 8.7 %shard_map.95 = (f32[4,3,2,32,128]{4,3,2,1,0:T(8,128)S(1)}, f32[4,3,2,32,128]{4,3,2,1,0:T(8,128)S(1)}) custom-call(f32[3]{0:T(128)S(1)} %pad_maximum_fusion.2.scal_ref, f32[2,32,128]{2,1,0:T(8,128)S(1)} %pad_maximum_fusion.1.mask_ref, f32[4,3,2,32,128]{4,3,2,1,0:T(8,128)S(1)} %concatenate.35.md_ref, f32[4,3,2,32,128]{4,3,2,1,0:T(8,128)S(1)} %concatenate.36.ld_ref, ...), custom_call_target="tpu_custom_call" | custom-call | flops 153354240 | bytes 1966080 | tf_op jit(solution)/shard_map/pallas_call | solution.py:288
  102.3 1.2 %maximum_bitcast_fusion.1 = f32[4,3,64,2,128]{4,2,3,1,0:T(8,128)S(1)} fusion(f32[4,3,2,8,128]{4,3,2,1,0:T(8,128)S(1)} %get-tuple-element.102, f32[4,3,2,48,128]{4,3,2,1,0:T(8,128)} %slice.439, f32[4,3,2,8,128]{4,3,2,1,0:T(8,128)S(1)} %get-tuple-element.103), kind=kLoop, calls=%fused_computation.2 | loop fusion | flops 393216 | bytes 1572864 | tf_op jit(solution)/shard_map/transpose | solution.py:464
  103.5 1.5 %copy.89 = f32[4,3,64,2,128]{4,3,2,1,0:T(2,128)} copy(f32[4,3,64,2,128]{4,2,3,1,0:T(8,128)S(1)} %maximum_bitcast_fusion.1) | data formatting | bytes 1572864
  105.1 1.5 %copy.88 = f32[4,3,64,2,128]{4,3,2,1,0:T(2,128)} copy(f32[4,3,64,2,128]{4,2,3,1,0:T(8,128)S(1)} %maximum_bitcast_fusion) | data formatting | bytes 1572864
  (61 shorter events, 1.6 us)
Async XLA Ops:
  7.2 57.8 %all-gather.4.cloned.1.call-start = ((), (), s32[]{:S(2)}) async-start(), calls=%async_computation.1 | async-start | bytes 2228224 | tf_op jit(solution)/shard_map/all_gather | solution.py:331
  14.7 2.6 %copy-start.2 = (s32[128]{0:T(128)S(1)}, s32[128]{0:T(128)}, u32[]{:S(2)}) copy-start(s32[128]{0:T(128)} %param.12) | copy-start | bytes 1540
  14.7 2.8 %copy-start.1 = (s32[2,128]{1,0:T(2,128)S(1)}, s32[2,128]{1,0:T(2,128)}, u32[]{:S(2)}) copy-start(s32[2,128]{1,0:T(2,128)} %param.13) | copy-start | bytes 3076
  70.3 20.3 %all-to-all-start = ((f32[8,252,128]{2,1,0:T(8,128)}), f32[8,252,128]{2,1,0:T(8,128)}, u32[]{:S(2)}, u32[]{:S(2)}) async-start(f32[8,252,128]{2,1,0:T(8,128)} %pad_maximum_fusion), calls=%async_computation | async-start | bytes 2097152 | tf_op jit(solution)/shard_map/all_to_all | solution.py:343
  102.2 2.8 %copy-start = (f32[4,3,2,48,128]{4,3,2,1,0:T(8,128)S(1)}, f32[4,3,2,48,128]{4,3,2,1,0:T(8,128)}, u32[]{:S(2)}) copy-start(f32[4,3,2,48,128]{4,3,2,1,0:T(8,128)} %slice.434) | copy-start | bytes 1769476
Sparse Core Ops, SparseCore 0:
  17.4 47.4 all-gather.3

commit v12 on v9

--- a/solution.py
+++ b/solution.py
@@ -228,14 +228,21 @@
 
 
 def chain_kernel(
-    scal_ref, mask_ref, md_ref, ld_ref, mod_ref, disp_ref, res_ref,
-    edge_s, cm_s, jac_s, k_s, a_s, step0_s, step1_s,
+    scal_ref, moduli_ref, mask_ref, md_ref, ld_ref, ids_ref, disp_ref, res_ref,
+    mod_s, edge_s, cm_s, jac_s, k_s, a_s, step0_s, step1_s,
 ):
     samples, _, rows_y, depth, width = md_ref.shape
     theta = scal_ref[0]
     c1 = scal_ref[1]
     c2 = scal_ref[2]
-    edges_body(mod_ref, edge_s, cm_s, jac_s)
+    keep_mod = mask_ref[2] > 0.0
+    for y in range(rows_y):
+        ids = ids_ref[y]
+        modulus = jnp.zeros(ids.shape, jnp.float32)
+        for index in range(MATERIALS):
+            modulus = modulus + jnp.where(ids == float(index), moduli_ref[index], jnp.float32(0.0))
+        mod_s[y] = jnp.where(keep_mod, modulus, jnp.float32(0.0))
+    edges_body(mod_s, edge_s, cm_s, jac_s)
     stencil_body(md_ref, edge_s, cm_s, k_s)
     keep0 = mask_ref[0] > 0.0
     keep1 = mask_ref[1] > 0.0
@@ -279,7 +286,7 @@
     lax.fori_loop(0, samples * 3, third, 0)
 
 
-def run_chain(scalars, masks, md, ld, mod):
+def run_chain(scalars, moduli, masks, md, ld, ids):
     samples, _, rows_y, depth, width = md.shape
     vmem = pl.BlockSpec(memory_space=pltpu.VMEM)
     smem = pl.BlockSpec(memory_space=pltpu.SMEM)
@@ -288,9 +295,10 @@
     return pl.pallas_call(
         chain_kernel,
         out_shape=(field, field),
-        in_specs=[smem, vmem, vmem, vmem, vmem],
+        in_specs=[smem, smem, vmem, vmem, vmem, vmem],
         out_specs=(vmem, vmem),
         scratch_shapes=[
+            pltpu.VMEM((rows_y, depth, width), jnp.float32),
             pltpu.VMEM((len(OFFSETS), rows_y, depth, width), jnp.float32),
             pltpu.VMEM((rows_y, depth, width), jnp.float32),
             pltpu.VMEM((3, rows_y, depth, width), jnp.float32),
@@ -300,7 +308,7 @@
         cost_estimate=pl.CostEstimate(
             flops=3 * 26 * 20 * size, bytes_accessed=4 * 5 * size, transcendentals=0
         ),
-    )(scalars, masks, md, ld, mod)
+    )(scalars, moduli, masks, md, ld, ids)
 
 
 def lookup_modulus(material, moduli):
@@ -356,18 +364,15 @@
 def on_device(loads, modal_disp, material, moduli, part_device, partners, low_bound, high_bound):
     up_dev, low_dev = neighbour_devices(part_device, partners)
     samples, _, depth, rows_y, width = loads.shape
-    loads = jnp.transpose(loads, (0, 1, 3, 2, 4))
-    modal_disp = jnp.transpose(modal_disp, (0, 1, 3, 2, 4))
-    ids = lax.optimization_barrier(jnp.transpose(material.astype(jnp.float32), (1, 0, 2)))
-    modulus = lookup_modulus(ids, moduli)
+    ids_orig = material.astype(jnp.float32)
     plane = (samples, 3, rows_y, width)
     plane_size = samples * 3 * rows_y * width
     mod_size = rows_y * width
 
     def pack(md_rows, load_rows):
-        parts = [modal_disp[:, :, :, r].reshape(-1) for r in md_rows]
-        parts += [loads[:, :, :, r].reshape(-1) for r in load_rows]
-        parts += [modulus[:, r].reshape(-1) for r in md_rows]
+        parts = [modal_disp[:, :, r].reshape(-1) for r in md_rows]
+        parts += [loads[:, :, r].reshape(-1) for r in load_rows]
+        parts += [ids_orig[r].reshape(-1) for r in md_rows]
         flat = jnp.concatenate(parts)
         return flat.reshape(flat.shape[0] // width, width)
 
@@ -384,34 +389,32 @@
     md_above = planes_of(above, 3, 0, plane_size, plane)
     ld_below = planes_of(below, 2, 3 * plane_size, plane_size, plane)
     ld_above = planes_of(above, 2, 3 * plane_size, plane_size, plane)
-    mod_below = planes_of(below, 3, 5 * plane_size, mod_size, (rows_y, width))
-    mod_above = planes_of(above, 3, 5 * plane_size, mod_size, (rows_y, width))
-
-    def extend(own, lower, upper, axis):
-        zero = jnp.zeros_like(lower[0])
-        rows = [zero] * (8 - len(lower)) + list(lower)
-        tail = list(upper) + [zero] * (8 - len(upper))
-        return jnp.concatenate(
-            [jnp.stack(rows, axis=axis), own, jnp.stack(tail, axis=axis)], axis=axis
-        )
-
-    low_on = low_dev[col_grp_index()] != col_grp_index()
-    up_on = up_dev[col_grp_index()] != col_grp_index()
-    zero_mod = jnp.zeros((rows_y, width), jnp.float32)
-    zero_plane = jnp.zeros(plane, jnp.float32)
+    ids_below = planes_of(below, 3, 5 * plane_size, mod_size, (rows_y, width))
+    ids_above = planes_of(above, 3, 5 * plane_size, mod_size, (rows_y, width))
+
+    loads = jnp.transpose(loads, (0, 1, 3, 2, 4))
+    modal_disp = jnp.transpose(modal_disp, (0, 1, 3, 2, 4))
+    ids = jnp.transpose(ids_orig, (1, 0, 2))
+
+    mine = jnp.arange(up_dev.shape[0], dtype=jnp.int32) == col_grp_index()
+    low_on = jnp.sum(jnp.where(mine, low_dev, 0)) != col_grp_index()
+    up_on = jnp.sum(jnp.where(mine, up_dev, 0)) != col_grp_index()
 
     theta = (high_bound[0] + low_bound[0]) / 2.0
     half = (high_bound[0] - low_bound[0]) / 2.0
     sigma = theta / half
     rho0 = 1.0 / sigma
     rho1 = 1.0 / (2.0 * sigma - rho0)
-
     scalars = jnp.stack([theta, rho1 * rho0, 2.0 * rho1 / half]).astype(jnp.float32)
 
-    def chain(md, ld, mod, masks):
-        return run_chain(scalars, masks, md, ld, mod)
-
-    disp_local, res_local = chain(modal_disp, loads, modulus, jnp.ones((2, depth, width), jnp.float32))
+    def chain(md, ld, material_ids, masks):
+        return run_chain(scalars, moduli, masks, md, ld, material_ids)
+
+    disp_local, res_local = chain(modal_disp, loads, ids, jnp.ones((3, depth, width), jnp.float32))
+    out_local = (
+        jnp.transpose(disp_local, (0, 1, 3, 2, 4)),
+        jnp.transpose(res_local, (0, 1, 3, 2, 4)),
+    )
 
     edge_rows = 8
     head = slice(0, edge_rows)
@@ -432,7 +435,7 @@
 
     md_win = window(modal_disp, md_below, md_above, 3)
     ld_win = window(loads, ld_below, ld_above, 3)
-    mod_win = window(modulus, mod_below, mod_above, 1)
+    ids_win = window(ids, ids_below, ids_above, 1)
     logical = jnp.concatenate(
         [
             jnp.arange(-8, edge_rows, dtype=jnp.int32),
@@ -446,23 +449,18 @@
         keep = keep | (up_on & (logical >= depth) & (logical < depth + reach))
         return jnp.broadcast_to(keep.astype(jnp.float32)[:, None], (logical.shape[0], width))
 
-    masks = jnp.stack([valid(2), valid(1)], axis=0)
-    disp_win, res_win = chain(md_win, ld_win, mod_win, masks)
+    masks = jnp.stack([valid(2), valid(1), valid(3)], axis=0)
+    disp_win, res_win = chain(md_win, ld_win, ids_win, masks)
 
     reach = 3
-    sub_row = lax.broadcasted_iota(jnp.int32, (8, 1), 0)
-
-    def merge(local, win):
-        top = jnp.where(sub_row < reach, win[:, :, :, 8:16], local[:, :, :, 0:8])
-        bottom = jnp.where(sub_row >= 8 - reach, win[:, :, :, 16:24], local[:, :, :, depth - 8 : depth])
-        return jnp.concatenate([top, local[:, :, :, 8 : depth - 8], bottom], axis=3)
-
-    displacement = merge(disp_local, disp_win)
-    residual = merge(res_local, res_win)
-    return (
-        jnp.transpose(displacement, (0, 1, 3, 2, 4)),
-        jnp.transpose(residual, (0, 1, 3, 2, 4)),
-    )
+
+    def patch(out, win):
+        top = jnp.transpose(win[:, :, :, 8 : 8 + reach], (0, 1, 3, 2, 4))
+        bottom = jnp.transpose(win[:, :, :, 8 + 2 * edge_rows - reach : 8 + 2 * edge_rows], (0, 1, 3, 2, 4))
+        out = lax.dynamic_update_slice_in_dim(out, top, 0, axis=2)
+        return lax.dynamic_update_slice_in_dim(out, bottom, depth - reach, axis=2)
+
+    return (patch(out_local[0], disp_win), patch(out_local[1], res_win))
 
 
 def col_grp_index():

time: 82.6 us -> 75.5 us (0.914)
  other arithmetic: 12.3 us -> 7.12 us
  local copies, waits for them, and re-layouts: 10.3 us -> 8.13 us
  between operations: 9.06 us -> 10.3 us
  waiting for transfers between devices: 3.21 us -> 2 us
    add x1 -> x0, other arithmetic: 5.08 us -> none  [lookup_modulus(): modulus + jnp.where(material == float(index), moduli[index], jnp.float32(...]
    transpose x3 -> x0, other arithmetic: 2.1 us -> none  [the longest x1 1.19 us: on_device(): jnp.transpose(residual, (0, 1, 3, 2, 4))]
    slice x6 -> x3, local copies, waits for them, and re-layouts: 3.45 us -> 1.6 us  [the longest x1 0.81 us: pack(): parts = [modal_disp[:, :, r].reshape(-1) for r in md_rows]]
    transpose x1, local copies, waits for them, and re-layouts: 1.56 us -> 0.2 us  [on_device(): loads = jnp.transpose(loads, (0, 1, 3, 2, 4))]
    reduce_sum x0 -> x2, other arithmetic: none -> 1.34 us  [the longest x1 0.71 us: on_device(): low_on = jnp.sum(jnp.where(mine, low_dev, 0)) != col_grp_index()]
    all_to_all x1, waiting for transfers between devices: 3.21 us -> 2 us  [exchange(): got = lax.all_to_all(slots, 'col', 0, 0, tiled=True)]
    dynamic_update_slice x0 -> x4, local copies, waits for them, and re-layouts: none -> 0.91 us  [the longest x2 0.49 us: patch(): out = lax.dynamic_update_slice_in_dim(out, top, 0, axis=2)]
    convert_element_type x0 -> x1, other arithmetic: none -> 0.85 us  [on_device(): ids_orig = material.astype(jnp.float32)]
  transfers between devices with their start and end apart: 1 -> 1, of which waited for: 1 -> 1; matrix products, arithmetic and copies ran while one was open for 4% -> 4% of each run, Pallas kernels for 20% -> 22%
where the time goes in v12:
time: 75.5 us; the launch traced here: 75 us
  Pallas kernels  25.1 us (33%)
  blocking collectives  14.3 us (19%)
  between operations  10.3 us (14%)
  local copies, waits for them, and re-layouts  8.13 us (11%)
  starting transfers between devices  8.06 us (11%)
  other arithmetic  7.12 us (9%)
  waiting for transfers between devices  2 us (3%)
    pallas_call x2, Pallas kernels, run_chain(): pl.pallas_call(chain_kernel, out_shape=(field, field), in_specs=[smem, sm...  25.1 us
    all_gather x1, blocking collectives, exchange(): held = lax.all_gather(pack, 'grp', axis=0, tiled=True)  14.3 us
    all_to_all x1, starting transfers between devices, exchange(): got = lax.all_to_all(slots, 'col', 0, 0, tiled=True)  8.06 us
    unnamed x26, local copies, waits for them, and re-layouts  3.08 us
    all_to_all x1, waiting for transfers between devices, exchange(): got = lax.all_to_all(slots, 'col', 0, 0, tiled=True)  2 us
  transfers between devices with their start and end apart: 1, of which 1 were waited for; matrix products, arithmetic and copies ran while one was open for 4% of the time, Pallas kernels for 22%

profile of v12, /device:TPU:0, one launch (start us, length us, event | category | flops | bytes accessed | tf_op | source)
XLA Modules:
  0.0 75.0 jit_solution(17523158835410820944)
XLA Ops:
  0.6 0.8 %fusion.9 = (f32[4,3,1,2,128]{4,3,2,1,0:T(2,128)S(1)}, f32[4,3,1,2,128]{4,3,2,1,0:T(2,128)S(1)}, f32[4,3,1,2,128]{4,3,2,1,0:T(2,128)S(1)}, f32[4,3,1,2,128]{4,3,...) fusion(f32[4,3,64,2,128]{4,3,2,1,0:T(2,128)} %param.9), kind=kLoop, calls=%fused_computation.110 | loop fusion | bytes 147456 | tf_op jit(solution)/shard_map/slice | solution.py:373
  1.5 0.8 %fusion.8 = (f32[4,3,1,2,128]{4,3,2,1,0:T(2,128)S(1)}, f32[4,3,1,2,128]{4,3,2,1,0:T(2,128)S(1)}, f32[4,3,1,2,128]{4,3,2,1,0:T(2,128)S(1)}, f32[4,3,1,2,128]{4,3,2,1,0:T(2,128)S(1)}) fusion(f32[4,3,64,2,128]{4,3,2,1,0:T(2,128)} %param.8), kind=kLoop, calls=%fused_computation.109 | loop fusion | bytes 98304 | tf_op jit(solution)/shard_map/slice | solution.py:374
  2.3 0.9 %copy_convert_fusion = (f32[64,2,128]{2,0,1:T(8,128)S(1)}, f32[2,64,128]{2,1,0:T(8,128)S(1)}) fusion(s32[64,2,128]{2,1,0:T(2,128)} %param.10), kind=kLoop, calls=%fused_computation.24 | loop fusion | flops 16384 | bytes 196608 | tf_op jit(solution)/shard_map/convert_element_type | solution.py:367
  3.3 14.3 %all-gather.1 = f32[8,252,128]{2,1,0:T(8,128)S(1)} all-gather(f32[1,252,128]{2,1,0:T(8,128)S(1)} %maximum_bitcast_fusion), channel_id=2, replica_groups=mesh['col'=16,'grp'=8] {'grp'}, dimensions={0}, use_global_device_ids=true | all-gather | bytes 1161216 | tf_op jit(solution)/shard_map/all_gather | solution.py:339
  18.4 1.0 %select_select_fusion.1 = f32[16,126,128]{2,1,0:T(8,128)S(1)} fusion(f32[126,128]{1,0:T(8,128)S(1)} %get-tuple-element.41, f32[126,128]{1,0:T(8,128)S(1)} %get-tuple-element.42, f32[126,128]{1,0:T(8,128)S(1)} %get-tuple-element.43, f32[126,128]{1,0:T(8,128)S(1)} %get-tuple-element.44, f32[126,128]{1,0:T(8,128)S(1)} %get-tuple-element.45, ...), kind=kLoop, calls=%fused_computation.2 | loop fusion | flops 2064384 | bytes 1548416 | tf_op jit(solution)/shard_map/jit(_where)/select_n | solution.py:350
  19.4 1.0 %select_select_fusion = f32[16,126,128]{2,1,0:T(8,128)S(1)} fusion(f32[126,128]{1,0:T(8,128)S(1)} %get-tuple-element.48, f32[126,128]{1,0:T(8,128)S(1)} %get-tuple-element.34, f32[126,128]{1,0:T(8,128)S(1)} %get-tuple-element.35, f32[126,128]{1,0:T(8,128)S(1)} %get-tuple-element.36, f32[126,128]{1,0:T(8,128)S(1)} %get-tuple-element.37, ...), kind=kLoop, calls=%fused_computation.1 | loop fusion | flops 2064384 | bytes 1548416 | tf_op jit(solution)/shard_map/jit(_where)/select_n | solution.py:351
  20.4 1.5 %pad_maximum_fusion = f32[16,252,128]{2,1,0:T(8,128)} fusion(f32[16,126,128]{2,1,0:T(8,128)S(1)} %select_select_fusion, f32[16,126,128]{2,1,0:T(8,128)S(1)} %select_select_fusion.1), kind=kLoop, calls=%fused_computation | loop fusion | flops 516096 | bytes 4128768 | tf_op jit(solution)/shard_map/concatenate | solution.py:353
  21.9 8.1 %all-to-all-start = ((f32[16,252,128]{2,1,0:T(8,128)}), f32[16,252,128]{2,1,0:T(8,128)}, u32[]{:S(2)}, u32[]{:S(2)}) async-start(f32[16,252,128]{2,1,0:T(8,128)} %pad_maximum_fusion), calls=%async_computation | async-start | bytes 4194304 | tf_op jit(solution)/shard_map/all_to_all | solution.py:354
  30.0 0.7 fusion.2
  30.7 0.6 fusion.3
  31.3 0.6 dynamic_slice.15
  33.8 0.6 dynamic_slice.13
  41.8 0.2 copy_bitcast_fusion
  42.0 16.4 %shard_map.95 = (f32[4,3,2,64,128]{4,3,2,1,0:T(8,128)S(1)}, f32[4,3,2,64,128]{4,3,2,1,0:T(8,128)S(1)}) custom-call(f32[3]{0:T(128)S(1)} %pad_maximum_fusion.2.scal_ref, f32[8]{0:T(128)S(1)} %copy-done, f32[3,64,128]{2,1,0:T(8,128)S(1)} %broadcast_in_dim.248.mask_ref, f32[4,3,2,64,128]{4,3,2,1,0:T(8,128)S(1)} %get-tuple-element.111.md_ref, ...), custom_call_target="tpu_custom_call" | custom-call | flops 306708480 | bytes 3932160 | tf_op jit(solution)/shard_map/pallas_call | solution.py:295
  58.8 2.0 %all-to-all-done = f32[16,252,128]{2,1,0:T(8,128)} async-done(((f32[16,252,128]{2,1,0:T(8,128)}), f32[16,252,128]{2,1,0:T(8,128)}, u32[]{:S(2)}, u32[]{:S(2)}) %all-to-all-start) | async-done | bytes 2064416 | tf_op jit(solution)/shard_map/all_to_all | solution.py:354
  60.8 0.9 %dynamic-slice_select_fusion = (f32[1,126,128]{2,1,0:T(8,128)S(1)}, f32[1,126,128]{2,1,0:T(8,128)S(1)}) fusion(f32[16,252,128]{2,1,0:T(8,128)} %all-to-all-done, s32[]{:T(128)S(6)} %select_n.364, pred[]{:T(512)S(6)} %ne.296, s32[]{:T(128)S(6)} %select_n.360, s32[]{:T(128)S(6)} %add.175, pred[]{:T(512)S(6)} %ne.287), kind=kLoop, calls=%fused_computation.6 | loop fusion | flops 32256 | bytes 258062 | tf_op jit(solution)/shard_map/jit(_where)/select_n | solution.py:359
  62.0 0.2 concatenate.29.md_ref
  62.3 8.7 %shard_map.96 = (f32[4,3,2,32,128]{4,3,2,1,0:T(8,128)S(1)}, f32[4,3,2,32,128]{4,3,2,1,0:T(8,128)S(1)}) custom-call(f32[3]{0:T(128)S(1)} %pad_maximum_fusion.2.scal_ref, f32[8]{0:T(128)S(1)} %copy-done, f32[3,32,128]{2,1,0:T(8,128)S(1)} %pad_maximum_fusion.1.mask_ref, f32[4,3,2,32,128]{4,3,2,1,0:T(8,128)S(1)} %concatenate.29.md_ref, ...), custom_call_target="tpu_custom_call" | custom-call | flops 153354240 | bytes 1966080 | tf_op jit(solution)/shard_map/pallas_call | solution.py:295
  71.1 0.2 dynamic_update_slice.14
  71.3 0.2 dynamic_update_slice.15
  71.5 1.5 %copy.89 = f32[4,3,64,2,128]{4,3,2,1,0:T(2,128)} copy(f32[4,3,64,2,128]{4,2,3,1,0:T(8,128)S(1)} %dynamic_update_slice.15) | data formatting | bytes 1572864
  73.1 0.2 dynamic_update_slice.12
  73.3 0.2 dynamic_update_slice.13
  73.5 1.5 %copy.88 = f32[4,3,64,2,128]{4,3,2,1,0:T(2,128)} copy(f32[4,3,64,2,128]{4,2,3,1,0:T(8,128)S(1)} %dynamic_update_slice.13) | data formatting | bytes 1572864
  (63 shorter events, 1.5 us)
Async XLA Ops:
  1.4 16.3 %copy-start.3 = (s32[2,128]{1,0:T(2,128)S(1)}, s32[2,128]{1,0:T(2,128)}, u32[]{:S(2)}) copy-start(s32[2,128]{1,0:T(2,128)} %param.13) | copy-start | bytes 3076
  1.5 16.5 %copy-start.4 = (s32[128]{0:T(128)S(1)}, s32[128]{0:T(128)}, u32[]{:S(2)}) copy-start(s32[128]{0:T(128)} %param.12) | copy-start | bytes 1540
  21.9 19.9 %copy-start.1 = (f32[4,3,64,2,128]{4,3,2,1,0:T(2,128)S(1)}, f32[4,3,64,2,128]{4,3,2,1,0:T(2,128)}, u32[]{:S(2)}) copy-start(f32[4,3,64,2,128]{4,3,2,1,0:T(2,128)} %param.9) | copy-start | bytes 2359300
  21.9 19.9 %copy-start.2 = (f32[4,3,64,2,128]{4,3,2,1,0:T(2,128)S(1)}, f32[4,3,64,2,128]{4,3,2,1,0:T(2,128)}, u32[]{:S(2)}) copy-start(f32[4,3,64,2,128]{4,3,2,1,0:T(2,128)} %param.8) | copy-start | bytes 2359300
  21.9 38.9 %all-to-all-start = ((f32[16,252,128]{2,1,0:T(8,128)}), f32[16,252,128]{2,1,0:T(8,128)}, u32[]{:S(2)}, u32[]{:S(2)}) async-start(f32[16,252,128]{2,1,0:T(8,128)} %pad_maximum_fusion), calls=%async_computation | async-start | bytes 4194304 | tf_op jit(solution)/shard_map/all_to_all | solution.py:354
  30.0 12.1 %copy-start = (f32[8]{0:T(128)S(1)}, f32[8]{0:T(128)}, u32[]{:S(2)}) copy-start(f32[8]{0:T(128)} %moduli_ref.3) | copy-start | bytes 100

commit v13 on v12

--- a/solution.py
+++ b/solution.py
@@ -340,17 +340,13 @@
     pick = (jnp.arange(GROUP, dtype=jnp.int32) == grp)[None, :]
     t_up = jnp.sum(jnp.where(pick, up_dev.reshape(cols, GROUP), 0), axis=1)
     t_low = jnp.sum(jnp.where(pick, low_dev.reshape(cols, GROUP), 0), axis=1)
-    up_at = jnp.where(t_up // GROUP == col, t_up % GROUP, -1)[:, None]
-    low_at = jnp.where(t_low // GROUP == col, t_low % GROUP, -1)[:, None]
-    up_at = up_at[:, :, None]
-    low_at = low_at[:, :, None]
-    from_up = jnp.zeros((cols,) + first.shape, jnp.float32)
-    from_low = jnp.zeros((cols,) + first.shape, jnp.float32)
+    up_at = jnp.where(t_up // GROUP == col, t_up % GROUP, -1)[:, None, None]
+    low_at = jnp.where(t_low // GROUP == col, t_low % GROUP, -1)[:, None, None]
+    row = lax.broadcasted_iota(jnp.int32, (1, 2 * rows, 1), 1)
+    source = jnp.where(row < rows, up_at, low_at)
+    slots = jnp.zeros((cols, 2 * rows) + first.shape[1:], jnp.float32)
     for k in range(GROUP):
-        from_up = jnp.where(up_at == k, held[k, :rows][None], from_up)
-        from_low = jnp.where(low_at == k, held[k, rows:][None], from_low)
-    rows = first.shape[0]
-    slots = jnp.concatenate([from_up, from_low], axis=1)
+        slots = jnp.where(source == k, held[k][None], slots)
     got = lax.all_to_all(slots, "col", 0, 0, tiled=True)
     my_up = up_dev[me]
     my_low = low_dev[me]
@@ -416,30 +412,38 @@
         jnp.transpose(res_local, (0, 1, 3, 2, 4)),
     )
 
-    edge_rows = 8
-    head = slice(0, edge_rows)
-    tail = slice(depth - edge_rows, depth)
+    reach = 3
+    margin = 2 * reach
+    pad_rows = (-(2 * reach + 2 * margin)) % 8
 
     def window(own, lower, upper, axis):
-        zero = jnp.zeros_like(lower[0])
-        rows = [zero] * (8 - len(lower)) + list(lower)
-        after = list(upper) + [zero] * (8 - len(upper))
         index = [slice(None)] * own.ndim
-        index[axis] = head
+        index[axis] = slice(0, margin)
         own_head = own[tuple(index)]
-        index[axis] = tail
+        index[axis] = slice(depth - margin, depth)
         own_tail = own[tuple(index)]
+        zero_shape = list(own.shape)
+        zero_shape[axis] = pad_rows
         return jnp.concatenate(
-            [jnp.stack(rows, axis=axis), own_head, own_tail, jnp.stack(after, axis=axis)], axis=axis
+            [
+                jnp.stack(list(lower), axis=axis),
+                own_head,
+                own_tail,
+                jnp.stack(list(upper), axis=axis),
+                jnp.zeros(zero_shape, jnp.float32),
+            ],
+            axis=axis,
         )
 
     md_win = window(modal_disp, md_below, md_above, 3)
-    ld_win = window(loads, ld_below, ld_above, 3)
+    ld_zero = jnp.zeros(plane, jnp.float32)
+    ld_win = window(loads, [ld_zero] + ld_below, ld_above + [ld_zero], 3)
     ids_win = window(ids, ids_below, ids_above, 1)
     logical = jnp.concatenate(
         [
-            jnp.arange(-8, edge_rows, dtype=jnp.int32),
-            jnp.arange(depth - edge_rows, depth + 8, dtype=jnp.int32),
+            jnp.arange(-reach, margin, dtype=jnp.int32),
+            jnp.arange(depth - margin, depth + reach, dtype=jnp.int32),
+            jnp.full((pad_rows,), depth + 8, dtype=jnp.int32),
         ]
     )
 
@@ -452,11 +456,9 @@
     masks = jnp.stack([valid(2), valid(1), valid(3)], axis=0)
     disp_win, res_win = chain(md_win, ld_win, ids_win, masks)
 
-    reach = 3
-
     def patch(out, win):
-        top = jnp.transpose(win[:, :, :, 8 : 8 + reach], (0, 1, 3, 2, 4))
-        bottom = jnp.transpose(win[:, :, :, 8 + 2 * edge_rows - reach : 8 + 2 * edge_rows], (0, 1, 3, 2, 4))
+        top = jnp.transpose(win[:, :, :, reach : 2 * reach], (0, 1, 3, 2, 4))
+        bottom = jnp.transpose(win[:, :, :, reach + 2 * margin - reach : reach + 2 * margin], (0, 1, 3, 2, 4))
         out = lax.dynamic_update_slice_in_dim(out, top, 0, axis=2)
         return lax.dynamic_update_slice_in_dim(out, bottom, depth - reach, axis=2)
 

time: 75.5 us -> 76.6 us (1.015)
  other arithmetic: 7.12 us -> 9.69 us
  Pallas kernels: 25.1 us -> 23.3 us
    select_n x2, other arithmetic: 2 us -> 6.04 us  [the longest x1 6.02 us: exchange(): slots = jnp.where(source == k, held[k][None], slots)]
    pallas_call x2, Pallas kernels: 25.1 us -> 23.3 us  [run_chain(): pl.pallas_call(chain_kernel, out_shape=(field, field), in_specs=[smem, sm...]
    concatenate x1 -> x0, other arithmetic: 1.5 us -> none  [exchange(): slots = jnp.concatenate([from_up, from_low], axis=1)]
where the time goes in v13:
time: 76.6 us; the launch traced here: 76.1 us
  Pallas kernels  23.3 us (30%)
  blocking collectives  14.3 us (19%)
  between operations  10.3 us (13%)
  other arithmetic  9.69 us (13%)
  local copies, waits for them, and re-layouts  8.44 us (11%)
  starting transfers between devices  8.06 us (11%)
  waiting for transfers between devices  2.01 us (3%)
    pallas_call x2, Pallas kernels, run_chain(): pl.pallas_call(chain_kernel, out_shape=(field, field), in_specs=[smem, sm...  23.3 us
    all_gather x1, blocking collectives, exchange(): held = lax.all_gather(pack, 'grp', axis=0, tiled=True)  14.3 us
    all_to_all x1, starting transfers between devices, exchange(): got = lax.all_to_all(slots, 'col', 0, 0, tiled=True)  8.06 us
    select_n x1, other arithmetic, exchange(): slots = jnp.where(source == k, held[k][None], slots)  6.02 us
    unnamed x26, local copies, waits for them, and re-layouts  3.08 us
    all_to_all x1, waiting for transfers between devices, exchange(): got = lax.all_to_all(slots, 'col', 0, 0, tiled=True)  2.01 us
  transfers between devices with their start and end apart: 1, of which 1 were waited for; matrix products, arithmetic and copies ran while one was open for 4% of the time, Pallas kernels for 22%

profile of v13, /device:TPU:0, one launch (start us, length us, event | category | flops | bytes accessed | tf_op | source)
XLA Modules:
  0.0 76.1 jit_solution(17013452019515580581)
XLA Ops:
  0.6 0.8 %fusion.9 = (f32[4,3,1,2,128]{4,3,2,1,0:T(2,128)S(1)}, f32[4,3,1,2,128]{4,3,2,1,0:T(2,128)S(1)}, f32[4,3,1,2,128]{4,3,2,1,0:T(2,128)S(1)}, f32[4,3,1,2,128]{4,3,...) fusion(f32[4,3,64,2,128]{4,3,2,1,0:T(2,128)} %param.9), kind=kLoop, calls=%fused_computation.93 | loop fusion | bytes 147456 | tf_op jit(solution)/shard_map/slice | solution.py:369
  1.5 0.8 %fusion.8 = (f32[4,3,1,2,128]{4,3,2,1,0:T(2,128)S(1)}, f32[4,3,1,2,128]{4,3,2,1,0:T(2,128)S(1)}, f32[4,3,1,2,128]{4,3,2,1,0:T(2,128)S(1)}, f32[4,3,1,2,128]{4,3,2,1,0:T(2,128)S(1)}) fusion(f32[4,3,64,2,128]{4,3,2,1,0:T(2,128)} %param.8), kind=kLoop, calls=%fused_computation.92 | loop fusion | bytes 98304 | tf_op jit(solution)/shard_map/slice | solution.py:370
  2.3 0.9 %copy_convert_fusion = (f32[64,2,128]{2,0,1:T(8,128)S(1)}, f32[2,64,128]{2,1,0:T(8,128)S(1)}) fusion(s32[64,2,128]{2,1,0:T(2,128)} %param.10), kind=kLoop, calls=%fused_computation.22 | loop fusion | flops 16384 | bytes 196608 | tf_op jit(solution)/shard_map/convert_element_type | solution.py:363
  3.4 14.3 %all-gather.1 = f32[8,252,128]{2,1,0:T(8,128)S(1)} all-gather(f32[1,252,128]{2,1,0:T(8,128)S(1)} %maximum_bitcast_fusion), channel_id=2, replica_groups=mesh['col'=16,'grp'=8] {'grp'}, dimensions={0}, use_global_device_ids=true | all-gather | bytes 1161216 | tf_op jit(solution)/shard_map/all_gather | solution.py:339
  18.4 6.0 %select_select_fusion = f32[16,252,128]{2,1,0:T(8,128)} fusion(f32[252,128]{1,0:T(8,128)S(1)} %get-tuple-element.36, f32[252,128]{1,0:T(8,128)S(1)} %get-tuple-element.30, f32[252,128]{1,0:T(8,128)S(1)} %get-tuple-element.31, f32[252,128]{1,0:T(8,128)S(1)} %get-tuple-element.32, f32[252,128]{1,0:T(8,128)S(1)} %get-tuple-element.33, ...), kind=kLoop, calls=%fused_computation | loop fusion | flops 4128768 | bytes 3128832 | tf_op jit(solution)/shard_map/jit(_where)/select_n | solution.py:349
  24.4 8.1 %all-to-all-start = ((f32[16,252,128]{2,1,0:T(8,128)}), f32[16,252,128]{2,1,0:T(8,128)}, u32[]{:S(2)}, u32[]{:S(2)}) async-start(f32[16,252,128]{2,1,0:T(8,128)} %select_select_fusion), calls=%async_computation | async-start | bytes 4194304 | tf_op jit(solution)/shard_map/all_to_all | solution.py:350
  32.5 0.7 fusion.2
  33.2 0.6 fusion.3
  33.8 0.6 dynamic_slice.15
  36.4 0.6 dynamic_slice.13
  44.3 0.2 copy_bitcast_fusion
  44.6 16.4 %shard_map.95 = (f32[4,3,2,64,128]{4,3,2,1,0:T(8,128)S(1)}, f32[4,3,2,64,128]{4,3,2,1,0:T(8,128)S(1)}) custom-call(f32[3]{0:T(128)S(1)} %pad_maximum_fusion.1.scal_ref, f32[8]{0:T(128)S(1)} %copy-done, f32[3,64,128]{2,1,0:T(8,128)S(1)} %broadcast_in_dim.184.mask_ref, f32[4,3,2,64,128]{4,3,2,1,0:T(8,128)S(1)} %get-tuple-element.93.md_ref, ...), custom_call_target="tpu_custom_call" | custom-call | flops 306708480 | bytes 3932160 | tf_op jit(solution)/shard_map/pallas_call | solution.py:295
  61.3 2.0 %all-to-all-done = f32[16,252,128]{2,1,0:T(8,128)} async-done(((f32[16,252,128]{2,1,0:T(8,128)}), f32[16,252,128]{2,1,0:T(8,128)}, u32[]{:S(2)}, u32[]{:S(2)}) %all-to-all-start) | async-done | bytes 2064416 | tf_op jit(solution)/shard_map/all_to_all | solution.py:350
  63.3 0.9 %dynamic-slice_select_fusion = (f32[1,126,128]{2,1,0:T(8,128)S(1)}, f32[1,126,128]{2,1,0:T(8,128)S(1)}) fusion(f32[16,252,128]{2,1,0:T(8,128)} %all-to-all-done, s32[]{:T(128)S(6)} %select_n.237, pred[]{:T(512)S(6)} %ne.128, s32[]{:T(128)S(6)} %select_n.233, s32[]{:T(128)S(6)} %add.92, pred[]{:T(512)S(6)} %ne.119), kind=kLoop, calls=%fused_computation.20 | loop fusion | flops 32256 | bytes 258062 | tf_op jit(solution)/shard_map/jit(_where)/select_n | solution.py:355
  64.4 0.3 concatenate.26.ld_ref
  64.7 0.3 concatenate.25.md_ref
  65.0 0.1 concatenate.27.ids_ref
  65.2 6.9 %shard_map.96 = (f32[4,3,2,24,128]{4,3,2,1,0:T(8,128)S(1)}, f32[4,3,2,24,128]{4,3,2,1,0:T(8,128)S(1)}) custom-call(f32[3]{0:T(128)S(1)} %pad_maximum_fusion.1.scal_ref, f32[8]{0:T(128)S(1)} %copy-done, f32[3,24,128]{2,1,0:T(8,128)S(1)} %pad_maximum_fusion.mask_ref, f32[4,3,2,24,128]{4,3,2,1,0:T(8,128)S(1)} %concatenate.25.md_ref, ...), custom_call_target="tpu_custom_call" | custom-call | flops 115015680 | bytes 1474560 | tf_op jit(solution)/shard_map/pallas_call | solution.py:295
  72.2 0.2 dynamic_update_slice.14
  72.4 0.2 dynamic_update_slice.15
  72.6 1.5 %copy.89 = f32[4,3,64,2,128]{4,3,2,1,0:T(2,128)} copy(f32[4,3,64,2,128]{4,2,3,1,0:T(8,128)S(1)} %dynamic_update_slice.15) | data formatting | bytes 1572864
  74.1 0.2 dynamic_update_slice.12
  74.4 0.2 dynamic_update_slice.13
  74.6 1.5 %copy.88 = f32[4,3,64,2,128]{4,3,2,1,0:T(2,128)} copy(f32[4,3,64,2,128]{4,2,3,1,0:T(8,128)S(1)} %dynamic_update_slice.13) | data formatting | bytes 1572864
  (60 shorter events, 1.4 us)
Async XLA Ops:
  1.5 16.3 %copy-start.3 = (s32[2,128]{1,0:T(2,128)S(1)}, s32[2,128]{1,0:T(2,128)}, u32[]{:S(2)}) copy-start(s32[2,128]{1,0:T(2,128)} %param.13) | copy-start | bytes 3076
  1.5 16.5 %copy-start.4 = (s32[128]{0:T(128)S(1)}, s32[128]{0:T(128)}, u32[]{:S(2)}) copy-start(s32[128]{0:T(128)} %param.12) | copy-start | bytes 1540
  24.4 19.9 %copy-start.1 = (f32[4,3,64,2,128]{4,3,2,1,0:T(2,128)S(1)}, f32[4,3,64,2,128]{4,3,2,1,0:T(2,128)}, u32[]{:S(2)}) copy-start(f32[4,3,64,2,128]{4,3,2,1,0:T(2,128)} %param.9) | copy-start | bytes 2359300
  24.4 19.9 %copy-start.2 = (f32[4,3,64,2,128]{4,3,2,1,0:T(2,128)S(1)}, f32[4,3,64,2,128]{4,3,2,1,0:T(2,128)}, u32[]{:S(2)}) copy-start(f32[4,3,64,2,128]{4,3,2,1,0:T(2,128)} %param.8) | copy-start | bytes 2359300
  24.4 38.9 %all-to-all-start = ((f32[16,252,128]{2,1,0:T(8,128)}), f32[16,252,128]{2,1,0:T(8,128)}, u32[]{:S(2)}, u32[]{:S(2)}) async-start(f32[16,252,128]{2,1,0:T(8,128)} %select_select_fusion), calls=%async_computation | async-start | bytes 4194304 | tf_op jit(solution)/shard_map/all_to_all | solution.py:350
  32.5 12.1 %copy-start = (f32[8]{0:T(128)S(1)}, f32[8]{0:T(128)}, u32[]{:S(2)}) copy-start(f32[8]{0:T(128)} %moduli_ref.3) | copy-start | bytes 100

commit v14 on v13

--- a/solution.py
+++ b/solution.py
@@ -342,11 +342,12 @@
     t_low = jnp.sum(jnp.where(pick, low_dev.reshape(cols, GROUP), 0), axis=1)
     up_at = jnp.where(t_up // GROUP == col, t_up % GROUP, -1)[:, None, None]
     low_at = jnp.where(t_low // GROUP == col, t_low % GROUP, -1)[:, None, None]
-    row = lax.broadcasted_iota(jnp.int32, (1, 2 * rows, 1), 1)
-    source = jnp.where(row < rows, up_at, low_at)
-    slots = jnp.zeros((cols, 2 * rows) + first.shape[1:], jnp.float32)
+    from_up = jnp.zeros((cols,) + first.shape, jnp.float32)
+    from_low = jnp.zeros((cols,) + first.shape, jnp.float32)
     for k in range(GROUP):
-        slots = jnp.where(source == k, held[k][None], slots)
+        from_up = jnp.where(up_at == k, held[k, :rows][None], from_up)
+        from_low = jnp.where(low_at == k, held[k, rows:][None], from_low)
+    slots = jnp.concatenate([from_up, from_low], axis=1)
     got = lax.all_to_all(slots, "col", 0, 0, tiled=True)
     my_up = up_dev[me]
     my_low = low_dev[me]

time: 76.6 us -> 74.1 us (0.967)
  other arithmetic: 9.69 us -> 7.12 us
    select_n x2, other arithmetic: 6.04 us -> 2 us  [the longest x1 1 us: exchange(): from_low = jnp.where(low_at == k, held[k, rows:][None], from_low)]
    concatenate x0 -> x1, other arithmetic: none -> 1.5 us  [exchange(): slots = jnp.concatenate([from_up, from_low], axis=1)]
where the time goes in v14:
time: 74.1 us; the launch traced here: 73.6 us
  Pallas kernels  23.3 us (31%)
  blocking collectives  14.3 us (19%)
  between operations  10.3 us (14%)
  local copies, waits for them, and re-layouts  8.47 us (11%)
  starting transfers between devices  8.06 us (11%)
  other arithmetic  7.12 us (10%)
  waiting for transfers between devices  1.98 us (3%)
    pallas_call x2, Pallas kernels, run_chain(): pl.pallas_call(chain_kernel, out_shape=(field, field), in_specs=[smem, sm...  23.3 us
    all_gather x1, blocking collectives, exchange(): held = lax.all_gather(pack, 'grp', axis=0, tiled=True)  14.3 us
    all_to_all x1, starting transfers between devices, exchange(): got = lax.all_to_all(slots, 'col', 0, 0, tiled=True)  8.06 us
    unnamed x26, local copies, waits for them, and re-layouts  3.08 us
    all_to_all x1, waiting for transfers between devices, exchange(): got = lax.all_to_all(slots, 'col', 0, 0, tiled=True)  1.98 us
    concatenate x1, other arithmetic, exchange(): slots = jnp.concatenate([from_up, from_low], axis=1)  1.5 us
  transfers between devices with their start and end apart: 1, of which 1 were waited for; matrix products, arithmetic and copies ran while one was open for 4% of the time, Pallas kernels for 22%

profile of v14, /device:TPU:0, one launch (start us, length us, event | category | flops | bytes accessed | tf_op | source)
XLA Modules:
  0.0 73.6 jit_solution(5535958512640081050)
XLA Ops:
  0.6 0.8 %fusion.9 = (f32[4,3,1,2,128]{4,3,2,1,0:T(2,128)S(1)}, f32[4,3,1,2,128]{4,3,2,1,0:T(2,128)S(1)}, f32[4,3,1,2,128]{4,3,2,1,0:T(2,128)S(1)}, f32[4,3,1,2,128]{4,3,...) fusion(f32[4,3,64,2,128]{4,3,2,1,0:T(2,128)} %param.9), kind=kLoop, calls=%fused_computation.110 | loop fusion | bytes 147456 | tf_op jit(solution)/shard_map/slice | solution.py:370
  1.5 0.8 %fusion.8 = (f32[4,3,1,2,128]{4,3,2,1,0:T(2,128)S(1)}, f32[4,3,1,2,128]{4,3,2,1,0:T(2,128)S(1)}, f32[4,3,1,2,128]{4,3,2,1,0:T(2,128)S(1)}, f32[4,3,1,2,128]{4,3,2,1,0:T(2,128)S(1)}) fusion(f32[4,3,64,2,128]{4,3,2,1,0:T(2,128)} %param.8), kind=kLoop, calls=%fused_computation.109 | loop fusion | bytes 98304 | tf_op jit(solution)/shard_map/slice | solution.py:371
  2.3 0.9 %copy_convert_fusion = (f32[64,2,128]{2,0,1:T(8,128)S(1)}, f32[2,64,128]{2,1,0:T(8,128)S(1)}) fusion(s32[64,2,128]{2,1,0:T(2,128)} %param.10), kind=kLoop, calls=%fused_computation.24 | loop fusion | flops 16384 | bytes 196608 | tf_op jit(solution)/shard_map/convert_element_type | solution.py:364
  3.3 14.3 %all-gather.1 = f32[8,252,128]{2,1,0:T(8,128)S(1)} all-gather(f32[1,252,128]{2,1,0:T(8,128)S(1)} %maximum_bitcast_fusion), channel_id=2, replica_groups=mesh['col'=16,'grp'=8] {'grp'}, dimensions={0}, use_global_device_ids=true | all-gather | bytes 1161216 | tf_op jit(solution)/shard_map/all_gather | solution.py:339
  18.4 1.0 %select_select_fusion.1 = f32[16,126,128]{2,1,0:T(8,128)S(1)} fusion(f32[126,128]{1,0:T(8,128)S(1)} %get-tuple-element.41, f32[126,128]{1,0:T(8,128)S(1)} %get-tuple-element.42, f32[126,128]{1,0:T(8,128)S(1)} %get-tuple-element.43, f32[126,128]{1,0:T(8,128)S(1)} %get-tuple-element.44, f32[126,128]{1,0:T(8,128)S(1)} %get-tuple-element.45, ...), kind=kLoop, calls=%fused_computation.2 | loop fusion | flops 2064384 | bytes 1548416 | tf_op jit(solution)/shard_map/jit(_where)/select_n | solution.py:348
  19.4 1.0 %select_select_fusion = f32[16,126,128]{2,1,0:T(8,128)S(1)} fusion(f32[126,128]{1,0:T(8,128)S(1)} %get-tuple-element.48, f32[126,128]{1,0:T(8,128)S(1)} %get-tuple-element.34, f32[126,128]{1,0:T(8,128)S(1)} %get-tuple-element.35, f32[126,128]{1,0:T(8,128)S(1)} %get-tuple-element.36, f32[126,128]{1,0:T(8,128)S(1)} %get-tuple-element.37, ...), kind=kLoop, calls=%fused_computation.1 | loop fusion | flops 2064384 | bytes 1548416 | tf_op jit(solution)/shard_map/jit(_where)/select_n | solution.py:349
  20.4 1.5 %pad_maximum_fusion = f32[16,252,128]{2,1,0:T(8,128)} fusion(f32[16,126,128]{2,1,0:T(8,128)S(1)} %select_select_fusion, f32[16,126,128]{2,1,0:T(8,128)S(1)} %select_select_fusion.1), kind=kLoop, calls=%fused_computation | loop fusion | flops 516096 | bytes 4128768 | tf_op jit(solution)/shard_map/concatenate | solution.py:350
  21.9 8.1 %all-to-all-start = ((f32[16,252,128]{2,1,0:T(8,128)}), f32[16,252,128]{2,1,0:T(8,128)}, u32[]{:S(2)}, u32[]{:S(2)}) async-start(f32[16,252,128]{2,1,0:T(8,128)} %pad_maximum_fusion), calls=%async_computation | async-start | bytes 4194304 | tf_op jit(solution)/shard_map/all_to_all | solution.py:351
  30.0 0.7 fusion.2
  30.7 0.6 fusion.3
  31.3 0.6 dynamic_slice.15
  33.8 0.6 dynamic_slice.13
  42.0 16.4 %shard_map.95 = (f32[4,3,2,64,128]{4,3,2,1,0:T(8,128)S(1)}, f32[4,3,2,64,128]{4,3,2,1,0:T(8,128)S(1)}) custom-call(f32[3]{0:T(128)S(1)} %pad_maximum_fusion.2.scal_ref, f32[8]{0:T(128)S(1)} %copy-done, f32[3,64,128]{2,1,0:T(8,128)S(1)} %broadcast_in_dim.253.mask_ref, f32[4,3,2,64,128]{4,3,2,1,0:T(8,128)S(1)} %get-tuple-element.111.md_ref, ...), custom_call_target="tpu_custom_call" | custom-call | flops 306708480 | bytes 3932160 | tf_op jit(solution)/shard_map/pallas_call | solution.py:295
  58.8 2.0 %all-to-all-done = f32[16,252,128]{2,1,0:T(8,128)} async-done(((f32[16,252,128]{2,1,0:T(8,128)}), f32[16,252,128]{2,1,0:T(8,128)}, u32[]{:S(2)}, u32[]{:S(2)}) %all-to-all-start) | async-done | bytes 2064416 | tf_op jit(solution)/shard_map/all_to_all | solution.py:351
  60.8 0.9 %dynamic-slice_select_fusion = (f32[1,126,128]{2,1,0:T(8,128)S(1)}, f32[1,126,128]{2,1,0:T(8,128)S(1)}) fusion(f32[16,252,128]{2,1,0:T(8,128)} %all-to-all-done, s32[]{:T(128)S(6)} %select_n.364, pred[]{:T(512)S(6)} %ne.296, s32[]{:T(128)S(6)} %select_n.360, s32[]{:T(128)S(6)} %add.176, pred[]{:T(512)S(6)} %ne.287), kind=kLoop, calls=%fused_computation.6 | loop fusion | flops 32256 | bytes 258062 | tf_op jit(solution)/shard_map/jit(_where)/select_n | solution.py:356
  61.8 0.3 concatenate.30.ld_ref
  62.1 0.3 concatenate.29.md_ref
  62.6 6.9 %shard_map.96 = (f32[4,3,2,24,128]{4,3,2,1,0:T(8,128)S(1)}, f32[4,3,2,24,128]{4,3,2,1,0:T(8,128)S(1)}) custom-call(f32[3]{0:T(128)S(1)} %pad_maximum_fusion.2.scal_ref, f32[8]{0:T(128)S(1)} %copy-done, f32[3,24,128]{2,1,0:T(8,128)S(1)} %pad_maximum_fusion.1.mask_ref, f32[4,3,2,24,128]{4,3,2,1,0:T(8,128)S(1)} %concatenate.29.md_ref, ...), custom_call_target="tpu_custom_call" | custom-call | flops 115015680 | bytes 1474560 | tf_op jit(solution)/shard_map/pallas_call | solution.py:295
  69.6 0.2 dynamic_update_slice.14
  69.9 0.2 dynamic_update_slice.15
  70.1 1.5 %copy.89 = f32[4,3,64,2,128]{4,3,2,1,0:T(2,128)} copy(f32[4,3,64,2,128]{4,2,3,1,0:T(8,128)S(1)} %dynamic_update_slice.15) | data formatting | bytes 1572864
  71.6 0.2 dynamic_update_slice.12
  71.8 0.2 dynamic_update_slice.13
  72.1 1.5 %copy.88 = f32[4,3,64,2,128]{4,3,2,1,0:T(2,128)} copy(f32[4,3,64,2,128]{4,2,3,1,0:T(8,128)S(1)} %dynamic_update_slice.13) | data formatting | bytes 1572864
  (62 shorter events, 1.7 us)
Async XLA Ops:
  1.4 16.3 %copy-start.3 = (s32[2,128]{1,0:T(2,128)S(1)}, s32[2,128]{1,0:T(2,128)}, u32[]{:S(2)}) copy-start(s32[2,128]{1,0:T(2,128)} %param.13) | copy-start | bytes 3076
  1.5 16.5 %copy-start.4 = (s32[128]{0:T(128)S(1)}, s32[128]{0:T(128)}, u32[]{:S(2)}) copy-start(s32[128]{0:T(128)} %param.12) | copy-start | bytes 1540
  21.9 19.9 %copy-start.1 = (f32[4,3,64,2,128]{4,3,2,1,0:T(2,128)S(1)}, f32[4,3,64,2,128]{4,3,2,1,0:T(2,128)}, u32[]{:S(2)}) copy-start(f32[4,3,64,2,128]{4,3,2,1,0:T(2,128)} %param.9) | copy-start | bytes 2359300
  21.9 19.9 %copy-start.2 = (f32[4,3,64,2,128]{4,3,2,1,0:T(2,128)S(1)}, f32[4,3,64,2,128]{4,3,2,1,0:T(2,128)}, u32[]{:S(2)}) copy-start(f32[4,3,64,2,128]{4,3,2,1,0:T(2,128)} %param.8) | copy-start | bytes 2359300
  21.9 38.9 %all-to-all-start = ((f32[16,252,128]{2,1,0:T(8,128)}), f32[16,252,128]{2,1,0:T(8,128)}, u32[]{:S(2)}, u32[]{:S(2)}) async-start(f32[16,252,128]{2,1,0:T(8,128)} %pad_maximum_fusion), calls=%async_computation | async-start | bytes 4194304 | tf_op jit(solution)/shard_map/all_to_all | solution.py:351
  30.0 12.1 %copy-start = (f32[8]{0:T(128)S(1)}, f32[8]{0:T(128)}, u32[]{:S(2)}) copy-start(f32[8]{0:T(128)} %moduli_ref.3) | copy-start | bytes 100

commit v15 on v14

--- a/solution.py
+++ b/solution.py
@@ -408,10 +408,6 @@
         return run_chain(scalars, moduli, masks, md, ld, material_ids)
 
     disp_local, res_local = chain(modal_disp, loads, ids, jnp.ones((3, depth, width), jnp.float32))
-    out_local = (
-        jnp.transpose(disp_local, (0, 1, 3, 2, 4)),
-        jnp.transpose(res_local, (0, 1, 3, 2, 4)),
-    )
 
     reach = 3
     margin = 2 * reach
@@ -458,12 +454,13 @@
     disp_win, res_win = chain(md_win, ld_win, ids_win, masks)
 
     def patch(out, win):
-        top = jnp.transpose(win[:, :, :, reach : 2 * reach], (0, 1, 3, 2, 4))
-        bottom = jnp.transpose(win[:, :, :, reach + 2 * margin - reach : reach + 2 * margin], (0, 1, 3, 2, 4))
-        out = lax.dynamic_update_slice_in_dim(out, top, 0, axis=2)
-        return lax.dynamic_update_slice_in_dim(out, bottom, depth - reach, axis=2)
-
-    return (patch(out_local[0], disp_win), patch(out_local[1], res_win))
+        out = lax.dynamic_update_slice_in_dim(out, win[:, :, :, reach : 2 * reach], 0, axis=3)
+        out = lax.dynamic_update_slice_in_dim(
+            out, win[:, :, :, reach + 2 * margin - reach : reach + 2 * margin], depth - reach, axis=3
+        )
+        return jnp.transpose(out, (0, 1, 3, 2, 4))
+
+    return (patch(disp_local, disp_win), patch(res_local, res_win))
 
 
 def col_grp_index():

time: 74.1 us -> 74.1 us (level)
  no operation moved by 1% of the time
where the time goes in v15:
time: 74.1 us; the launch traced here: 73.6 us
  Pallas kernels  23.3 us (31%)
  blocking collectives  14.3 us (19%)
  between operations  10.3 us (14%)
  local copies, waits for them, and re-layouts  8.47 us (11%)
  starting transfers between devices  8.06 us (11%)
  other arithmetic  7.12 us (10%)
  waiting for transfers between devices  1.98 us (3%)
    pallas_call x2, Pallas kernels, run_chain(): pl.pallas_call(chain_kernel, out_shape=(field, field), in_specs=[smem, sm...  23.3 us
    all_gather x1, blocking collectives, exchange(): held = lax.all_gather(pack, 'grp', axis=0, tiled=True)  14.3 us
    all_to_all x1, starting transfers between devices, exchange(): got = lax.all_to_all(slots, 'col', 0, 0, tiled=True)  8.06 us
    unnamed x26, local copies, waits for them, and re-layouts  3.08 us
    all_to_all x1, waiting for transfers between devices, exchange(): got = lax.all_to_all(slots, 'col', 0, 0, tiled=True)  1.98 us
    concatenate x1, other arithmetic, exchange(): slots = jnp.concatenate([from_up, from_low], axis=1)  1.5 us
  transfers between devices with their start and end apart: 1, of which 1 were waited for; matrix products, arithmetic and copies ran while one was open for 4% of the time, Pallas kernels for 22%

profile of v15, /device:TPU:0, one launch (start us, length us, event | category | flops | bytes accessed | tf_op | source)
XLA Modules:
  0.0 73.6 jit_solution(15993643985853852017)
XLA Ops:
  0.6 0.8 %fusion.9 = (f32[4,3,1,2,128]{4,3,2,1,0:T(2,128)S(1)}, f32[4,3,1,2,128]{4,3,2,1,0:T(2,128)S(1)}, f32[4,3,1,2,128]{4,3,2,1,0:T(2,128)S(1)}, f32[4,3,1,2,128]{4,3,...) fusion(f32[4,3,64,2,128]{4,3,2,1,0:T(2,128)} %param.9), kind=kLoop, calls=%fused_computation.106 | loop fusion | bytes 147456 | tf_op jit(solution)/shard_map/slice | solution.py:370
  1.5 0.8 %fusion.8 = (f32[4,3,1,2,128]{4,3,2,1,0:T(2,128)S(1)}, f32[4,3,1,2,128]{4,3,2,1,0:T(2,128)S(1)}, f32[4,3,1,2,128]{4,3,2,1,0:T(2,128)S(1)}, f32[4,3,1,2,128]{4,3,2,1,0:T(2,128)S(1)}) fusion(f32[4,3,64,2,128]{4,3,2,1,0:T(2,128)} %param.8), kind=kLoop, calls=%fused_computation.105 | loop fusion | bytes 98304 | tf_op jit(solution)/shard_map/slice | solution.py:371
  2.3 0.9 %copy_convert_fusion = (f32[64,2,128]{2,0,1:T(8,128)S(1)}, f32[2,64,128]{2,1,0:T(8,128)S(1)}) fusion(s32[64,2,128]{2,1,0:T(2,128)} %param.10), kind=kLoop, calls=%fused_computation.24 | loop fusion | flops 16384 | bytes 196608 | tf_op jit(solution)/shard_map/convert_element_type | solution.py:364
  3.3 14.3 %all-gather.1 = f32[8,252,128]{2,1,0:T(8,128)S(1)} all-gather(f32[1,252,128]{2,1,0:T(8,128)S(1)} %maximum_bitcast_fusion), channel_id=2, replica_groups=mesh['col'=16,'grp'=8] {'grp'}, dimensions={0}, use_global_device_ids=true | all-gather | bytes 1161216 | tf_op jit(solution)/shard_map/all_gather | solution.py:339
  18.4 1.0 %select_select_fusion.1 = f32[16,126,128]{2,1,0:T(8,128)S(1)} fusion(f32[126,128]{1,0:T(8,128)S(1)} %get-tuple-element.41, f32[126,128]{1,0:T(8,128)S(1)} %get-tuple-element.42, f32[126,128]{1,0:T(8,128)S(1)} %get-tuple-element.43, f32[126,128]{1,0:T(8,128)S(1)} %get-tuple-element.44, f32[126,128]{1,0:T(8,128)S(1)} %get-tuple-element.45, ...), kind=kLoop, calls=%fused_computation.2 | loop fusion | flops 2064384 | bytes 1548416 | tf_op jit(solution)/shard_map/jit(_where)/select_n | solution.py:348
  19.4 1.0 %select_select_fusion = f32[16,126,128]{2,1,0:T(8,128)S(1)} fusion(f32[126,128]{1,0:T(8,128)S(1)} %get-tuple-element.48, f32[126,128]{1,0:T(8,128)S(1)} %get-tuple-element.34, f32[126,128]{1,0:T(8,128)S(1)} %get-tuple-element.35, f32[126,128]{1,0:T(8,128)S(1)} %get-tuple-element.36, f32[126,128]{1,0:T(8,128)S(1)} %get-tuple-element.37, ...), kind=kLoop, calls=%fused_computation.1 | loop fusion | flops 2064384 | bytes 1548416 | tf_op jit(solution)/shard_map/jit(_where)/select_n | solution.py:349
  20.4 1.5 %pad_maximum_fusion = f32[16,252,128]{2,1,0:T(8,128)} fusion(f32[16,126,128]{2,1,0:T(8,128)S(1)} %select_select_fusion, f32[16,126,128]{2,1,0:T(8,128)S(1)} %select_select_fusion.1), kind=kLoop, calls=%fused_computation | loop fusion | flops 516096 | bytes 4128768 | tf_op jit(solution)/shard_map/concatenate | solution.py:350
  21.9 8.1 %all-to-all-start = ((f32[16,252,128]{2,1,0:T(8,128)}), f32[16,252,128]{2,1,0:T(8,128)}, u32[]{:S(2)}, u32[]{:S(2)}) async-start(f32[16,252,128]{2,1,0:T(8,128)} %pad_maximum_fusion), calls=%async_computation | async-start | bytes 4194304 | tf_op jit(solution)/shard_map/all_to_all | solution.py:351
  30.0 0.7 fusion.2
  30.7 0.6 fusion.3
  31.3 0.6 dynamic_slice.15
  33.8 0.6 dynamic_slice.13
  42.0 16.4 %shard_map.95 = (f32[4,3,2,64,128]{4,3,2,1,0:T(8,128)S(1)}, f32[4,3,2,64,128]{4,3,2,1,0:T(8,128)S(1)}) custom-call(f32[3]{0:T(128)S(1)} %pad_maximum_fusion.2.scal_ref, f32[8]{0:T(128)S(1)} %copy-done, f32[3,64,128]{2,1,0:T(8,128)S(1)} %broadcast_in_dim.253.mask_ref, f32[4,3,2,64,128]{4,3,2,1,0:T(8,128)S(1)} %get-tuple-element.120.md_ref, ...), custom_call_target="tpu_custom_call" | custom-call | flops 306708480 | bytes 3932160 | tf_op jit(solution)/shard_map/pallas_call | solution.py:295
  58.8 2.0 %all-to-all-done = f32[16,252,128]{2,1,0:T(8,128)} async-done(((f32[16,252,128]{2,1,0:T(8,128)}), f32[16,252,128]{2,1,0:T(8,128)}, u32[]{:S(2)}, u32[]{:S(2)}) %all-to-all-start) | async-done | bytes 2064416 | tf_op jit(solution)/shard_map/all_to_all | solution.py:351
  60.8 0.9 %dynamic-slice_select_fusion = (f32[1,126,128]{2,1,0:T(8,128)S(1)}, f32[1,126,128]{2,1,0:T(8,128)S(1)}) fusion(f32[16,252,128]{2,1,0:T(8,128)} %all-to-all-done, s32[]{:T(128)S(6)} %select_n.364, pred[]{:T(512)S(6)} %ne.296, s32[]{:T(128)S(6)} %select_n.360, s32[]{:T(128)S(6)} %add.176, pred[]{:T(512)S(6)} %ne.287), kind=kLoop, calls=%fused_computation.6 | loop fusion | flops 32256 | bytes 258062 | tf_op jit(solution)/shard_map/jit(_where)/select_n | solution.py:356
  61.8 0.3 concatenate.30.ld_ref
  62.1 0.3 concatenate.29.md_ref
  62.6 6.9 %shard_map.96 = (f32[4,3,2,24,128]{4,3,2,1,0:T(8,128)S(1)}, f32[4,3,2,24,128]{4,3,2,1,0:T(8,128)S(1)}) custom-call(f32[3]{0:T(128)S(1)} %pad_maximum_fusion.2.scal_ref, f32[8]{0:T(128)S(1)} %copy-done, f32[3,24,128]{2,1,0:T(8,128)S(1)} %pad_maximum_fusion.1.mask_ref, f32[4,3,2,24,128]{4,3,2,1,0:T(8,128)S(1)} %concatenate.29.md_ref, ...), custom_call_target="tpu_custom_call" | custom-call | flops 115015680 | bytes 1474560 | tf_op jit(solution)/shard_map/pallas_call | solution.py:295
  69.6 0.2 dynamic_update_slice.14
  69.9 0.2 dynamic_update_slice.15
  70.1 1.5 %copy.89 = f32[4,3,64,2,128]{4,3,2,1,0:T(2,128)} copy(f32[4,3,64,2,128]{4,2,3,1,0:T(8,128)S(1)} %bitcast.123) | data formatting | bytes 1572864
  71.6 0.2 dynamic_update_slice.12
  71.8 0.2 dynamic_update_slice.13
  72.1 1.5 %copy.88 = f32[4,3,64,2,128]{4,3,2,1,0:T(2,128)} copy(f32[4,3,64,2,128]{4,2,3,1,0:T(8,128)S(1)} %bitcast.122) | data formatting | bytes 1572864
  (62 shorter events, 1.7 us)
Async XLA Ops:
  1.4 16.3 %copy-start.3 = (s32[2,128]{1,0:T(2,128)S(1)}, s32[2,128]{1,0:T(2,128)}, u32[]{:S(2)}) copy-start(s32[2,128]{1,0:T(2,128)} %param.13) | copy-start | bytes 3076
  1.5 16.5 %copy-start.4 = (s32[128]{0:T(128)S(1)}, s32[128]{0:T(128)}, u32[]{:S(2)}) copy-start(s32[128]{0:T(128)} %param.12) | copy-start | bytes 1540
  21.9 19.9 %copy-start.1 = (f32[4,3,64,2,128]{4,3,2,1,0:T(2,128)S(1)}, f32[4,3,64,2,128]{4,3,2,1,0:T(2,128)}, u32[]{:S(2)}) copy-start(f32[4,3,64,2,128]{4,3,2,1,0:T(2,128)} %param.9) | copy-start | bytes 2359300
  21.9 19.9 %copy-start.2 = (f32[4,3,64,2,128]{4,3,2,1,0:T(2,128)S(1)}, f32[4,3,64,2,128]{4,3,2,1,0:T(2,128)}, u32[]{:S(2)}) copy-start(f32[4,3,64,2,128]{4,3,2,1,0:T(2,128)} %param.8) | copy-start | bytes 2359300
  21.9 38.9 %all-to-all-start = ((f32[16,252,128]{2,1,0:T(8,128)}), f32[16,252,128]{2,1,0:T(8,128)}, u32[]{:S(2)}, u32[]{:S(2)}) async-start(f32[16,252,128]{2,1,0:T(8,128)} %pad_maximum_fusion), calls=%async_computation | async-start | bytes 4194304 | tf_op jit(solution)/shard_map/all_to_all | solution.py:351
  30.0 12.1 %copy-start = (f32[8]{0:T(128)S(1)}, f32[8]{0:T(128)}, u32[]{:S(2)}) copy-start(f32[8]{0:T(128)} %moduli_ref.3) | copy-start | bytes 100

commit v16 on v15

--- a/solution.py
+++ b/solution.py
@@ -342,12 +342,14 @@
     t_low = jnp.sum(jnp.where(pick, low_dev.reshape(cols, GROUP), 0), axis=1)
     up_at = jnp.where(t_up // GROUP == col, t_up % GROUP, -1)[:, None, None]
     low_at = jnp.where(t_low // GROUP == col, t_low % GROUP, -1)[:, None, None]
-    from_up = jnp.zeros((cols,) + first.shape, jnp.float32)
-    from_low = jnp.zeros((cols,) + first.shape, jnp.float32)
+    slot_shape = (cols, 2 * rows) + first.shape[1:]
+    from_up = jnp.zeros(slot_shape, jnp.float32)
+    from_low = jnp.zeros(slot_shape, jnp.float32)
     for k in range(GROUP):
-        from_up = jnp.where(up_at == k, held[k, :rows][None], from_up)
-        from_low = jnp.where(low_at == k, held[k, rows:][None], from_low)
-    slots = jnp.concatenate([from_up, from_low], axis=1)
+        from_up = jnp.where(up_at == k, held[k][None], from_up)
+        from_low = jnp.where(low_at == k, held[k][None], from_low)
+    half_row = lax.broadcasted_iota(jnp.int32, slot_shape, 1)
+    slots = jnp.where(half_row < rows, from_up, from_low)
     got = lax.all_to_all(slots, "col", 0, 0, tiled=True)
     my_up = up_dev[me]
     my_low = low_dev[me]

time: 74.1 us -> 75.4 us (1.018)
  other arithmetic: 7.12 us -> 8.5 us
    select_n x2 -> x1, other arithmetic: 2 us -> 4.88 us  [exchange(): slots = jnp.where(half_row < rows, from_up, from_low)]
    concatenate x1 -> x0, other arithmetic: 1.5 us -> none  [exchange(): slots = jnp.concatenate([from_up, from_low], axis=1)]
where the time goes in v16:
time: 75.4 us; the launch traced here: 74.9 us
  Pallas kernels  23.3 us (31%)
  blocking collectives  14.3 us (19%)
  between operations  10.3 us (14%)
  other arithmetic  8.5 us (11%)
  local copies, waits for them, and re-layouts  8.44 us (11%)
  starting transfers between devices  8.06 us (11%)
  waiting for transfers between devices  1.98 us (3%)
    pallas_call x2, Pallas kernels, run_chain(): pl.pallas_call(chain_kernel, out_shape=(field, field), in_specs=[smem, sm...  23.3 us
    all_gather x1, blocking collectives, exchange(): held = lax.all_gather(pack, 'grp', axis=0, tiled=True)  14.3 us
    all_to_all x1, starting transfers between devices, exchange(): got = lax.all_to_all(slots, 'col', 0, 0, tiled=True)  8.06 us
    select_n x1, other arithmetic, exchange(): slots = jnp.where(half_row < rows, from_up, from_low)  4.88 us
    unnamed x26, local copies, waits for them, and re-layouts  3.08 us
    all_to_all x1, waiting for transfers between devices, exchange(): got = lax.all_to_all(slots, 'col', 0, 0, tiled=True)  1.98 us
  transfers between devices with their start and end apart: 1, of which 1 were waited for; matrix products, arithmetic and copies ran while one was open for 4% of the time, Pallas kernels for 22%

profile of v16, /device:TPU:0, one launch (start us, length us, event | category | flops | bytes accessed | tf_op | source)
XLA Modules:
  0.0 74.9 jit_solution(3933323870338643560)
XLA Ops:
  0.6 0.8 %fusion.9 = (f32[4,3,1,2,128]{4,3,2,1,0:T(2,128)S(1)}, f32[4,3,1,2,128]{4,3,2,1,0:T(2,128)S(1)}, f32[4,3,1,2,128]{4,3,2,1,0:T(2,128)S(1)}, f32[4,3,1,2,128]{4,3,...) fusion(f32[4,3,64,2,128]{4,3,2,1,0:T(2,128)} %param.9), kind=kLoop, calls=%fused_computation.97 | loop fusion | bytes 147456 | tf_op jit(solution)/shard_map/slice | solution.py:372
  1.5 0.8 %fusion.8 = (f32[4,3,1,2,128]{4,3,2,1,0:T(2,128)S(1)}, f32[4,3,1,2,128]{4,3,2,1,0:T(2,128)S(1)}, f32[4,3,1,2,128]{4,3,2,1,0:T(2,128)S(1)}, f32[4,3,1,2,128]{4,3,2,1,0:T(2,128)S(1)}) fusion(f32[4,3,64,2,128]{4,3,2,1,0:T(2,128)} %param.8), kind=kLoop, calls=%fused_computation.96 | loop fusion | bytes 98304 | tf_op jit(solution)/shard_map/slice | solution.py:373
  2.3 0.9 %copy_convert_fusion = (f32[64,2,128]{2,0,1:T(8,128)S(1)}, f32[2,64,128]{2,1,0:T(8,128)S(1)}) fusion(s32[64,2,128]{2,1,0:T(2,128)} %param.10), kind=kLoop, calls=%fused_computation.14 | loop fusion | flops 16384 | bytes 196608 | tf_op jit(solution)/shard_map/convert_element_type | solution.py:366
  3.4 14.3 %all-gather.1 = f32[8,252,128]{2,1,0:T(8,128)S(1)} all-gather(f32[1,252,128]{2,1,0:T(8,128)S(1)} %maximum_bitcast_fusion), channel_id=2, replica_groups=mesh['col'=16,'grp'=8] {'grp'}, dimensions={0}, use_global_device_ids=true | all-gather | bytes 1161216 | tf_op jit(solution)/shard_map/all_gather | solution.py:339
  18.3 4.9 %select_select_fusion = f32[16,252,128]{2,1,0:T(8,128)} fusion(f32[252,128]{1,0:T(8,128)S(1)} %get-tuple-element.40, f32[252,128]{1,0:T(8,128)S(1)} %get-tuple-element.34, f32[252,128]{1,0:T(8,128)S(1)} %get-tuple-element.35, f32[252,128]{1,0:T(8,128)S(1)} %get-tuple-element.36, f32[252,128]{1,0:T(8,128)S(1)} %get-tuple-element.37, ...), kind=kLoop, calls=%fused_computation | loop fusion | flops 8773632 | bytes 3097084 | tf_op jit(solution)/shard_map/jit(_where)/select_n | solution.py:352
  23.2 8.1 %all-to-all-start = ((f32[16,252,128]{2,1,0:T(8,128)}), f32[16,252,128]{2,1,0:T(8,128)}, u32[]{:S(2)}, u32[]{:S(2)}) async-start(f32[16,252,128]{2,1,0:T(8,128)} %select_select_fusion), calls=%async_computation | async-start | bytes 4194304 | tf_op jit(solution)/shard_map/all_to_all | solution.py:353
  31.3 0.7 fusion.2
  32.0 0.6 fusion.3
  32.7 0.6 dynamic_slice.15
  35.2 0.6 dynamic_slice.13
  43.2 0.2 copy_bitcast_fusion
  43.4 16.4 %shard_map.95 = (f32[4,3,2,64,128]{4,3,2,1,0:T(8,128)S(1)}, f32[4,3,2,64,128]{4,3,2,1,0:T(8,128)S(1)}) custom-call(f32[3]{0:T(128)S(1)} %pad_maximum_fusion.1.scal_ref, f32[8]{0:T(128)S(1)} %copy-done, f32[3,64,128]{2,1,0:T(8,128)S(1)} %broadcast_in_dim.221.mask_ref, f32[4,3,2,64,128]{4,3,2,1,0:T(8,128)S(1)} %get-tuple-element.112.md_ref, ...), custom_call_target="tpu_custom_call" | custom-call | flops 306708480 | bytes 3932160 | tf_op jit(solution)/shard_map/pallas_call | solution.py:295
  60.2 2.0 %all-to-all-done = f32[16,252,128]{2,1,0:T(8,128)} async-done(((f32[16,252,128]{2,1,0:T(8,128)}), f32[16,252,128]{2,1,0:T(8,128)}, u32[]{:S(2)}, u32[]{:S(2)}) %all-to-all-start) | async-done | bytes 2064416 | tf_op jit(solution)/shard_map/all_to_all | solution.py:353
  62.1 0.9 %dynamic-slice_select_fusion = (f32[1,126,128]{2,1,0:T(8,128)S(1)}, f32[1,126,128]{2,1,0:T(8,128)S(1)}) fusion(f32[16,252,128]{2,1,0:T(8,128)} %all-to-all-done, s32[]{:T(128)S(6)} %select_n.369, pred[]{:T(512)S(6)} %ne.296, s32[]{:T(128)S(6)} %select_n.365, s32[]{:T(128)S(6)} %add.176, pred[]{:T(512)S(6)} %ne.287), kind=kLoop, calls=%fused_computation.12 | loop fusion | flops 32256 | bytes 258062 | tf_op jit(solution)/shard_map/jit(_where)/select_n | solution.py:358
  63.2 0.3 concatenate.26.ld_ref
  63.5 0.3 concatenate.25.md_ref
  63.8 0.1 concatenate.27.ids_ref
  64.0 6.9 %shard_map.96 = (f32[4,3,2,24,128]{4,3,2,1,0:T(8,128)S(1)}, f32[4,3,2,24,128]{4,3,2,1,0:T(8,128)S(1)}) custom-call(f32[3]{0:T(128)S(1)} %pad_maximum_fusion.1.scal_ref, f32[8]{0:T(128)S(1)} %copy-done, f32[3,24,128]{2,1,0:T(8,128)S(1)} %pad_maximum_fusion.mask_ref, f32[4,3,2,24,128]{4,3,2,1,0:T(8,128)S(1)} %concatenate.25.md_ref, ...), custom_call_target="tpu_custom_call" | custom-call | flops 115015680 | bytes 1474560 | tf_op jit(solution)/shard_map/pallas_call | solution.py:295
  70.9 0.2 dynamic_update_slice.14
  71.2 0.2 dynamic_update_slice.15
  71.4 1.5 %copy.89 = f32[4,3,64,2,128]{4,3,2,1,0:T(2,128)} copy(f32[4,3,64,2,128]{4,2,3,1,0:T(8,128)S(1)} %bitcast.107) | data formatting | bytes 1572864
  72.9 0.2 dynamic_update_slice.12
  73.2 0.2 dynamic_update_slice.13
  73.4 1.5 %copy.88 = f32[4,3,64,2,128]{4,3,2,1,0:T(2,128)} copy(f32[4,3,64,2,128]{4,2,3,1,0:T(8,128)S(1)} %bitcast.106) | data formatting | bytes 1572864
  (61 shorter events, 1.3 us)
Async XLA Ops:
  1.5 16.3 %copy-start.3 = (s32[2,128]{1,0:T(2,128)S(1)}, s32[2,128]{1,0:T(2,128)}, u32[]{:S(2)}) copy-start(s32[2,128]{1,0:T(2,128)} %param.13) | copy-start | bytes 3076
  1.5 16.5 %copy-start.4 = (s32[128]{0:T(128)S(1)}, s32[128]{0:T(128)}, u32[]{:S(2)}) copy-start(s32[128]{0:T(128)} %param.12) | copy-start | bytes 1540
  23.2 19.9 %copy-start.1 = (f32[4,3,64,2,128]{4,3,2,1,0:T(2,128)S(1)}, f32[4,3,64,2,128]{4,3,2,1,0:T(2,128)}, u32[]{:S(2)}) copy-start(f32[4,3,64,2,128]{4,3,2,1,0:T(2,128)} %param.9) | copy-start | bytes 2359300
  23.2 19.9 %copy-start.2 = (f32[4,3,64,2,128]{4,3,2,1,0:T(2,128)S(1)}, f32[4,3,64,2,128]{4,3,2,1,0:T(2,128)}, u32[]{:S(2)}) copy-start(f32[4,3,64,2,128]{4,3,2,1,0:T(2,128)} %param.8) | copy-start | bytes 2359300
  23.2 38.9 %all-to-all-start = ((f32[16,252,128]{2,1,0:T(8,128)}), f32[16,252,128]{2,1,0:T(8,128)}, u32[]{:S(2)}, u32[]{:S(2)}) async-start(f32[16,252,128]{2,1,0:T(8,128)} %select_select_fusion), calls=%async_computation | async-start | bytes 4194304 | tf_op jit(solution)/shard_map/all_to_all | solution.py:353
  31.3 12.1 %copy-start = (f32[8]{0:T(128)S(1)}, f32[8]{0:T(128)}, u32[]{:S(2)}) copy-start(f32[8]{0:T(128)} %moduli_ref.3) | copy-start | bytes 100
